TPU v7x, 512 devices: a whole 4x8x8 slice. The times are simulated.
512 devices in a mesh: dp: 64 (over z, y), seq: 8 (over x, core).
Axes of the slice: x: 4, y: 8, z: 8, core: 2. Of those that a mesh axis runs over, the one named last changes fastest.
Arguments:
- checkpoint: bfloat16 [65536, 8192], P(('dp', 'seq')), may hold values from -6 to 6
- norm_gain: float32 [8192], replicated, may hold values from 0.1 to 1.9
- key_cotangent: bfloat16 [65536, 1024], P(('dp', 'seq')), may hold values from -6 to 6
- positions: int32 [65536], P(('dp', 'seq')), may hold values from 0 to 4095, as said below
- kept_cols: int32 [128, 6], replicated, may hold values from 0 to 15, as said below
- kept_count: int32 [128], replicated, may hold values from 2 to 6
- key_blocks: bfloat16 [128, 6, 4096], P('dp'), may hold values from -0.375 to 0.375
Outputs:
- input_grad: bfloat16 [65536, 8192], P(('dp', 'seq'))
- block_grad: float32 [128, 6, 4096], P('dp', None, 'seq')
Inputs may be any that keep to these rules, and one draw needn't show every extreme that they name: `kept_cols`: the 6 entries of a row are different block columns; only the first kept_count entries of a row name kept blocks, the others are unused slots. Inside a document the positions rise by one from token to token.
All inputs are finite; a program needn't handle non-finite values.
Results may differ from a plain program's by a relative error of at most 0.0049.
Values may be sent and summed in bfloat16 or wider, within the bound.
No kernel may reach another device: no remote copies, remote signals or barrier semaphores. Data moves between devices by JAX's collectives and lax.ppermute only.
A program may use at most 128 MiB of HBM per device.

v0:
```python
import math

import jax
import jax.numpy as jnp
from jax import lax
from jax.sharding import PartitionSpec as P

D = 8192
KVW = 1024
HEAD_DIM = 128
BLK = 64
MOSTR = 6
SEQ_LEN = 1024


def rope_back(grad, positions):
    heads = KVW // HEAD_DIM
    half = HEAD_DIM // 2
    values = grad.astype(jnp.float32).reshape(-1, heads, 2, half)
    freqs = 10000.0 ** (-2.0 * jnp.arange(half).astype(jnp.float32) / HEAD_DIM)
    angle = positions.astype(jnp.float32)[:, None] * freqs[None, :]
    cosine = jnp.cos(angle)[:, None, :]
    sine = jnp.sin(angle)[:, None, :]
    first = values[:, :, 0] * cosine + values[:, :, 1] * sine
    second = values[:, :, 1] * cosine - values[:, :, 0] * sine
    return jnp.stack([first, second], axis=2).reshape(-1, KVW).astype(jnp.bfloat16)


def densify(blocks, cols, count, rows):
    count_rows = blocks.shape[0]
    col_blocks = KVW // BLK
    slot_ids = lax.broadcasted_iota(jnp.int32, (count_rows, MOSTR), 1)
    live = slot_ids < count[:, None]
    col_ids = lax.broadcasted_iota(jnp.int32, (count_rows, MOSTR, col_blocks), 2)
    onehot = ((cols[:, :, None] == col_ids) & live[:, :, None]).astype(jnp.bfloat16)
    placed = lax.dot_general(
        onehot, blocks, (((1,), (1,)), ((0,), (0,))), preferred_element_type=jnp.bfloat16
    )
    dense = placed.reshape(count_rows, col_blocks, rows, BLK).transpose(0, 2, 1, 3)
    return dense.reshape(count_rows * rows, KVW)


def shards(checkpoint, norm_gain, key_cotangent, positions, kept_cols, kept_count, key_blocks):
    tok_rows = checkpoint.shape[0]
    groups = lax.axis_size("seq")
    part_rows = BLK // groups
    row_blocks = D // BLK
    col_blocks = KVW // BLK
    xf = checkpoint.astype(jnp.float32)
    inv_rms = lax.rsqrt(jnp.mean(xf * xf, axis=1, keepdims=True) + 1e-05)
    normed = (xf * inv_rms * norm_gain).astype(jnp.bfloat16)
    grad_pre = rope_back(key_cotangent, positions)
    grad_all = lax.all_gather(grad_pre, "seq", axis=0, tiled=True)
    split_normed = (
        normed.reshape(tok_rows, row_blocks, groups, part_rows)
        .transpose(0, 2, 1, 3)
        .reshape(tok_rows, groups, row_blocks * part_rows)
    )
    received = lax.all_to_all(split_normed, "seq", split_axis=1, concat_axis=0, tiled=True)
    normed_rows = received.reshape(groups * tok_rows, row_blocks, part_rows)
    divisor = math.sqrt(SEQ_LEN * lax.axis_size("dp"))
    count = row_blocks // lax.axis_size("dp") * lax.axis_size("dp")
    slab = normed_rows.reshape(groups * tok_rows, count * part_rows)
    product = lax.dot_general(
        slab, grad_all, (((0,), (0,)), ((), ())), preferred_element_type=jnp.float32
    )
    shaped = (
        product.reshape(count, part_rows, col_blocks, BLK)
        .transpose(0, 2, 1, 3)
        .reshape(count, col_blocks, part_rows * BLK)
    )
    cols = kept_cols
    counts = kept_count
    picked = jnp.take_along_axis(shaped, cols[:, :, None], axis=1)
    live = lax.broadcasted_iota(jnp.int32, (count, MOSTR), 1) < counts[:, None]
    block_grad = lax.psum_scatter(
        jnp.where(live[:, :, None], picked / divisor, jnp.float32(0.0)),
        "dp",
        scatter_dimension=0,
        tiled=True,
    )
    piece = lax.all_gather(key_blocks, "dp", axis=0, tiled=True)
    cols = kept_cols
    counts = kept_count
    dense = densify(piece, cols, counts, BLK)
    normed_grad = lax.dot_general(
        grad_pre, dense, (((1,), (1,)), ((), ())), preferred_element_type=jnp.float32
    )
    scaled = norm_gain * normed_grad
    grads = inv_rms * scaled - inv_rms**3 * xf * jnp.mean(scaled * xf, axis=1, keepdims=True)
    return (grads.astype(jnp.bfloat16), block_grad)


def solution(mesh):
    placed = (
        P(("dp", "seq"), None),
        P(),
        P(("dp", "seq"), None),
        P(("dp", "seq")),
        P(),
        P(),
        P("dp", None, None),
    )
    return jax.shard_map(
        shards,
        mesh=mesh,
        in_specs=placed,
        out_specs=(P(("dp", "seq"), None), P("dp", None, "seq")),
        check_vma=False,
    )
```

profile of v0, /device:TPU:6, one launch (start us, length us, event | category | flops | bytes accessed | tf_op | source)
XLA Modules:
  0.0 578.2 jit_solution(3472981876656661758)
XLA Ops:
  7.2 1.6 copy.31
  9.6 1.1 copy.29
  12.5 0.8 copy.30
  13.3 102.3 %all-gather.3.cloned.1.call-done = bf16[128,6,4096]{2,1,0:T(8,128)(2,1)} async-done(((bf16[2,6,4096]{2,1,0:T(8,128)(2,1)}), bf16[128,6,4096]{2,1,0:T(8,128)(2,1)}) %all-gather.3.cloned.1.call-update) | async-done | bytes 6291472 | tf_op jit(solution)/shard_map/all_gather | solution.py:82
  115.6 14.6 %fusion.9 = bf16[128,16,4096]{2,1,0:T(8,128)(2,1)} fusion(bf16[128,6,4096]{2,1,0:T(8,128)(2,1)} %all-gather.3.cloned.1.call-done, s32[128,6]{1,0:T(8,128)S(1)} %copy.30, pred[128,6]{1,0:T(8,128)(4,1)S(1)} %iota_compare_fusion.1), kind=kOutput, calls=%fused_computation.20 | convolution fusion | flops 100687872 | bytes 23072512 | tf_op jit(solution)/shard_map/dot_general | solution.py:36
  130.2 22.6 %copy.32 = bf16[128,16,4096]{0,2,1:T(8,128)(2,1)} copy(bf16[128,16,4096]{2,1,0:T(8,128)(2,1)} %fusion.9) | data formatting | bytes 33554432 | tf_op jit(solution)/shard_map/dot_general | solution.py:36
  152.8 46.0 %copy.33 = bf16[128,64,16,64]{3,2,1,0:T(8,128)(2,1)} copy(bf16[128,64,16,64]{0,3,1,2:T(8,128)(2,1)} %bitcast.39) | data formatting | bytes 33554432 | tf_op jit(solution)/shard_map/transpose | solution.py:39
  198.8 44.3 %reshape.139 = bf16[8192,1024]{1,0:T(8,128)(2,1)} reshape(bf16[128,64,16,64]{3,2,1,0:T(8,128)(2,1)} %copy.33) | data formatting | bytes 33554432 | tf_op jit(solution)/shard_map/reshape | solution.py:40
  243.1 13.6 %fusion = (f32[128]{0:T(128)S(1)}, f32[128]{0:T(128)S(1)}, f32[128,8192]{1,0:T(8,128)}) fusion(bf16[128,8192]{1,0:T(8,128)(2,1)S(1)} %copy-done, bf16[128,1024]{0,1:T(8,128)(2,1)S(1)} %bitcast.46, bf16[8192,1024]{1,0:T(8,128)(2,1)} %reshape.139, f32[8192]{0:T(1024)S(1)} %copy-done.2), kind=kOutput, calls=%fused_computation.6 | convolution fusion | flops 2153775104 | bytes 23364608 | tf_op jit(solution)/shard_map/dot_general | solution.py:86
  256.8 6.0 %fusion.6 = (bf16[128,8192]{1,0:T(8,128)(2,1)}, bf16[128,8192]{1,0:T(8,128)(2,1)}) fusion(bf16[128,8192]{1,0:T(8,128)(2,1)S(1)} %copy-done, f32[8192]{0:T(1024)S(1)} %copy-done.2, f32[128]{0:T(128)S(1)} %get-tuple-element.14, f32[128]{0:T(128)S(1)} %get-tuple-element.17, f32[128]{0:T(128)S(1)} %get-tuple-element.15, f32[128,8192]{1,0:T(8,128)} %get-tuple-element.16), kind=kLoop, calls=%fused_computation.12 | loop fusion | flops 9437184 | bytes 10520064 | tf_op jit(solution)/shard_map/convert_element_type | solution.py:51
  262.8 3.4 copy.35
  266.2 1.7 copy.50
  267.9 4.8 all-to-all-start
  273.1 24.7 %all-to-all-done = bf16[128,8,1024]{0,2,1:T(8,128)(2,1)S(1)} async-done(((bf16[128,8,1024]{0,2,1:T(8,128)(2,1)}), bf16[128,8,1024]{0,2,1:T(8,128)(2,1)S(1)}, u32[]{:S(2)}, u32[]{:S(2)}) %all-to-all-start) | async-done | bytes 2097184 | tf_op jit(solution)/shard_map/all_to_all | solution.py:59
  297.8 2.6 copy.37
  300.4 2.9 copy.38
  303.3 4.9 convolution_bitcast_fusion
  308.2 2.3 copy.40
  310.5 5.5 copy.42
  316.0 7.5 %gather_fusion = f32[768,512]{1,0:T(8,128)S(1)} fusion(f32[128,16,512]{2,1,0:T(8,128)} %copy.42, s32[768]{0:T(1024)S(1)} %reshape.145), kind=kCustom, calls=%fused_computation | custom fusion | bytes 3151872 | tf_op jit(solution)/shard_map/jit(take_along_axis)/gather | solution.py:74
  323.5 1.5 reshape.148
  325.1 2.8 multiply_select_fusion
  327.9 242.4 %reduce-scatter.2.cloned.1.call-done = f32[2,6,512]{2,1,0:T(8,128)} async-done(((f32[128,6,512]{2,1,0:T(8,128)}), f32[2,6,512]{2,1,0:T(8,128)}) %reduce-scatter.2.cloned.1.call-update) | async-done | bytes 24592 | tf_op jit(solution)/shard_map/reduce_scatter | solution.py:76
  570.3 1.4 copy.43
  (28 shorter events, 3.0 us)
Async XLA Ops:
  7.2 108.5 %all-gather.3.cloned.1.call-start = ((), (), s32[]{:S(2)}) async-start(), calls=%async_computation.2 | async-start | bytes 8519680 | tf_op jit(solution)/shard_map/all_gather | solution.py:82
  8.8 294.5 %all-gather.5.cloned.1.call-start = ((), (), s32[]{:S(2)}) async-start(), calls=%async_computation.3 | async-start | bytes 2359296 | tf_op jit(solution)/shard_map/all_gather | solution.py:53
  198.8 44.3 %copy-start = (bf16[128,8192]{1,0:T(8,128)(2,1)S(1)}, bf16[128,8192]{1,0:T(8,128)(2,1)}, u32[]{:S(2)}) copy-start(bf16[128,8192]{1,0:T(8,128)(2,1)} %param.7) | copy-start | bytes 6291460
  198.8 44.3 %copy-start.1 = (bf16[128,8,2,64]{0,3,2,1:T(8,128)(2,1)S(1)}, bf16[128,8,2,64]{0,3,2,1:T(8,128)(2,1)}, u32[]{:S(2)}) copy-start(bf16[128,8,2,64]{0,3,2,1:T(8,128)(2,1)} %maximum_convert_fusion) | copy-start | bytes 786436
  198.8 44.3 %copy-start.2 = (f32[8192]{0:T(1024)S(1)}, f32[8192]{0:T(1024)}, u32[]{:S(2)}) copy-start(f32[8192]{0:T(1024)} %param.8) | copy-start | bytes 98308
  266.2 6.5 %copy-start.3 = (s32[128,6]{0,1:T(8,128)S(1)}, s32[128,6]{0,1:T(8,128)}, u32[]{:S(2)}) copy-start(s32[128,6]{0,1:T(8,128)} %param.11) | copy-start | bytes 9220
  267.9 29.9 %all-to-all-start = ((bf16[128,8,1024]{0,2,1:T(8,128)(2,1)}), bf16[128,8,1024]{0,2,1:T(8,128)(2,1)S(1)}, u32[]{:S(2)}, u32[]{:S(2)}) async-start(bf16[128,8,1024]{0,2,1:T(8,128)(2,1)} %bitcast.42), calls=%async_computation | async-start | bytes 4194304 | tf_op jit(solution)/shard_map/all_to_all | solution.py:59
  272.7 297.6 %reduce-scatter.2.cloned.1.call-start = ((), (), s32[]{:S(2)}) async-start(), calls=%async_computation.4 | async-start | bytes 2129920 | tf_op jit(solution)/shard_map/reduce_scatter | solution.py:76
Sparse Core Ops, SparseCore 0:
  11.6 103.9 all-gather.2
  117.7 30.0 all-gather.4
  328.0 242.2 reduce-scatter.1
where the time goes:
time: 582 us; the launch traced here: 578 us
  waiting for transfers between devices  369 us (63%)
  local copies, waits for them, and re-layouts  146 us (25%)
  matrix products  33.1 us (6%)
  between operations  13.9 us (2%)
  other arithmetic  11.3 us (2%)
    reduce_scatter x1, waiting for transfers between devices, shards(): lax.psum_scatter(jnp.where(live[:, :, None], picked / divisor, jnp.float3...  242 us
    all_gather x1, waiting for transfers between devices, shards(): piece = lax.all_gather(key_blocks, 'dp', axis=0, tiled=True)  102 us
    transpose x1, local copies, waits for them, and re-layouts, densify(): placed.reshape(count_rows, col_blocks, rows, BLK).transpose(0, 2, 1, 3)  46 us
    reshape x1, local copies, waits for them, and re-layouts, densify(): return dense.reshape(count_rows * rows, KVW)  44.3 us
    all_to_all x1, waiting for transfers between devices, shards(): lax.all_to_all(split_normed, 'seq', split_axis=1, concat_axis=0, tiled=True)  24.7 us
    dot_general x1, local copies, waits for them, and re-layouts, densify(): lax.dot_general(onehot, blocks, (((1,), (1,)), ((0,), (0,))), preferred_e...  22.6 us
    dot_general x1, matrix products, densify(): lax.dot_general(onehot, blocks, (((1,), (1,)), ((0,), (0,))), preferred_e...  14.6 us
    dot_general x1, matrix products, shards(): lax.dot_general(grad_pre, dense, (((1,), (1,)), ((), ())), preferred_elem...  13.6 us
  transfers between devices with their start and end apart: 4, of which 3 were waited for; matrix products, arithmetic and copies ran while one was open for 28% of the time, Pallas kernels for 0%

commit v1 on v0

v1 whole, which is shorter than its diff:
```python
import math

import jax
import jax.numpy as jnp
import numpy as np
from jax import lax
from jax.experimental import pallas as pl
from jax.experimental.pallas import tpu as pltpu
from jax.sharding import Mesh
from jax.sharding import PartitionSpec as P

D = 8192
KVW = 1024
HEAD_DIM = 128
BLK = 64
MOSTR = 6
SEQ_LEN = 1024
ROWS_PER_STEP = 8


def rope_back(grad, positions):
    heads = KVW // HEAD_DIM
    half = HEAD_DIM // 2
    values = grad.astype(jnp.float32).reshape(-1, heads, 2, half)
    freqs = 10000.0 ** (-2.0 * jnp.arange(half).astype(jnp.float32) / HEAD_DIM)
    angle = positions.astype(jnp.float32)[:, None] * freqs[None, :]
    cosine = jnp.cos(angle)[:, None, :]
    sine = jnp.sin(angle)[:, None, :]
    first = values[:, :, 0] * cosine + values[:, :, 1] * sine
    second = values[:, :, 1] * cosine - values[:, :, 0] * sine
    return jnp.stack([first, second], axis=2).reshape(-1, KVW).astype(jnp.bfloat16)


def _normed_grad_kernel(cols_ref, cnt_ref, gp_ref, bt_ref, out_ref, w_ref):
    step = pl.program_id(0)
    w_ref[...] = jnp.zeros(w_ref.shape, w_ref.dtype)
    for rr in range(ROWS_PER_STEP):
        row = step * ROWS_PER_STEP + rr
        live = cnt_ref[row]
        for k in range(MOSTR):
            col = cols_ref[row * MOSTR + k]

            @pl.when(k < live)
            def _():
                start = pl.multiple_of(col * BLK, BLK)
                w_ref[pl.ds(start, BLK), rr * BLK:(rr + 1) * BLK] = bt_ref[rr, k].astype(jnp.float32)

    out_ref[...] = jnp.dot(
        gp_ref[...], w_ref[...].astype(jnp.bfloat16), preferred_element_type=jnp.float32
    )


def normed_grad_of(grad_pre, blocks_t, cols, counts):
    tok = grad_pre.shape[0]
    row_blocks = blocks_t.shape[0]
    width = ROWS_PER_STEP * BLK
    spec = pltpu.PrefetchScalarGridSpec(
        num_scalar_prefetch=2,
        grid=(row_blocks // ROWS_PER_STEP,),
        in_specs=[
            pl.BlockSpec((tok, KVW), lambda g, c, n: (0, 0)),
            pl.BlockSpec((ROWS_PER_STEP, MOSTR, BLK, BLK), lambda g, c, n: (g, 0, 0, 0)),
        ],
        out_specs=pl.BlockSpec((tok, width), lambda g, c, n: (0, g)),
        scratch_shapes=[pltpu.VMEM((KVW, width), jnp.float32)],
    )
    return pl.pallas_call(
        _normed_grad_kernel,
        grid_spec=spec,
        out_shape=jax.ShapeDtypeStruct((tok, row_blocks * BLK), jnp.float32),
    )(cols.reshape(-1), counts, grad_pre, blocks_t)


def shards(checkpoint, norm_gain, key_cotangent, positions, kept_cols, kept_count, key_blocks):
    tok_rows = checkpoint.shape[0]
    groups = lax.axis_size("x") * lax.axis_size("c")
    dp_size = lax.axis_size("z") * lax.axis_size("y")
    part_rows = BLK // groups
    row_blocks = D // BLK
    col_blocks = KVW // BLK
    xf = checkpoint.astype(jnp.float32)
    inv_rms = lax.rsqrt(jnp.mean(xf * xf, axis=1, keepdims=True) + 1e-05)
    normed = (xf * inv_rms * norm_gain).astype(jnp.bfloat16)
    grad_pre = rope_back(key_cotangent, positions)

    local_t = key_blocks.reshape(key_blocks.shape[0], MOSTR, BLK, BLK).transpose(0, 1, 3, 2)
    piece = lax.all_gather(local_t, "y", axis=0, tiled=True)
    piece = lax.all_gather(piece, "z", axis=0, tiled=True)

    grad_all = lax.all_gather(grad_pre, ("x", "c"), axis=0, tiled=True)
    split_normed = (
        normed.reshape(tok_rows, row_blocks, groups, part_rows)
        .transpose(0, 2, 1, 3)
        .reshape(tok_rows, groups, row_blocks * part_rows)
    )
    received = lax.all_to_all(split_normed, ("x", "c"), split_axis=1, concat_axis=0, tiled=True)
    normed_rows = received.reshape(groups * tok_rows, row_blocks, part_rows)
    divisor = math.sqrt(SEQ_LEN * dp_size)
    count = row_blocks
    slab = normed_rows.reshape(groups * tok_rows, count * part_rows)
    product = lax.dot_general(
        slab, grad_all, (((0,), (0,)), ((), ())), preferred_element_type=jnp.float32
    )
    shaped = (
        product.reshape(count, part_rows, col_blocks, BLK)
        .transpose(0, 2, 1, 3)
        .reshape(count, col_blocks, part_rows * BLK)
    )
    picked = jnp.take_along_axis(shaped, kept_cols[:, :, None], axis=1)
    live = lax.broadcasted_iota(jnp.int32, (count, MOSTR), 1) < kept_count[:, None]
    partial = jnp.where(live[:, :, None], picked / divisor, jnp.float32(0.0))
    block_grad = lax.psum_scatter(partial, "z", scatter_dimension=0, tiled=True)
    block_grad = lax.psum_scatter(block_grad, "y", scatter_dimension=0, tiled=True)

    normed_grad = normed_grad_of(grad_pre, piece, kept_cols, kept_count)
    scaled = norm_gain * normed_grad
    grads = inv_rms * scaled - inv_rms**3 * xf * jnp.mean(scaled * xf, axis=1, keepdims=True)
    return (grads.astype(jnp.bfloat16), block_grad)


def _split_mesh(mesh):
    devs = mesh.devices
    dp, seq = devs.shape
    ys = len({d.coords[1] for d in devs[:, 0]}) if hasattr(devs[0, 0], "coords") else 1
    cores = 2 if seq % 2 == 0 else 1
    return Mesh(devs.reshape(dp // ys, ys, seq // cores, cores), ("z", "y", "x", "c"))


def solution(mesh):
    fine = _split_mesh(mesh)
    rows = ("z", "y", "x", "c")
    placed = (
        P(rows, None),
        P(),
        P(rows, None),
        P(rows),
        P(),
        P(),
        P(("z", "y"), None, None),
    )
    return jax.shard_map(
        shards,
        mesh=fine,
        in_specs=placed,
        out_specs=(P(rows, None), P(("z", "y"), None, ("x", "c"))),
        check_vma=False,
    )
```

time: 582 us -> 376 us (0.65)
  waiting for transfers between devices: 369 us -> 244 us
  local copies, waits for them, and re-layouts: 146 us -> 33.3 us
  blocking collectives: 0 us -> 31.6 us
  Pallas kernels: 0 us -> 31.4 us
  matrix products: 33.1 us -> 4.9 us
    reduce_scatter x1 -> x2, waiting for transfers between devices: 242 us -> 83.3 us  [the longest x1 43.6 us: shards(): block_grad = lax.psum_scatter(partial, 'z', scatter_dimension=0, tiled=True)]
    transpose x1, local copies, waits for them, and re-layouts: 46 us -> 0.15 us  [shards(): key_blocks.reshape(key_blocks.shape[0], MOSTR, BLK, BLK)]
    reshape x1 -> x2, local copies, waits for them, and re-layouts: 44.3 us -> 1.84 us  [the longest x1 1.11 us: shards(): key_blocks.reshape(key_blocks.shape[0], MOSTR, BLK, BLK)]
    all_gather x2, waiting for transfers between devices: 102 us -> 136 us  [the longest x1 136 us: shards(): piece = lax.all_gather(piece, 'z', axis=0, tiled=True)]
    all_gather x0 -> x1, blocking collectives: none -> 31.6 us  [shards(): piece = lax.all_gather(local_t, 'y', axis=0, tiled=True)]
    pallas_call x0 -> x1, Pallas kernels: none -> 31.4 us  [normed_grad_of(): pl.pallas_call(_normed_grad_kernel, grid_spec=spec, out_shape=jax.ShapeDt...]
    dot_general x2 -> x0, matrix products: 28.2 us -> none  [the longest x1 14.6 us: densify(): lax.dot_general(onehot, blocks, (((1,), (1,)), ((0,), (0,))), preferred_e...]
    dot_general x1 -> x0, local copies, waits for them, and re-layouts: 22.6 us -> none  [densify(): lax.dot_general(onehot, blocks, (((1,), (1,)), ((0,), (0,))), preferred_e...]
  transfers between devices with their start and end apart: 4 -> 5, of which waited for: 3 -> 4; matrix products, arithmetic and copies ran while one was open for 28% -> 6% of each run, Pallas kernels for 0% -> 8%
where the time goes in v1:
time: 376 us; the launch traced here: 375 us
  waiting for transfers between devices  244 us (65%)
  local copies, waits for them, and re-layouts  33.3 us (9%)
  blocking collectives  31.6 us (8%)
  Pallas kernels  31.4 us (8%)
  between operations  13.9 us (4%)
  other arithmetic  11 us (3%)
  starting transfers between devices  5.09 us (1%)
  matrix products  4.9 us (1%)
    all_gather x1, waiting for transfers between devices, shards(): piece = lax.all_gather(piece, 'z', axis=0, tiled=True)  136 us
    reduce_scatter x1, waiting for transfers between devices, shards(): block_grad = lax.psum_scatter(partial, 'z', scatter_dimension=0, tiled=True)  43.6 us
    reduce_scatter x1, waiting for transfers between devices, shards(): lax.psum_scatter(block_grad, 'y', scatter_dimension=0, tiled=True)  39.7 us
    all_gather x1, blocking collectives, shards(): piece = lax.all_gather(local_t, 'y', axis=0, tiled=True)  31.6 us
    pallas_call x1, Pallas kernels, normed_grad_of(): pl.pallas_call(_normed_grad_kernel, grid_spec=spec, out_shape=jax.ShapeDt...  31.4 us
    all_to_all x1, waiting for transfers between devices, shards(): lax.all_to_all(split_normed, ('x', 'c'), split_axis=1, concat_axis=0, til...  24.6 us
    gather x4, local copies, waits for them, and re-layouts, shards(): picked = jnp.take_along_axis(shaped, kept_cols[:, :, None], axis=1)  9.31 us
  transfers between devices with their start and end apart: 5, of which 4 were waited for; matrix products, arithmetic and copies ran while one was open for 6% of the time, Pallas kernels for 8%

profile of v1, /device:TPU:6, one launch (start us, length us, event | category | flops | bytes accessed | tf_op | source)
XLA Modules:
  0.0 375.2 jit_solution(16093682329302954658)
XLA Ops:
  7.2 1.1 reshape.131
  8.5 31.6 %all_gather.9 = bf16[16,6,64,64]{3,2,1,0:T(8,128)(2,1)} all-gather(bf16[2,6,64,64]{3,2,1,0:T(8,128)(2,1)S(1)} %copy.27), channel_id=1, replica_groups=mesh['z'=8,'y'=8,'x'=4,'c'=2] {'y'}, dimensions={0}, use_global_device_ids=true | all-gather | bytes 884736 | tf_op jit(solution)/shard_map/all_gather | solution.py:87
  40.7 0.7 pad_maximum_fusion
  41.5 1.8 copy.28.gp_ref
  43.4 0.7 reshape.128.cols_ref
  44.1 136.1 %all-gather.3.cloned.1.call-done.bt_ref = bf16[128,6,64,64]{3,2,1,0:T(8,128)(2,1)} async-done(((bf16[16,6,64,64]{3,2,1,0:T(8,128)(2,1)}), bf16[128,6,64,64]{3,2,1,0:T(8,128)(2,1)}) %all-gather.3.cloned.1.call-update) | async-done | bytes 6291472 | tf_op jit(solution)/shard_map/all_gather | solution.py:88
  180.2 31.4 %shard_map.86 = f32[128,8192]{1,0:T(8,128)} custom-call(s32[768]{0:T(1024)} %reshape.128.cols_ref, s32[128]{0:T(128)} %cnt_ref.1, bf16[128,1024]{1,0:T(8,128)(2,1)} %copy.28.gp_ref, bf16[128,6,64,64]{3,2,1,0:T(8,128)(2,1)} %all-gather.3.cloned.1.call-done.bt_ref), custom_call_target="tpu_custom_call" | custom-call | tf_op jit(solution)/shard_map/pallas_call | solution.py:67
  211.6 3.3 fusion
  215.1 3.7 fusion.6
  218.8 3.2 copy.30
  222.0 1.7 copy.45
  223.8 5.0 %all-to-all-start = ((bf16[128,8,1024]{0,2,1:T(8,128)(2,1)}), bf16[128,8,1024]{0,2,1:T(8,128)(2,1)S(1)}, u32[]{:S(2)}, u32[]{:S(2)}) async-start(bf16[128,8,1024]{0,2,1:T(8,128)(2,1)} %bitcast.36), calls=%async_computation | async-start | bytes 4194304 | tf_op jit(solution)/shard_map/all_to_all | solution.py:96
  229.2 24.6 %all-to-all-done = bf16[128,8,1024]{0,2,1:T(8,128)(2,1)S(1)} async-done(((bf16[128,8,1024]{0,2,1:T(8,128)(2,1)}), bf16[128,8,1024]{0,2,1:T(8,128)(2,1)S(1)}, u32[]{:S(2)}, u32[]{:S(2)}) %all-to-all-start) | async-done | bytes 2097184 | tf_op jit(solution)/shard_map/all_to_all | solution.py:96
  253.9 2.6 copy.32
  256.5 2.9 copy.33
  259.4 4.9 %convolution_bitcast_fusion = f32[128,16,8,64]{0,3,1,2:T(8,128)S(1)} fusion(bf16[16,64,1024,1]{2,1,0,3:T(8,128)(2,1)} %bitcast.44, bf16[128,8,1024,1]{2,1,0,3:T(8,128)(2,1)S(1)} %bitcast.41), kind=kOutput, calls=%fused_computation.12 | convolution fusion | flops 2147483648 | bytes 8388608 | tf_op jit(solution)/shard_map/dot_general | solution.py:101
  264.3 2.3 copy.35
  266.5 5.5 %copy.37 = f32[128,16,512]{2,1,0:T(8,128)} copy(f32[128,16,512]{0,2,1:T(8,128)} %bitcast.34) | data formatting | bytes 8388608 | tf_op jit(solution)/shard_map/reshape | solution.py:107
  272.0 7.5 %gather_fusion = f32[768,512]{1,0:T(8,128)S(1)} fusion(f32[128,16,512]{2,1,0:T(8,128)} %copy.37, s32[768]{0:T(1024)S(1)} %reshape.137), kind=kCustom, calls=%fused_computation | custom fusion | bytes 3151872 | tf_op jit(solution)/shard_map/jit(take_along_axis)/gather | solution.py:109
  279.6 1.5 reshape.140
  281.1 2.8 multiply_select_fusion
  284.0 43.6 %reduce-scatter.3.cloned.1.call-done = f32[16,6,512]{2,1,0:T(8,128)} async-done(((f32[128,6,512]{2,1,0:T(8,128)}), f32[16,6,512]{2,1,0:T(8,128)}) %reduce-scatter.3.cloned.1.call-update) | async-done | bytes 196624 | tf_op jit(solution)/shard_map/reduce_scatter | solution.py:112
  327.6 39.7 %reduce-scatter.5.cloned.1.call-done = f32[2,6,512]{2,1,0:T(8,128)} async-done(((f32[16,6,512]{2,1,0:T(8,128)}), f32[2,6,512]{2,1,0:T(8,128)}) %reduce-scatter.5.cloned.1.call-update) | async-done | bytes 24592 | tf_op jit(solution)/shard_map/reduce_scatter | solution.py:113
  367.3 1.4 copy.38
  (38 shorter events, 1.7 us)
Async XLA Ops:
  7.2 33.0 %copy-start.6 = (s32[128]{0:T(128)S(1)}, s32[128]{0:T(128)}, u32[]{:S(2)}) copy-start(s32[128]{0:T(128)} %param.10) | copy-start | bytes 1540
  7.2 33.0 %copy-start.2 = (bf16[128,1024]{1,0:T(8,128)(2,1)S(1)}, bf16[128,1024]{1,0:T(8,128)(2,1)}, u32[]{:S(2)}) copy-start(bf16[128,1024]{1,0:T(8,128)(2,1)} %param.9) | copy-start | bytes 786436
  7.2 173.0 %all-gather.3.cloned.1.call-start = ((), (), s32[]{:S(2)}) async-start(), calls=%async_computation.3 | async-start | bytes 14155776 | tf_op jit(solution)/shard_map/all_gather | solution.py:88
  40.1 3.2 copy-start.4
  40.1 219.2 %all-gather.5.cloned.1.call-start = ((), (), s32[]{:S(2)}) async-start(), calls=%async_computation.4 | async-start | bytes 2359296 | tf_op jit(solution)/shard_map/all_gather | solution.py:90
  44.1 167.5 %copy-start.1 = (bf16[128,8192]{1,0:T(8,128)(2,1)S(1)}, bf16[128,8192]{1,0:T(8,128)(2,1)}, u32[]{:S(2)}) copy-start(bf16[128,8192]{1,0:T(8,128)(2,1)} %param.7) | copy-start | bytes 6291460
  44.1 167.5 %copy-start.3 = (f32[8192]{0:T(1024)S(1)}, f32[8192]{0:T(1024)}, u32[]{:S(2)}) copy-start(f32[8192]{0:T(1024)} %param.8) | copy-start | bytes 98308
  211.6 3.5 copy-start
  223.8 5.4 %copy-start.5 = (s32[128]{0:T(128)S(1)}, s32[128]{0:T(128)}, u32[]{:S(2)}) copy-start(s32[128]{0:T(128)} %cnt_ref.1) | copy-start | bytes 1540
  223.8 30.1 %all-to-all-start = ((bf16[128,8,1024]{0,2,1:T(8,128)(2,1)}), bf16[128,8,1024]{0,2,1:T(8,128)(2,1)S(1)}, u32[]{:S(2)}, u32[]{:S(2)}) async-start(bf16[128,8,1024]{0,2,1:T(8,128)(2,1)} %bitcast.36), calls=%async_computation | async-start | bytes 4194304 | tf_op jit(solution)/shard_map/all_to_all | solution.py:96
  228.7 98.9 %reduce-scatter.3.cloned.1.call-start = ((), (), s32[]{:S(2)}) async-start(), calls=%async_computation.5 | async-start | bytes 2359296 | tf_op jit(solution)/shard_map/reduce_scatter | solution.py:112
  283.9 83.4 %reduce-scatter.5.cloned.1.call-start = ((), (), s32[]{:S(2)}) async-start(), calls=%async_computation.6 | async-start | bytes 294912 | tf_op jit(solution)/shard_map/reduce_scatter | solution.py:113
Sparse Core Ops, SparseCore 0:
  40.2 139.9 all-gather.2
  182.3 30.1 all-gather.4
  284.1 43.4 reduce-scatter.2
  330.2 37.0 reduce-scatter.4

commit v2 on v1

--- a/solution.py
+++ b/solution.py
@@ -33,21 +33,31 @@
 
 def _normed_grad_kernel(cols_ref, cnt_ref, gp_ref, bt_ref, out_ref, w_ref):
     step = pl.program_id(0)
-    w_ref[...] = jnp.zeros(w_ref.shape, w_ref.dtype)
-    for rr in range(ROWS_PER_STEP):
-        row = step * ROWS_PER_STEP + rr
-        live = cnt_ref[row]
-        for k in range(MOSTR):
-            col = cols_ref[row * MOSTR + k]
 
-            @pl.when(k < live)
-            def _():
-                start = pl.multiple_of(col * BLK, BLK)
-                w_ref[pl.ds(start, BLK), rr * BLK:(rr + 1) * BLK] = bt_ref[rr, k].astype(jnp.float32)
+    @pl.when(step == 0)
+    def _():
+        w_ref[...] = jnp.zeros(w_ref.shape, w_ref.dtype)
 
-    out_ref[...] = jnp.dot(
-        gp_ref[...], w_ref[...].astype(jnp.bfloat16), preferred_element_type=jnp.float32
-    )
+    def place(fill):
+        for rr in range(ROWS_PER_STEP):
+            row = step * ROWS_PER_STEP + rr
+            live = cnt_ref[row]
+            for k in range(MOSTR):
+                col = cols_ref[row * MOSTR + k]
+
+                @pl.when(k < live)
+                def _():
+                    start = pl.multiple_of(col * BLK, BLK)
+                    half = (k % 2) * BLK
+                    if fill:
+                        value = bt_ref[rr, k // 2, :, half:half + BLK]
+                    else:
+                        value = jnp.zeros((BLK, BLK), w_ref.dtype)
+                    w_ref[pl.ds(start, BLK), rr * BLK:(rr + 1) * BLK] = value
+
+    place(True)
+    out_ref[...] = jnp.dot(gp_ref[...], w_ref[...], preferred_element_type=jnp.float32)
+    place(False)
 
 
 def normed_grad_of(grad_pre, blocks_t, cols, counts):
@@ -59,15 +69,16 @@
         grid=(row_blocks // ROWS_PER_STEP,),
         in_specs=[
             pl.BlockSpec((tok, KVW), lambda g, c, n: (0, 0)),
-            pl.BlockSpec((ROWS_PER_STEP, MOSTR, BLK, BLK), lambda g, c, n: (g, 0, 0, 0)),
+            pl.BlockSpec((ROWS_PER_STEP, MOSTR // 2, BLK, 2 * BLK), lambda g, c, n: (g, 0, 0, 0)),
         ],
         out_specs=pl.BlockSpec((tok, width), lambda g, c, n: (0, g)),
-        scratch_shapes=[pltpu.VMEM((KVW, width), jnp.float32)],
+        scratch_shapes=[pltpu.VMEM((KVW, width), jnp.bfloat16)],
     )
     return pl.pallas_call(
         _normed_grad_kernel,
         grid_spec=spec,
         out_shape=jax.ShapeDtypeStruct((tok, row_blocks * BLK), jnp.float32),
+        compiler_params=pltpu.CompilerParams(dimension_semantics=("arbitrary",)),
     )(cols.reshape(-1), counts, grad_pre, blocks_t)
 
 
@@ -83,18 +94,25 @@
     normed = (xf * inv_rms * norm_gain).astype(jnp.bfloat16)
     grad_pre = rope_back(key_cotangent, positions)
 
-    local_t = key_blocks.reshape(key_blocks.shape[0], MOSTR, BLK, BLK).transpose(0, 1, 3, 2)
-    piece = lax.all_gather(local_t, "y", axis=0, tiled=True)
-    piece = lax.all_gather(piece, "z", axis=0, tiled=True)
+    local_t = (
+        key_blocks.reshape(key_blocks.shape[0], MOSTR // 2, 2, BLK, BLK)
+        .transpose(0, 1, 4, 2, 3)
+        .reshape(key_blocks.shape[0], MOSTR // 2, BLK, 2 * BLK)
+    )
+    piece = lax.all_gather(local_t, ("z", "y"), axis=0, tiled=True)
 
-    grad_all = lax.all_gather(grad_pre, ("x", "c"), axis=0, tiled=True)
     split_normed = (
         normed.reshape(tok_rows, row_blocks, groups, part_rows)
         .transpose(0, 2, 1, 3)
         .reshape(tok_rows, groups, row_blocks * part_rows)
     )
-    received = lax.all_to_all(split_normed, ("x", "c"), split_axis=1, concat_axis=0, tiled=True)
-    normed_rows = received.reshape(groups * tok_rows, row_blocks, part_rows)
+    sent = jnp.concatenate(
+        [split_normed, jnp.broadcast_to(grad_pre[:, None, :], (tok_rows, groups, KVW))], axis=2
+    )
+    received = lax.all_to_all(sent, ("x", "c"), split_axis=1, concat_axis=0, tiled=True)
+    received = received.reshape(groups * tok_rows, row_blocks * part_rows + KVW)
+    grad_all = received[:, row_blocks * part_rows:]
+    normed_rows = received[:, : row_blocks * part_rows].reshape(groups * tok_rows, row_blocks, part_rows)
     divisor = math.sqrt(SEQ_LEN * dp_size)
     count = row_blocks
     slab = normed_rows.reshape(groups * tok_rows, count * part_rows)
@@ -109,6 +127,7 @@
     picked = jnp.take_along_axis(shaped, kept_cols[:, :, None], axis=1)
     live = lax.broadcasted_iota(jnp.int32, (count, MOSTR), 1) < kept_count[:, None]
     partial = jnp.where(live[:, :, None], picked / divisor, jnp.float32(0.0))
+    partial, piece = lax.optimization_barrier((partial, piece))
     block_grad = lax.psum_scatter(partial, "z", scatter_dimension=0, tiled=True)
     block_grad = lax.psum_scatter(block_grad, "y", scatter_dimension=0, tiled=True)
 

time: 376 us -> 226 us (0.60)
  waiting for transfers between devices: 244 us -> 89.6 us
  blocking collectives: 31.6 us -> 0 us
  local copies, waits for them, and re-layouts: 33.3 us -> 53 us
  other arithmetic: 11 us -> 17.6 us
  starting transfers between devices: 5.09 us -> 10.7 us
    all_gather x2 -> x1, waiting for transfers between devices: 136 us -> 0.01 us  [shards(): piece = lax.all_gather(local_t, ('z', 'y'), axis=0, tiled=True)]
    reduce_scatter x1, waiting for transfers between devices: 43.6 us -> 7.07 us  [shards(): block_grad = lax.psum_scatter(partial, 'z', scatter_dimension=0, tiled=True)]
    all_gather x1 -> x0, blocking collectives: 31.6 us -> none  [shards(): piece = lax.all_gather(local_t, 'y', axis=0, tiled=True)]
    all_to_all x1, waiting for transfers between devices: 24.6 us -> 47.2 us  [shards(): lax.all_to_all(sent, ('x', 'c'), split_axis=1, concat_axis=0, tiled=True)]
    reshape x1 -> x4, local copies, waits for them, and re-layouts: 1.11 us -> 9.51 us  [the longest x1 7.37 us: shards(): product.reshape(count, part_rows, col_blocks, BLK).transpose(0, 2, 1, 3)]
    transpose x1, local copies, waits for them, and re-layouts: 2.26 us -> 8.08 us  [shards(): shaped = product.reshape(count, part_rows, col_blocks, BLK).transpose(0,...]
    all_to_all x1, starting transfers between devices: 4.96 us -> 10.4 us  [shards(): lax.all_to_all(sent, ('x', 'c'), split_axis=1, concat_axis=0, tiled=True)]
    convert_element_type x0 -> x1, other arithmetic: none -> 4.7 us  [shards(): return (grads.astype(jnp.bfloat16), block_grad)]
  transfers between devices with their start and end apart: 5 -> 4, of which waited for: 4 -> 3; matrix products, arithmetic and copies ran while one was open for 6% -> 33% of each run, Pallas kernels for 8% -> 15%
where the time goes in v2:
time: 226 us; the launch traced here: 224 us
  waiting for transfers between devices  89.6 us (40%)
  local copies, waits for them, and re-layouts  53 us (23%)
  Pallas kernels  32.8 us (15%)
  other arithmetic  17.6 us (8%)
  between operations  13.9 us (6%)
  starting transfers between devices  10.7 us (5%)
  matrix products  6.68 us (3%)
    all_to_all x1, waiting for transfers between devices, shards(): lax.all_to_all(sent, ('x', 'c'), split_axis=1, concat_axis=0, tiled=True)  47.2 us
    reduce_scatter x1, waiting for transfers between devices, shards(): lax.psum_scatter(block_grad, 'y', scatter_dimension=0, tiled=True)  35.3 us
    pallas_call x1, Pallas kernels, normed_grad_of(): pl.pallas_call(_normed_grad_kernel, grid_spec=spec, out_shape=jax.ShapeDt...  32.8 us
    gather x4, local copies, waits for them, and re-layouts, shards(): picked = jnp.take_along_axis(shaped, kept_cols[:, :, None], axis=1)  12.6 us
    all_to_all x1, starting transfers between devices, shards(): lax.all_to_all(sent, ('x', 'c'), split_axis=1, concat_axis=0, tiled=True)  10.4 us
    transpose x1, local copies, waits for them, and re-layouts, shards(): shaped = product.reshape(count, part_rows, col_blocks, BLK).transpose(0,...  8.08 us
    reshape x1, local copies, waits for them, and re-layouts, shards(): product.reshape(count, part_rows, col_blocks, BLK).transpose(0, 2, 1, 3)  7.37 us
    reduce_scatter x1, waiting for transfers between devices, shards(): block_grad = lax.psum_scatter(partial, 'z', scatter_dimension=0, tiled=True)  7.07 us
  transfers between devices with their start and end apart: 4, of which 3 were waited for; matrix products, arithmetic and copies ran while one was open for 33% of the time, Pallas kernels for 15%

profile of v2, /device:TPU:6, one launch (start us, length us, event | category | flops | bytes accessed | tf_op | source)
XLA Modules:
  0.0 224.3 jit_solution(17908082648125437391)
XLA Ops:
  7.2 1.2 reshape.147
  10.1 1.1 copy.25
  11.2 2.1 fusion
  13.3 1.9 fusion.2
  15.2 4.1 %copy.27 = bf16[128,8192]{0,1:T(8,128)(2,1)} copy(bf16[128,8192]{1,0:T(8,128)(2,1)} %fusion.2) | data formatting | bytes 4194304 | tf_op jit(solution)/shard_map/convert_element_type | solution.py:94
  19.3 2.0 copy.37
  21.9 2.2 %pad_maximum_fusion = bf16[128,8,2048]{0,2,1:T(8,128)(2,1)} fusion(bf16[128,8,1024]{0,2,1:T(8,128)(2,1)S(1)} %broadcast_in_dim.20, bf16[128,8,1024]{0,2,1:T(8,128)(2,1)S(1)} %bitcast.25), kind=kLoop, calls=%fused_computation.12 | loop fusion | flops 8388608 | bytes 8388608 | tf_op jit(solution)/shard_map/concatenate | solution.py:109
  24.2 10.4 %all-to-all-start = ((bf16[128,8,2048]{0,2,1:T(8,128)(2,1)}), bf16[128,8,2048]{0,2,1:T(8,128)(2,1)}, u32[]{:S(2)}, u32[]{:S(2)}) async-start(bf16[128,8,2048]{0,2,1:T(8,128)(2,1)} %pad_maximum_fusion), calls=%async_computation | async-start | bytes 8388608 | tf_op jit(solution)/shard_map/all_to_all | solution.py:112
  35.1 47.2 %all-to-all-done = bf16[128,8,2048]{0,2,1:T(8,128)(2,1)} async-done(((bf16[128,8,2048]{0,2,1:T(8,128)(2,1)}), bf16[128,8,2048]{0,2,1:T(8,128)(2,1)}, u32[]{:S(2)}, u32[]{:S(2)}) %all-to-all-start) | async-done | bytes 4194336 | tf_op jit(solution)/shard_map/all_to_all | solution.py:112
  82.3 6.6 %copy.29 = bf16[8,128,1,2048]{3,1,0,2:T(8,128)(2,1)} copy(bf16[8,128,1,2048]{1,3,0,2:T(8,128)(2,1)} %bitcast.7) | data formatting | bytes 8388608 | tf_op jit(solution)/shard_map/all_to_all | solution.py:112
  88.9 6.7 %fusion.7 = f32[1024,1024]{1,0:T(8,128)} fusion(bf16[1024,2048]{1,0:T(8,128)(2,1)} %bitcast.26), kind=kOutput, calls=%fused_computation.13 | convolution fusion | flops 2147483648 | bytes 8388608 | tf_op jit(solution)/shard_map/dot_general | solution.py:119
  95.6 7.4 %reshape.145 = f32[128,8,16,64]{3,2,1,0:T(8,128)} reshape(f32[1024,1024]{1,0:T(8,128)} %fusion.7) | data formatting | bytes 8388608 | tf_op jit(solution)/shard_map/reshape | solution.py:123
  102.9 8.1 %copy.30 = f32[128,16,8,64]{0,3,2,1:T(8,128)} copy(f32[128,16,8,64]{3,1,2,0:T(8,128)} %bitcast.22) | data formatting | bytes 8388608 | tf_op jit(solution)/shard_map/transpose | solution.py:124
  111.0 5.5 %copy.32 = f32[128,16,512]{2,1,0:T(8,128)} copy(f32[128,16,512]{0,2,1:T(8,128)} %bitcast.23) | data formatting | bytes 8388608 | tf_op jit(solution)/shard_map/reshape | solution.py:125
  116.5 9.8 %gather_fusion = f32[768,512]{1,0:T(8,128)} fusion(f32[128,16,512]{2,1,0:T(8,128)} %copy.32, s32[768]{0:T(1024)S(1)} %reshape.151), kind=kCustom, calls=%fused_computation | custom fusion | bytes 3151872 | tf_op jit(solution)/shard_map/jit(take_along_axis)/gather | solution.py:127
  126.3 2.6 %reshape.154 = f32[128,6,512]{2,1,0:T(8,128)} reshape(f32[768,512]{1,0:T(8,128)} %gather_fusion) | data formatting | bytes 3145728 | tf_op jit(solution)/shard_map/jit(take_along_axis)/gather | solution.py:127
  128.9 2.8 %multiply_select_fusion = f32[128,6,512]{2,1,0:T(8,128)} fusion(f32[128,6,512]{2,1,0:T(8,128)} %reshape.154, pred[128,6]{1,0:T(8,128)(4,1)S(1)} %copy.26, pred[128,6]{1,0:T(8,128)(4,1)S(1)} %iota_compare_fusion), kind=kLoop, calls=%fused_computation.17 | loop fusion | flops 1179648 | bytes 3147264 | tf_op jit(solution)/shard_map/jit(_where)/select_n | solution.py:129
  132.0 0.9 copy.34.gp_ref
  133.7 32.8 %shard_map.86 = f32[128,8192]{1,0:T(8,128)} custom-call(s32[768]{0:T(1024)} %reshape.139.cols_ref, s32[128]{0:T(128)} %cnt_ref.1, bf16[128,1024]{1,0:T(8,128)(2,1)} %copy.34.gp_ref, bf16[128,3,64,128]{3,2,1,0:T(8,128)(2,1)} %all-gather.2.cloned.1.call-done.bt_ref), custom_call_target="tpu_custom_call" | custom-call | tf_op jit(solution)/shard_map/pallas_call | solution.py:77
  166.4 2.8 %fusion.6 = f32[128]{0:T(128)S(1)} fusion(bf16[128,8192]{1,0:T(8,128)(2,1)S(1)} %copy-done, f32[128,8192]{1,0:T(8,128)} %shard_map.86, f32[8192]{0:T(1024)S(1)} %copy-done.1), kind=kLoop, calls=%fused_computation.11 | loop fusion | flops 4194176 | bytes 6324736 | tf_op jit(solution)/shard_map/reduce_sum | solution.py:136
  169.3 7.1 %reduce-scatter.3.cloned.1.call-done = f32[16,6,512]{2,1,0:T(8,128)} async-done(((f32[128,6,512]{2,1,0:T(8,128)}), f32[16,6,512]{2,1,0:T(8,128)}) %reduce-scatter.3.cloned.1.call-update) | async-done | bytes 196624 | tf_op jit(solution)/shard_map/reduce_scatter | solution.py:131
  176.4 4.7 %fusion.5 = bf16[128,8192]{1,0:T(8,128)(2,1)} fusion(bf16[128,8192]{1,0:T(8,128)(2,1)S(1)} %copy-done, f32[128,8192]{1,0:T(8,128)} %shard_map.86, f32[128]{0:T(128)S(1)} %broadcast_multiply_fusion, f32[128]{0:T(128)S(1)} %get-tuple-element.14, f32[8192]{0:T(1024)S(1)} %copy-done.1, f32[128]{0:T(128)S(1)} %get-tuple-element.15), kind=kLoop, calls=%fused_computation.10 | loop fusion | flops 7340032 | bytes 8422912 | tf_op jit(solution)/shard_map/convert_element_type | solution.py:137
  181.1 35.3 %reduce-scatter.5.cloned.1.call-done = f32[2,6,512]{2,1,0:T(8,128)} async-done(((f32[16,6,512]{2,1,0:T(8,128)}), f32[2,6,512]{2,1,0:T(8,128)}) %reduce-scatter.5.cloned.1.call-update) | async-done | bytes 24592 | tf_op jit(solution)/shard_map/reduce_scatter | solution.py:132
  216.4 1.4 copy.35
  (34 shorter events, 3.9 us)
Async XLA Ops:
  7.2 6.2 %copy-start = (bf16[128,8192]{1,0:T(8,128)(2,1)S(1)}, bf16[128,8192]{1,0:T(8,128)(2,1)}, u32[]{:S(2)}) copy-start(bf16[128,8192]{1,0:T(8,128)(2,1)} %param.7) | copy-start | bytes 6291460
  7.2 6.2 %copy-start.1 = (f32[8192]{0:T(1024)S(1)}, f32[8192]{0:T(1024)}, u32[]{:S(2)}) copy-start(f32[8192]{0:T(1024)} %param.8) | copy-start | bytes 98308
  7.2 124.5 %all-gather.2.cloned.1.call-start = ((), (), s32[]{:S(2)}) async-start(), calls=%async_computation.3 | async-start | bytes 6389760 | tf_op jit(solution)/shard_map/all_gather | solution.py:102
  24.2 10.5 %copy-start.2 = (s32[128,6]{0,1:T(8,128)S(1)}, s32[128,6]{0,1:T(8,128)}, u32[]{:S(2)}) copy-start(s32[128,6]{0,1:T(8,128)} %param.11) | copy-start | bytes 9220
  24.2 10.9 %copy-start.3 = (s32[128]{0:T(128)S(1)}, s32[128]{0:T(128)}, u32[]{:S(2)}) copy-start(s32[128]{0:T(128)} %cnt_ref.1) | copy-start | bytes 1540
  24.2 58.1 %all-to-all-start = ((bf16[128,8,2048]{0,2,1:T(8,128)(2,1)}), bf16[128,8,2048]{0,2,1:T(8,128)(2,1)}, u32[]{:S(2)}, u32[]{:S(2)}) async-start(bf16[128,8,2048]{0,2,1:T(8,128)(2,1)} %pad_maximum_fusion), calls=%async_computation | async-start | bytes 8388608 | tf_op jit(solution)/shard_map/all_to_all | solution.py:112
  34.6 141.7 %reduce-scatter.3.cloned.1.call-start = ((), (), s32[]{:S(2)}) async-start(), calls=%async_computation.4 | async-start | bytes 2359296 | tf_op jit(solution)/shard_map/reduce_scatter | solution.py:131
  131.7 84.7 %reduce-scatter.5.cloned.1.call-start = ((), (), s32[]{:S(2)}) async-start(), calls=%async_computation.5 | async-start | bytes 294912 | tf_op jit(solution)/shard_map/reduce_scatter | solution.py:132
Sparse Core Ops, SparseCore 0:
  11.0 95.3 all-gather.1
  131.8 44.4 reduce-scatter.2
  179.2 37.2 reduce-scatter.4

commit v3 on v2

--- a/solution.py
+++ b/solution.py
@@ -43,17 +43,14 @@
             row = step * ROWS_PER_STEP + rr
             live = cnt_ref[row]
             for k in range(MOSTR):
-                col = cols_ref[row * MOSTR + k]
-
-                @pl.when(k < live)
-                def _():
-                    start = pl.multiple_of(col * BLK, BLK)
+                start = pl.multiple_of(cols_ref[row * MOSTR + k] * BLK, BLK)
+                if fill:
                     half = (k % 2) * BLK
-                    if fill:
-                        value = bt_ref[rr, k // 2, :, half:half + BLK]
-                    else:
-                        value = jnp.zeros((BLK, BLK), w_ref.dtype)
-                    w_ref[pl.ds(start, BLK), rr * BLK:(rr + 1) * BLK] = value
+                    value = bt_ref[rr, k // 2, :, half:half + BLK]
+                    value = jnp.where(k < live, value, jnp.zeros_like(value))
+                else:
+                    value = jnp.zeros((BLK, BLK), w_ref.dtype)
+                w_ref[pl.ds(start, BLK), rr * BLK:(rr + 1) * BLK] = value
 
     place(True)
     out_ref[...] = jnp.dot(gp_ref[...], w_ref[...], preferred_element_type=jnp.float32)
@@ -113,23 +110,37 @@
     received = received.reshape(groups * tok_rows, row_blocks * part_rows + KVW)
     grad_all = received[:, row_blocks * part_rows:]
     normed_rows = received[:, : row_blocks * part_rows].reshape(groups * tok_rows, row_blocks, part_rows)
-    divisor = math.sqrt(SEQ_LEN * dp_size)
-    count = row_blocks
-    slab = normed_rows.reshape(groups * tok_rows, count * part_rows)
+    divisor = math.sqrt(tok_rows * groups * dp_size)
+    nz = lax.axis_size("z")
+    ny = lax.axis_size("y")
+    slab = normed_rows.reshape(groups * tok_rows, row_blocks * part_rows)
     product = lax.dot_general(
-        slab, grad_all, (((0,), (0,)), ((), ())), preferred_element_type=jnp.float32
+        grad_all, slab, (((0,), (0,)), ((), ())), preferred_element_type=jnp.float32
     )
-    shaped = (
-        product.reshape(count, part_rows, col_blocks, BLK)
-        .transpose(0, 2, 1, 3)
-        .reshape(count, col_blocks, part_rows * BLK)
+    lanes = row_blocks * part_rows // nz
+    blocks4 = product.reshape(col_blocks, BLK, nz, lanes)
+    lane_row = (
+        lax.broadcasted_iota(jnp.int32, (nz, lanes), 0) * lanes
+        + lax.broadcasted_iota(jnp.int32, (nz, lanes), 1)
+    ) // part_rows
+    lane_cols = kept_cols[lane_row]
+    lane_live = lax.broadcasted_iota(jnp.int32, (nz, lanes, MOSTR), 2) < kept_count[lane_row][:, :, None]
+    partial = jnp.zeros((nz, MOSTR, BLK, lanes), jnp.float32)
+    for c in range(col_blocks):
+        hit = ((lane_cols == c) & lane_live).transpose(0, 2, 1)[:, :, None, :]
+        partial = partial + jnp.where(hit, blocks4[c].transpose(1, 0, 2)[:, None, :, :], 0.0)
+    partial = partial / divisor
+    partial, piece = lax.optimization_barrier((partial, piece))
+    summed = lax.psum_scatter(partial, "z", scatter_dimension=0, tiled=True)
+    sub = lanes // ny
+    summed = summed.reshape(MOSTR, BLK, ny, sub).transpose(2, 0, 3, 1)
+    summed = lax.all_to_all(summed, "y", split_axis=0, concat_axis=0, tiled=True).sum(axis=0)
+    own_rows = sub // part_rows
+    block_grad = (
+        summed.reshape(MOSTR, own_rows, part_rows, BLK)
+        .transpose(1, 0, 2, 3)
+        .reshape(own_rows, MOSTR, part_rows * BLK)
     )
-    picked = jnp.take_along_axis(shaped, kept_cols[:, :, None], axis=1)
-    live = lax.broadcasted_iota(jnp.int32, (count, MOSTR), 1) < kept_count[:, None]
-    partial = jnp.where(live[:, :, None], picked / divisor, jnp.float32(0.0))
-    partial, piece = lax.optimization_barrier((partial, piece))
-    block_grad = lax.psum_scatter(partial, "z", scatter_dimension=0, tiled=True)
-    block_grad = lax.psum_scatter(block_grad, "y", scatter_dimension=0, tiled=True)
 
     normed_grad = normed_grad_of(grad_pre, piece, kept_cols, kept_count)
     scaled = norm_gain * normed_grad

time: 226 us -> 244 us (1.080)
  local copies, waits for them, and re-layouts: 53 us -> 107 us
  waiting for transfers between devices: 89.6 us -> 47.4 us
  other arithmetic: 17.6 us -> 33.5 us
  Pallas kernels: 32.8 us -> 17.6 us
  starting transfers between devices: 10.7 us -> 17.2 us
    all_to_all x1, waiting for transfers between devices: 47.2 us -> 15.1 us  [shards(): lax.all_to_all(sent, ('x', 'c'), split_axis=1, concat_axis=0, tiled=True)]
    unnamed x11 -> x31, local copies, waits for them, and re-layouts: 2.63 us -> 28.8 us
    transpose x1 -> x17, local copies, waits for them, and re-layouts: 8.08 us -> 29.9 us  [the longest x16 28.8 us: shards(): blocks4[c].transpose(1, 0, 2)[:, None, :, :]]
    div x0 -> x1, other arithmetic: none -> 16.4 us  [shards(): partial = partial / divisor]
    reduce_scatter x2 -> x1, waiting for transfers between devices: 42.4 us -> 27.1 us  [shards(): summed = lax.psum_scatter(partial, 'z', scatter_dimension=0, tiled=True)]
    pallas_call x1, Pallas kernels: 32.8 us -> 17.6 us  [normed_grad_of(): pl.pallas_call(_normed_grad_kernel, grid_spec=spec, out_shape=jax.ShapeDt...]
    eq x0 -> x16, local copies, waits for them, and re-layouts: none -> 14.1 us  [shards(): hit = ((lane_cols == c) & lane_live).transpose(0, 2, 1)[:, :, None, :]]
    reshape x2 -> x1, local copies, waits for them, and re-layouts: 12.9 us -> 0.69 us  [shards(): block_grad = summed.reshape(MOSTR, own_rows, part_rows, BLK).transpose(1,...]
  transfers between devices with their start and end apart: 4 -> 4, of which waited for: 3 -> 3; matrix products, arithmetic and copies ran while one was open for 33% -> 57% of each run, Pallas kernels for 15% -> 7%
where the time goes in v3:
time: 244 us; the launch traced here: 241 us
  local copies, waits for them, and re-layouts  107 us (44%)
  waiting for transfers between devices  47.4 us (19%)
  other arithmetic  33.5 us (14%)
  Pallas kernels  17.6 us (7%)
  starting transfers between devices  17.2 us (7%)
  between operations  14.3 us (6%)
  matrix products  4.68 us (2%)
    transpose x16, local copies, waits for them, and re-layouts, shards(): blocks4[c].transpose(1, 0, 2)[:, None, :, :]  28.8 us
    unnamed x31, local copies, waits for them, and re-layouts  28.8 us
    reduce_scatter x1, waiting for transfers between devices, shards(): summed = lax.psum_scatter(partial, 'z', scatter_dimension=0, tiled=True)  27.1 us
    pallas_call x1, Pallas kernels, normed_grad_of(): pl.pallas_call(_normed_grad_kernel, grid_spec=spec, out_shape=jax.ShapeDt...  17.6 us
    div x1, other arithmetic, shards(): partial = partial / divisor  16.4 us
    all_to_all x1, waiting for transfers between devices, shards(): lax.all_to_all(sent, ('x', 'c'), split_axis=1, concat_axis=0, tiled=True)  15.1 us
    eq x16, local copies, waits for them, and re-layouts, shards(): hit = ((lane_cols == c) & lane_live).transpose(0, 2, 1)[:, :, None, :]  14.1 us
    all_to_all x1, starting transfers between devices, shards(): lax.all_to_all(sent, ('x', 'c'), split_axis=1, concat_axis=0, tiled=True)  10.5 us
  transfers between devices with their start and end apart: 4, of which 3 were waited for; matrix products, arithmetic and copies ran while one was open for 57% of the time, Pallas kernels for 7%

profile of v3, /device:TPU:6, one launch (start us, length us, event | category | flops | bytes accessed | tf_op | source)
XLA Modules:
  0.0 241.4 jit_solution(12634683148421962863)
XLA Ops:
  14.2 4.1 %copy.129 = bf16[128,8192]{0,1:T(8,128)(2,1)} copy(bf16[128,8192]{1,0:T(8,128)(2,1)} %fusion.2) | data formatting | bytes 4194304 | tf_op jit(solution)/shard_map/convert_element_type | solution.py:91
  18.3 2.0 copy.214
  20.9 2.3 pad_maximum_fusion
  23.3 10.5 %all-to-all-start = ((bf16[128,8,2048]{0,2,1:T(8,128)(2,1)}), bf16[128,8,2048]{0,2,1:T(8,128)(2,1)}, u32[]{:S(2)}, u32[]{:S(2)}) async-start(bf16[128,8,2048]{0,2,1:T(8,128)(2,1)} %pad_maximum_fusion), calls=%async_computation | async-start | bytes 8388608 | tf_op jit(solution)/shard_map/all_to_all | solution.py:109
  33.9 2.8 %gather_fusion = s32[1024,6]{1,0:T(8,128)S(1)} fusion(s32[128,6]{1,0:T(8,128)S(1)} %copy.124, s32[1024]{0:T(1024)S(1)} %fusion.28), kind=kCustom, calls=%fused_computation | custom fusion | bytes 53248 | tf_op jit(solution)/shard_map/gather | solution.py:126
  36.8 2.0 broadcast_compare_fusion.15
  52.9 6.6 %gather_fusion.1 = s32[1024]{0:T(1024)S(1)} fusion(s32[128]{0:T(128)S(1)} %copy-done, s32[1024]{0:T(1024)S(1)} %fusion.28), kind=kCustom, calls=%fused_computation.1 | custom fusion | bytes 12288 | tf_op jit(solution)/shard_map/gather | solution.py:127
  66.3 15.1 %all-to-all-done = bf16[128,8,2048]{0,2,1:T(8,128)(2,1)} async-done(((bf16[128,8,2048]{0,2,1:T(8,128)(2,1)}), bf16[128,8,2048]{0,2,1:T(8,128)(2,1)}, u32[]{:S(2)}, u32[]{:S(2)}) %all-to-all-start) | async-done | bytes 4194336 | tf_op jit(solution)/shard_map/all_to_all | solution.py:109
  81.4 6.5 %copy.131 = bf16[8,128,1,2048]{3,1,0,2:T(8,128)(2,1)} copy(bf16[8,128,1,2048]{1,3,0,2:T(8,128)(2,1)} %bitcast.11) | data formatting | bytes 8388608 | tf_op jit(solution)/shard_map/all_to_all | solution.py:109
  87.9 4.7 %fusion.7 = f32[1024,1024]{1,0:T(8,128)S(1)} fusion(bf16[1024,2048]{1,0:T(8,128)(2,1)} %bitcast.161), kind=kOutput, calls=%fused_computation.15 | convolution fusion | flops 2147483648 | bytes 8388608 | tf_op jit(solution)/shard_map/dot_general | solution.py:117
  98.3 2.0 copy.138
  102.0 2.0 copy.141
  109.4 2.0 copy.147
  113.1 2.0 copy.150
  116.8 2.0 copy.153
  135.0 2.0 copy.168
  138.7 2.0 copy.171
  148.0 16.4 %add_multiply_fusion = f32[8,6,64,128]{2,3,1,0:T(8,128)} fusion(f32[8,64,128]{1,2,0:T(8,128)} %copy.177, f32[8,64,128]{1,2,0:T(8,128)} %copy.174, f32[8,64,128]{1,2,0:T(8,128)} %copy.171, f32[8,64,128]{1,2,0:T(8,128)} %copy.168, f32[8,64,128]{1,2,0:T(8,128)} %copy.165, f32[8,64,128]{1,2,0:T(8,128)} %copy.162, f32[8,64,128]{1,2,0:T(8,128)} %copy.159, ...), kind=kLoop, calls=%fused_computation.14 | loop fusion | flops 12582912 | bytes 5865472 | tf_op jit(solution)/shard_map/div | solution.py:132
  166.0 17.6 %shard_map.86 = f32[128,8192]{1,0:T(8,128)} custom-call(s32[768]{0:T(1024)} %reshape.262.cols_ref, s32[128]{0:T(128)} %cnt_ref.1, bf16[128,1024]{1,0:T(8,128)(2,1)} %copy.179.gp_ref, bf16[128,3,64,128]{3,2,1,0:T(8,128)(2,1)} %all-gather.2.cloned.1.call-done.bt_ref), custom_call_target="tpu_custom_call" | custom-call | tf_op jit(solution)/shard_map/pallas_call | solution.py:74
  183.6 2.9 %fusion.6 = f32[128]{0:T(128)S(1)} fusion(bf16[128,8192]{1,0:T(8,128)(2,1)S(1)} %copy-done.1, f32[128,8192]{1,0:T(8,128)} %shard_map.86, f32[8192]{0:T(1024)S(1)} %copy-done.2), kind=kLoop, calls=%fused_computation.12 | loop fusion | flops 4194176 | bytes 6324736 | tf_op jit(solution)/shard_map/reduce_sum | solution.py:147
  186.5 27.1 %reduce-scatter.2.cloned.1.call-done = f32[1,6,64,128]{2,3,1,0:T(8,128)} async-done(((f32[8,6,64,128]{2,3,1,0:T(8,128)}), f32[1,6,64,128]{2,3,1,0:T(8,128)}) %reduce-scatter.2.cloned.1.call-update) | async-done | bytes 196624 | tf_op jit(solution)/shard_map/reduce_scatter | solution.py:134
  215.6 6.7 %all-to-all-start.1 = ((f32[8,1,6144]{2,1,0:T(1,128)}), f32[8,1,6144]{2,1,0:T(1,128)S(1)}, u32[]{:S(2)}, u32[]{:S(2)}) async-start(f32[8,1,6144]{2,1,0:T(1,128)} %reshape.325), calls=%async_computation.2 | async-start | bytes 393216 | tf_op jit(solution)/shard_map/all_to_all | solution.py:137
  222.3 4.7 %fusion.5 = bf16[128,8192]{1,0:T(8,128)(2,1)} fusion(bf16[128,8192]{1,0:T(8,128)(2,1)S(1)} %copy-done.1, f32[128,8192]{1,0:T(8,128)} %shard_map.86, f32[128]{0:T(128)S(1)} %broadcast_multiply_fusion, f32[128]{0:T(128)S(1)} %copy-done.4, f32[8192]{0:T(1024)S(1)} %copy-done.2, f32[128]{0:T(128)S(1)} %get-tuple-element.59), kind=kLoop, calls=%fused_computation.11 | loop fusion | flops 7340032 | bytes 8422912 | tf_op jit(solution)/shard_map/convert_element_type | solution.py:148
  227.0 5.1 %all-to-all-done.1 = f32[8,1,6144]{2,1,0:T(1,128)S(1)} async-done(((f32[8,1,6144]{2,1,0:T(1,128)}), f32[8,1,6144]{2,1,0:T(1,128)S(1)}, u32[]{:S(2)}, u32[]{:S(2)}) %all-to-all-start.1) | async-done | bytes 196640 | tf_op jit(solution)/shard_map/all_to_all | solution.py:137
  (101 shorter events, 76.1 us)
Async XLA Ops:
  7.2 4.1 %copy-start.1 = (bf16[128,8192]{1,0:T(8,128)(2,1)S(1)}, bf16[128,8192]{1,0:T(8,128)(2,1)}, u32[]{:S(2)}) copy-start(bf16[128,8192]{1,0:T(8,128)(2,1)} %param.7) | copy-start | bytes 6291460
  7.2 5.1 %copy-start.2 = (f32[8192]{0:T(1024)S(1)}, f32[8192]{0:T(1024)}, u32[]{:S(2)}) copy-start(f32[8192]{0:T(1024)} %param.8) | copy-start | bytes 98308
  7.2 157.2 %all-gather.2.cloned.1.call-start = ((), (), s32[]{:S(2)}) async-start(), calls=%async_computation.3 | async-start | bytes 6389760 | tf_op jit(solution)/shard_map/all_gather | solution.py:99
  23.3 10.5 %copy-start.3 = (s32[128,6]{0,1:T(8,128)S(1)}, s32[128,6]{0,1:T(8,128)}, u32[]{:S(2)}) copy-start(s32[128,6]{0,1:T(8,128)} %param.11) | copy-start | bytes 9220
  23.3 58.2 %all-to-all-start = ((bf16[128,8,2048]{0,2,1:T(8,128)(2,1)}), bf16[128,8,2048]{0,2,1:T(8,128)(2,1)}, u32[]{:S(2)}, u32[]{:S(2)}) async-start(bf16[128,8,2048]{0,2,1:T(8,128)(2,1)} %pad_maximum_fusion), calls=%async_computation | async-start | bytes 8388608 | tf_op jit(solution)/shard_map/all_to_all | solution.py:109
  33.7 179.9 %reduce-scatter.2.cloned.1.call-start = ((), (), s32[]{:S(2)}) async-start(), calls=%async_computation.4 | async-start | bytes 3538944 | tf_op jit(solution)/shard_map/reduce_scatter | solution.py:134
  36.8 16.2 %copy-start = (s32[128]{0:T(128)S(1)}, s32[128]{0:T(128)}, u32[]{:S(2)}) copy-start(s32[128]{0:T(128)} %cnt_ref.1) | copy-start | bytes 1540
  183.6 38.7 %copy-start.4 = (f32[128]{0:T(128)S(1)}, f32[128]{0:T(128)}, u32[]{:S(2)}) copy-start(f32[128]{0:T(128)} %get-tuple-element.58) | copy-start | bytes 1540
  215.6 16.5 %all-to-all-start.1 = ((f32[8,1,6144]{2,1,0:T(1,128)}), f32[8,1,6144]{2,1,0:T(1,128)S(1)}, u32[]{:S(2)}, u32[]{:S(2)}) async-start(f32[8,1,6144]{2,1,0:T(1,128)} %reshape.325), calls=%async_computation.2 | async-start | bytes 393216 | tf_op jit(solution)/shard_map/all_to_all | solution.py:137
Sparse Core Ops, SparseCore 0:
  11.0 95.3 all-gather.1
  164.5 49.0 reduce-scatter.1

commit v4 on v3

--- a/solution.py
+++ b/solution.py
@@ -1,3 +1,4 @@
+import functools
 import math
 
 import jax
@@ -79,6 +80,39 @@
     )(cols.reshape(-1), counts, grad_pre, blocks_t)
 
 
+def _pick_kernel(cols_ref, cnt_ref, pt_ref, out_ref, *, part_rows, divisor):
+    step = pl.program_id(0)
+    width = pt_ref.shape[1]
+    per_step = width // part_rows
+    group = lax.broadcasted_iota(jnp.int32, (BLK, width), 1) // part_rows
+    for k in range(MOSTR):
+        acc = jnp.zeros((BLK, width), jnp.float32)
+        for rr in range(per_step):
+            row = step * per_step + rr
+            start = pl.multiple_of(cols_ref[row * MOSTR + k] * BLK, BLK)
+            value = pt_ref[pl.ds(start, BLK), :]
+            value = jnp.where(k < cnt_ref[row], value, jnp.zeros_like(value))
+            acc = jnp.where(group == rr, value, acc)
+        out_ref[0, k] = acc / divisor
+
+
+def pick_blocks(product_t, cols, counts, part_rows, divisor):
+    width = 128
+    chunks = product_t.shape[1] // width
+    spec = pltpu.PrefetchScalarGridSpec(
+        num_scalar_prefetch=2,
+        grid=(chunks,),
+        in_specs=[pl.BlockSpec((product_t.shape[0], width), lambda g, c, n: (0, g))],
+        out_specs=pl.BlockSpec((1, MOSTR, BLK, width), lambda g, c, n: (g, 0, 0, 0)),
+    )
+    return pl.pallas_call(
+        functools.partial(_pick_kernel, part_rows=part_rows, divisor=divisor),
+        grid_spec=spec,
+        out_shape=jax.ShapeDtypeStruct((chunks, MOSTR, BLK, width), jnp.float32),
+        compiler_params=pltpu.CompilerParams(dimension_semantics=("arbitrary",)),
+    )(cols.reshape(-1), counts, product_t)
+
+
 def shards(checkpoint, norm_gain, key_cotangent, positions, kept_cols, kept_count, key_blocks):
     tok_rows = checkpoint.shape[0]
     groups = lax.axis_size("x") * lax.axis_size("c")
@@ -118,22 +152,11 @@
         grad_all, slab, (((0,), (0,)), ((), ())), preferred_element_type=jnp.float32
     )
     lanes = row_blocks * part_rows // nz
-    blocks4 = product.reshape(col_blocks, BLK, nz, lanes)
-    lane_row = (
-        lax.broadcasted_iota(jnp.int32, (nz, lanes), 0) * lanes
-        + lax.broadcasted_iota(jnp.int32, (nz, lanes), 1)
-    ) // part_rows
-    lane_cols = kept_cols[lane_row]
-    lane_live = lax.broadcasted_iota(jnp.int32, (nz, lanes, MOSTR), 2) < kept_count[lane_row][:, :, None]
-    partial = jnp.zeros((nz, MOSTR, BLK, lanes), jnp.float32)
-    for c in range(col_blocks):
-        hit = ((lane_cols == c) & lane_live).transpose(0, 2, 1)[:, :, None, :]
-        partial = partial + jnp.where(hit, blocks4[c].transpose(1, 0, 2)[:, None, :, :], 0.0)
-    partial = partial / divisor
+    partial = pick_blocks(product, kept_cols, kept_count, part_rows, divisor)
     partial, piece = lax.optimization_barrier((partial, piece))
     summed = lax.psum_scatter(partial, "z", scatter_dimension=0, tiled=True)
     sub = lanes // ny
-    summed = summed.reshape(MOSTR, BLK, ny, sub).transpose(2, 0, 3, 1)
+    summed = summed.transpose(1, 2, 0, 3).reshape(MOSTR, BLK, ny, sub).transpose(2, 0, 3, 1)
     summed = lax.all_to_all(summed, "y", split_axis=0, concat_axis=0, tiled=True).sum(axis=0)
     own_rows = sub // part_rows
     block_grad = (

time: 244 us -> 180 us (0.74)
  local copies, waits for them, and re-layouts: 107 us -> 21.3 us
  waiting for transfers between devices: 47.4 us -> 76.9 us
  other arithmetic: 33.5 us -> 16 us
  Pallas kernels: 17.6 us -> 26.1 us
    all_to_all x1, waiting for transfers between devices: 15.1 us -> 46.8 us  [shards(): lax.all_to_all(sent, ('x', 'c'), split_axis=1, concat_axis=0, tiled=True)]
    transpose x17 -> x1, local copies, waits for them, and re-layouts: 29.9 us -> 0.03 us  [shards(): summed.transpose(1, 2, 0, 3).reshape(MOSTR, BLK, ny, sub)]
    unnamed x31 -> x10, local copies, waits for them, and re-layouts: 28.8 us -> 2.3 us
    div x1 -> x0, other arithmetic: 16.4 us -> none  [shards(): partial = partial / divisor]
    eq x16 -> x0, local copies, waits for them, and re-layouts: 14.1 us -> none  [shards(): hit = ((lane_cols == c) & lane_live).transpose(0, 2, 1)[:, :, None, :]]
    gather x2 -> x0, local copies, waits for them, and re-layouts: 9.38 us -> none  [the longest x1 6.57 us: shards(): kept_count[lane_row][:, :, None]]
    pallas_call x0 -> x1, Pallas kernels: none -> 8.48 us  [pick_blocks(): pl.pallas_call(functools.partial(_pick_kernel, part_rows=part_rows, divis...]
    and x16 -> x0, local copies, waits for them, and re-layouts: 6.63 us -> none  [shards(): hit = ((lane_cols == c) & lane_live).transpose(0, 2, 1)[:, :, None, :]]
  transfers between devices with their start and end apart: 4 -> 4, of which waited for: 3 -> 4; matrix products, arithmetic and copies ran while one was open for 57% -> 21% of each run, Pallas kernels for 7% -> 15%
where the time goes in v4:
time: 180 us; the launch traced here: 178 us
  waiting for transfers between devices  76.9 us (43%)
  Pallas kernels  26.1 us (14%)
  local copies, waits for them, and re-layouts  21.3 us (12%)
  starting transfers between devices  17.1 us (10%)
  other arithmetic  16 us (9%)
  between operations  14.2 us (8%)
  matrix products  6.71 us (4%)
    all_to_all x1, waiting for transfers between devices, shards(): lax.all_to_all(sent, ('x', 'c'), split_axis=1, concat_axis=0, tiled=True)  46.8 us
    reduce_scatter x1, waiting for transfers between devices, shards(): summed = lax.psum_scatter(partial, 'z', scatter_dimension=0, tiled=True)  22.6 us
    pallas_call x1, Pallas kernels, normed_grad_of(): pl.pallas_call(_normed_grad_kernel, grid_spec=spec, out_shape=jax.ShapeDt...  17.6 us
    all_to_all x1, starting transfers between devices, shards(): lax.all_to_all(sent, ('x', 'c'), split_axis=1, concat_axis=0, tiled=True)  10.5 us
    pallas_call x1, Pallas kernels, pick_blocks(): pl.pallas_call(functools.partial(_pick_kernel, part_rows=part_rows, divis...  8.48 us
    dot_general x1, matrix products, shards(): lax.dot_general(grad_all, slab, (((0,), (0,)), ((), ())), preferred_eleme...  6.71 us
    all_to_all x1, starting transfers between devices, shards(): lax.all_to_all(summed, 'y', split_axis=0, concat_axis=0, tiled=True)  6.64 us
    all_to_all x1, local copies, waits for them, and re-layouts, shards(): lax.all_to_all(sent, ('x', 'c'), split_axis=1, concat_axis=0, tiled=True)  6.58 us
  transfers between devices with their start and end apart: 4, of which 4 were waited for; matrix products, arithmetic and copies ran while one was open for 21% of the time, Pallas kernels for 15%

profile of v4, /device:TPU:6, one launch (start us, length us, event | category | flops | bytes accessed | tf_op | source)
XLA Modules:
  0.0 178.2 jit_solution(14204293491458334684)
XLA Ops:
  7.2 1.2 reshape.119
  8.6 0.8 reshape.120
  10.1 1.1 copy.19
  11.2 2.1 %fusion = f32[128]{0:T(128)S(1)} fusion(bf16[128,8192]{1,0:T(8,128)(2,1)} %param.7), kind=kLoop, calls=%fused_computation.4 | loop fusion | flops 3145600 | bytes 2097664 | tf_op jit(solution)/shard_map/reduce_sum | solution.py:124
  13.3 1.9 %fusion.2 = bf16[128,8192]{1,0:T(8,128)(2,1)} fusion(bf16[128,8192]{1,0:T(8,128)(2,1)S(1)} %copy-done, f32[8192]{0:T(1024)S(1)} %copy-done.1, f32[128]{0:T(128)S(1)} %get-tuple-element.11), kind=kLoop, calls=%fused_computation.6 | loop fusion | flops 4194304 | bytes 4227584 | tf_op jit(solution)/shard_map/convert_element_type | solution.py:125
  15.2 4.1 %copy.20 = bf16[128,8192]{0,1:T(8,128)(2,1)} copy(bf16[128,8192]{1,0:T(8,128)(2,1)} %fusion.2) | data formatting | bytes 4194304 | tf_op jit(solution)/shard_map/convert_element_type | solution.py:125
  19.3 2.0 %copy.28 = bf16[128,8,128,8]{0,3,2,1:T(8,128)(2,1)S(1)} copy(bf16[128,8,128,8]{0,3,1,2:T(8,128)(2,1)} %bitcast.26) | data formatting | bytes 4194304 | tf_op jit(solution)/shard_map/transpose | solution.py:137
  21.9 2.3 %pad_maximum_fusion = bf16[128,8,2048]{0,2,1:T(8,128)(2,1)} fusion(bf16[128,8,1024]{0,2,1:T(8,128)(2,1)S(1)} %broadcast_in_dim.2, bf16[128,8,1024]{0,2,1:T(8,128)(2,1)S(1)} %bitcast.27), kind=kLoop, calls=%fused_computation.11 | loop fusion | flops 8388608 | bytes 8388608 | tf_op jit(solution)/shard_map/concatenate | solution.py:140
  24.3 10.5 %all-to-all-start = ((bf16[128,8,2048]{0,2,1:T(8,128)(2,1)}), bf16[128,8,2048]{0,2,1:T(8,128)(2,1)}, u32[]{:S(2)}, u32[]{:S(2)}) async-start(bf16[128,8,2048]{0,2,1:T(8,128)(2,1)} %pad_maximum_fusion), calls=%async_computation | async-start | bytes 8388608 | tf_op jit(solution)/shard_map/all_to_all | solution.py:143
  35.6 46.8 %all-to-all-done = bf16[128,8,2048]{0,2,1:T(8,128)(2,1)} async-done(((bf16[128,8,2048]{0,2,1:T(8,128)(2,1)}), bf16[128,8,2048]{0,2,1:T(8,128)(2,1)}, u32[]{:S(2)}, u32[]{:S(2)}) %all-to-all-start) | async-done | bytes 4194336 | tf_op jit(solution)/shard_map/all_to_all | solution.py:143
  82.4 6.6 %copy.22 = bf16[8,128,1,2048]{3,1,0,2:T(8,128)(2,1)} copy(bf16[8,128,1,2048]{1,3,0,2:T(8,128)(2,1)} %bitcast.7) | data formatting | bytes 8388608 | tf_op jit(solution)/shard_map/all_to_all | solution.py:143
  89.0 6.7 %fusion.7.pt_ref = f32[1024,1024]{1,0:T(8,128)} fusion(bf16[1024,2048]{1,0:T(8,128)(2,1)} %bitcast.28), kind=kOutput, calls=%fused_computation.12 | convolution fusion | flops 2147483648 | bytes 8388608 | tf_op jit(solution)/shard_map/dot_general | solution.py:151
  95.7 8.5 %shard_map.86 = f32[8,6,64,128]{3,2,1,0:T(8,128)} custom-call(s32[768]{0:T(1024)} %reshape.113.cols_ref, s32[128]{0:T(128)} %cnt_ref.3, f32[1024,1024]{1,0:T(8,128)} %fusion.7.pt_ref), custom_call_target="tpu_custom_call" | custom-call | tf_op jit(solution)/shard_map/pallas_call | solution.py:108
  104.2 2.3 %all-gather.2.cloned.1.call-done.bt_ref = bf16[128,3,64,128]{3,2,1,0:T(8,128)(2,1)} async-done(((bf16[2,3,64,128]{3,2,1,0:T(8,128)(2,1)}), bf16[128,3,64,128]{3,2,1,0:T(8,128)(2,1)}) %all-gather.2.cloned.1.call-update) | async-done | bytes 6291472 | tf_op jit(solution)/shard_map/all_gather | solution.py:133
  106.5 0.9 copy.24.gp_ref
  107.4 17.6 %shard_map.87 = f32[128,8192]{1,0:T(8,128)} custom-call(s32[768]{0:T(1024)} %reshape.113.cols_ref, s32[128]{0:T(128)} %cnt_ref.3, bf16[128,1024]{1,0:T(8,128)(2,1)} %copy.24.gp_ref, bf16[128,3,64,128]{3,2,1,0:T(8,128)(2,1)} %all-gather.2.cloned.1.call-done.bt_ref), custom_call_target="tpu_custom_call" | custom-call | tf_op jit(solution)/shard_map/pallas_call | solution.py:75
  124.9 2.8 %fusion.6 = f32[128]{0:T(128)S(1)} fusion(bf16[128,8192]{1,0:T(8,128)(2,1)S(1)} %copy-done, f32[128,8192]{1,0:T(8,128)} %shard_map.87, f32[8192]{0:T(1024)S(1)} %copy-done.1), kind=kLoop, calls=%fused_computation.10 | loop fusion | flops 4194176 | bytes 6324736 | tf_op jit(solution)/shard_map/reduce_sum | solution.py:170
  127.8 22.6 %reduce-scatter.2.cloned.1.call-done = f32[1,6,64,128]{3,2,1,0:T(8,128)} async-done(((f32[8,6,64,128]{3,2,1,0:T(8,128)}), f32[1,6,64,128]{3,2,1,0:T(8,128)}) %reduce-scatter.2.cloned.1.call-update) | async-done | bytes 196624 | tf_op jit(solution)/shard_map/reduce_scatter | solution.py:157
  150.4 1.1 copy.25
  151.5 0.9 reshape.125
  152.4 6.6 %all-to-all-start.1 = ((f32[8,1,6144]{2,1,0:T(1,128)}), f32[8,1,6144]{2,1,0:T(1,128)S(1)}, u32[]{:S(2)}, u32[]{:S(2)}) async-start(f32[8,1,6144]{2,1,0:T(1,128)} %reshape.125), calls=%async_computation.2 | async-start | bytes 393216 | tf_op jit(solution)/shard_map/all_to_all | solution.py:160
  159.1 4.7 %fusion.5 = bf16[128,8192]{1,0:T(8,128)(2,1)} fusion(bf16[128,8192]{1,0:T(8,128)(2,1)S(1)} %copy-done, f32[128,8192]{1,0:T(8,128)} %shard_map.87, f32[128]{0:T(128)S(1)} %broadcast_multiply_fusion, f32[128]{0:T(128)S(1)} %get-tuple-element.10, f32[8192]{0:T(1024)S(1)} %copy-done.1, f32[128]{0:T(128)S(1)} %get-tuple-element.11), kind=kLoop, calls=%fused_computation.9 | loop fusion | flops 7340032 | bytes 8422912 | tf_op jit(solution)/shard_map/convert_element_type | solution.py:171
  163.8 5.1 %all-to-all-done.1 = f32[8,1,6144]{2,1,0:T(1,128)S(1)} async-done(((f32[8,1,6144]{2,1,0:T(1,128)}), f32[8,1,6144]{2,1,0:T(1,128)S(1)}, u32[]{:S(2)}, u32[]{:S(2)}) %all-to-all-start.1) | async-done | bytes 196640 | tf_op jit(solution)/shard_map/all_to_all | solution.py:160
  169.3 1.1 reduce
  (27 shorter events, 3.8 us)
Async XLA Ops:
  7.2 6.2 %copy-start = (bf16[128,8192]{1,0:T(8,128)(2,1)S(1)}, bf16[128,8192]{1,0:T(8,128)(2,1)}, u32[]{:S(2)}) copy-start(bf16[128,8192]{1,0:T(8,128)(2,1)} %param.7) | copy-start | bytes 6291460
  7.2 6.2 %copy-start.1 = (f32[8192]{0:T(1024)S(1)}, f32[8192]{0:T(1024)}, u32[]{:S(2)}) copy-start(f32[8192]{0:T(1024)} %param.8) | copy-start | bytes 98308
  7.2 99.3 %all-gather.2.cloned.1.call-start = ((), (), s32[]{:S(2)}) async-start(), calls=%async_computation.3 | async-start | bytes 6389760 | tf_op jit(solution)/shard_map/all_gather | solution.py:133
  24.3 10.5 %copy-start.2 = (s32[128,6]{0,1:T(8,128)S(1)}, s32[128,6]{0,1:T(8,128)}, u32[]{:S(2)}) copy-start(s32[128,6]{0,1:T(8,128)} %param.11) | copy-start | bytes 9220
  24.3 58.1 %all-to-all-start = ((bf16[128,8,2048]{0,2,1:T(8,128)(2,1)}), bf16[128,8,2048]{0,2,1:T(8,128)(2,1)}, u32[]{:S(2)}, u32[]{:S(2)}) async-start(bf16[128,8,2048]{0,2,1:T(8,128)(2,1)} %pad_maximum_fusion), calls=%async_computation | async-start | bytes 8388608 | tf_op jit(solution)/shard_map/all_to_all | solution.py:143
  34.7 115.7 %reduce-scatter.2.cloned.1.call-start = ((), (), s32[]{:S(2)}) async-start(), calls=%async_computation.4 | async-start | bytes 1769472 | tf_op jit(solution)/shard_map/reduce_scatter | solution.py:157
  152.4 16.4 %all-to-all-start.1 = ((f32[8,1,6144]{2,1,0:T(1,128)}), f32[8,1,6144]{2,1,0:T(1,128)S(1)}, u32[]{:S(2)}, u32[]{:S(2)}) async-start(f32[8,1,6144]{2,1,0:T(1,128)} %reshape.125), calls=%async_computation.2 | async-start | bytes 393216 | tf_op jit(solution)/shard_map/all_to_all | solution.py:160
Sparse Core Ops, SparseCore 0:
  11.0 95.3 all-gather.1
  109.9 40.4 reduce-scatter.1

commit v5 on v4

--- a/solution.py
+++ b/solution.py
@@ -84,6 +84,8 @@
     step = pl.program_id(0)
     width = pt_ref.shape[1]
     per_step = width // part_rows
+    dests = out_ref.shape[0]
+    sub = width // dests
     group = lax.broadcasted_iota(jnp.int32, (BLK, width), 1) // part_rows
     for k in range(MOSTR):
         acc = jnp.zeros((BLK, width), jnp.float32)
@@ -93,22 +95,27 @@
             value = pt_ref[pl.ds(start, BLK), :]
             value = jnp.where(k < cnt_ref[row], value, jnp.zeros_like(value))
             acc = jnp.where(group == rr, value, acc)
-        out_ref[0, k] = acc / divisor
-
-
-def pick_blocks(product_t, cols, counts, part_rows, divisor):
-    width = 128
+        acc_t = (acc / divisor).T
+        half = (k % 2) * BLK
+        for d in range(dests):
+            out_ref[d, k // 2, :, half:half + BLK] = acc_t[d * sub:(d + 1) * sub, :]
+
+
+def pick_blocks(product_t, cols, counts, part_rows, divisor, devices):
+    per_dev = product_t.shape[1] // devices
+    width = max(128, per_dev)
+    dests = width // per_dev
     chunks = product_t.shape[1] // width
     spec = pltpu.PrefetchScalarGridSpec(
         num_scalar_prefetch=2,
         grid=(chunks,),
         in_specs=[pl.BlockSpec((product_t.shape[0], width), lambda g, c, n: (0, g))],
-        out_specs=pl.BlockSpec((1, MOSTR, BLK, width), lambda g, c, n: (g, 0, 0, 0)),
+        out_specs=pl.BlockSpec((dests, MOSTR // 2, per_dev, 2 * BLK), lambda g, c, n: (g, 0, 0, 0)),
     )
     return pl.pallas_call(
         functools.partial(_pick_kernel, part_rows=part_rows, divisor=divisor),
         grid_spec=spec,
-        out_shape=jax.ShapeDtypeStruct((chunks, MOSTR, BLK, width), jnp.float32),
+        out_shape=jax.ShapeDtypeStruct((devices, MOSTR // 2, per_dev, 2 * BLK), jnp.float32),
         compiler_params=pltpu.CompilerParams(dimension_semantics=("arbitrary",)),
     )(cols.reshape(-1), counts, product_t)
 
@@ -145,23 +152,17 @@
     grad_all = received[:, row_blocks * part_rows:]
     normed_rows = received[:, : row_blocks * part_rows].reshape(groups * tok_rows, row_blocks, part_rows)
     divisor = math.sqrt(tok_rows * groups * dp_size)
-    nz = lax.axis_size("z")
-    ny = lax.axis_size("y")
     slab = normed_rows.reshape(groups * tok_rows, row_blocks * part_rows)
     product = lax.dot_general(
         grad_all, slab, (((0,), (0,)), ((), ())), preferred_element_type=jnp.float32
     )
-    lanes = row_blocks * part_rows // nz
-    partial = pick_blocks(product, kept_cols, kept_count, part_rows, divisor)
+    partial = pick_blocks(product, kept_cols, kept_count, part_rows, divisor, dp_size)
     partial, piece = lax.optimization_barrier((partial, piece))
-    summed = lax.psum_scatter(partial, "z", scatter_dimension=0, tiled=True)
-    sub = lanes // ny
-    summed = summed.transpose(1, 2, 0, 3).reshape(MOSTR, BLK, ny, sub).transpose(2, 0, 3, 1)
-    summed = lax.all_to_all(summed, "y", split_axis=0, concat_axis=0, tiled=True).sum(axis=0)
-    own_rows = sub // part_rows
+    summed = lax.all_to_all(partial, ("z", "y"), split_axis=0, concat_axis=0, tiled=True).sum(axis=0)
+    own_rows = summed.shape[1] // part_rows
     block_grad = (
-        summed.reshape(MOSTR, own_rows, part_rows, BLK)
-        .transpose(1, 0, 2, 3)
+        summed.reshape(MOSTR // 2, own_rows, part_rows, 2, BLK)
+        .transpose(1, 0, 3, 2, 4)
         .reshape(own_rows, MOSTR, part_rows * BLK)
     )
 

time: 180 us -> 170 us (0.944)
  waiting for transfers between devices: 76.9 us -> 64.6 us
  starting transfers between devices: 17.1 us -> 20.9 us
  local copies, waits for them, and re-layouts: 21.3 us -> 19.2 us
    reduce_scatter x1 -> x0, waiting for transfers between devices: 22.6 us -> none  [shards(): summed = lax.psum_scatter(partial, 'z', scatter_dimension=0, tiled=True)]
    all_to_all x1, waiting for transfers between devices: 5.09 us -> 16.7 us  [shards(): lax.all_to_all(partial, ('z', 'y'), split_axis=0, concat_axis=0, tiled=True)]
    all_to_all x1, starting transfers between devices: 6.64 us -> 10.4 us  [shards(): lax.all_to_all(partial, ('z', 'y'), split_axis=0, concat_axis=0, tiled=True)]
    convert_element_type x1, other arithmetic: 4.7 us -> 2.6 us  [shards(): return (grads.astype(jnp.bfloat16), block_grad)]
  transfers between devices with their start and end apart: 4 -> 3, of which waited for: 4 -> 3; matrix products, arithmetic and copies ran while one was open for 21% -> 21% of each run, Pallas kernels for 15% -> 16%
where the time goes in v5:
time: 170 us; the launch traced here: 167 us
  waiting for transfers between devices  64.6 us (38%)
  Pallas kernels  27.3 us (16%)
  starting transfers between devices  20.9 us (12%)
  local copies, waits for them, and re-layouts  19.2 us (11%)
  other arithmetic  14.4 us (8%)
  between operations  14.2 us (8%)
  matrix products  6.7 us (4%)
    all_to_all x1, waiting for transfers between devices, shards(): lax.all_to_all(sent, ('x', 'c'), split_axis=1, concat_axis=0, tiled=True)  46.8 us
    pallas_call x1, Pallas kernels, normed_grad_of(): pl.pallas_call(_normed_grad_kernel, grid_spec=spec, out_shape=jax.ShapeDt...  17.5 us
    all_to_all x1, waiting for transfers between devices, shards(): lax.all_to_all(partial, ('z', 'y'), split_axis=0, concat_axis=0, tiled=True)  16.7 us
    all_to_all x1, starting transfers between devices, shards(): lax.all_to_all(sent, ('x', 'c'), split_axis=1, concat_axis=0, tiled=True)  10.5 us
    all_to_all x1, starting transfers between devices, shards(): lax.all_to_all(partial, ('z', 'y'), split_axis=0, concat_axis=0, tiled=True)  10.4 us
    pallas_call x1, Pallas kernels, pick_blocks(): pl.pallas_call(functools.partial(_pick_kernel, part_rows=part_rows, divis...  9.73 us
    dot_general x1, matrix products, shards(): lax.dot_general(grad_all, slab, (((0,), (0,)), ((), ())), preferred_eleme...  6.7 us
    all_to_all x1, local copies, waits for them, and re-layouts, shards(): lax.all_to_all(sent, ('x', 'c'), split_axis=1, concat_axis=0, tiled=True)  6.57 us
  transfers between devices with their start and end apart: 3, of which 3 were waited for; matrix products, arithmetic and copies ran while one was open for 21% of the time, Pallas kernels for 16%

profile of v5, /device:TPU:6, one launch (start us, length us, event | category | flops | bytes accessed | tf_op | source)
XLA Modules:
  0.0 167.2 jit_solution(11865944919253190942)
XLA Ops:
  7.2 1.2 reshape.119
  8.6 0.8 reshape.120
  9.4 0.7 convert_element_type.24
  10.1 1.1 copy.26
  11.3 2.1 %fusion = f32[128]{0:T(128)S(1)} fusion(bf16[128,8192]{1,0:T(8,128)(2,1)} %param.7), kind=kLoop, calls=%fused_computation.4 | loop fusion | flops 3145600 | bytes 2097664 | tf_op jit(solution)/shard_map/reduce_sum | solution.py:131
  13.4 1.9 %fusion.2 = bf16[128,8192]{1,0:T(8,128)(2,1)} fusion(bf16[128,8192]{1,0:T(8,128)(2,1)S(1)} %copy-done.1, f32[8192]{0:T(1024)S(1)} %copy-done.2, f32[128]{0:T(128)S(1)} %get-tuple-element.11), kind=kLoop, calls=%fused_computation.6 | loop fusion | flops 4194304 | bytes 4227584 | tf_op jit(solution)/shard_map/convert_element_type | solution.py:132
  15.3 4.1 %copy.27 = bf16[128,8192]{0,1:T(8,128)(2,1)} copy(bf16[128,8192]{1,0:T(8,128)(2,1)} %fusion.2) | data formatting | bytes 4194304 | tf_op jit(solution)/shard_map/convert_element_type | solution.py:132
  19.4 2.0 %copy.34 = bf16[128,8,128,8]{0,3,2,1:T(8,128)(2,1)S(1)} copy(bf16[128,8,128,8]{0,3,1,2:T(8,128)(2,1)} %bitcast.21) | data formatting | bytes 4194304 | tf_op jit(solution)/shard_map/transpose | solution.py:144
  22.0 2.3 %pad_maximum_fusion = bf16[128,8,2048]{0,2,1:T(8,128)(2,1)} fusion(bf16[128,8,1024]{0,2,1:T(8,128)(2,1)S(1)} %broadcast_in_dim.2, bf16[128,8,1024]{0,2,1:T(8,128)(2,1)S(1)} %bitcast.22), kind=kLoop, calls=%fused_computation.11 | loop fusion | flops 8388608 | bytes 8388608 | tf_op jit(solution)/shard_map/concatenate | solution.py:147
  24.3 10.5 %all-to-all-start = ((bf16[128,8,2048]{0,2,1:T(8,128)(2,1)}), bf16[128,8,2048]{0,2,1:T(8,128)(2,1)}, u32[]{:S(2)}, u32[]{:S(2)}) async-start(bf16[128,8,2048]{0,2,1:T(8,128)(2,1)} %pad_maximum_fusion), calls=%async_computation | async-start | bytes 8388608 | tf_op jit(solution)/shard_map/all_to_all | solution.py:150
  34.9 0.7 reshape.113.cols_ref
  35.6 46.8 %all-to-all-done = bf16[128,8,2048]{0,2,1:T(8,128)(2,1)} async-done(((bf16[128,8,2048]{0,2,1:T(8,128)(2,1)}), bf16[128,8,2048]{0,2,1:T(8,128)(2,1)}, u32[]{:S(2)}, u32[]{:S(2)}) %all-to-all-start) | async-done | bytes 4194336 | tf_op jit(solution)/shard_map/all_to_all | solution.py:150
  82.5 6.6 %copy.29 = bf16[8,128,1,2048]{3,1,0,2:T(8,128)(2,1)} copy(bf16[8,128,1,2048]{1,3,0,2:T(8,128)(2,1)} %bitcast.7) | data formatting | bytes 8388608 | tf_op jit(solution)/shard_map/all_to_all | solution.py:150
  89.0 6.7 %fusion.7.pt_ref = f32[1024,1024]{1,0:T(8,128)} fusion(bf16[1024,2048]{1,0:T(8,128)(2,1)} %bitcast.23), kind=kOutput, calls=%fused_computation.12 | convolution fusion | flops 2147483648 | bytes 8388608 | tf_op jit(solution)/shard_map/dot_general | solution.py:156
  95.7 9.7 %shard_map.86 = f32[64,3,16,128]{3,2,1,0:T(8,128)} custom-call(s32[768]{0:T(1024)} %reshape.113.cols_ref, s32[128]{0:T(128)} %cnt_ref.3, f32[1024,1024]{1,0:T(8,128)} %fusion.7.pt_ref), custom_call_target="tpu_custom_call" | custom-call | tf_op jit(solution)/shard_map/pallas_call | solution.py:115
  105.5 1.0 all-gather.2.cloned.1.call-done.bt_ref
  106.5 10.4 %all-to-all-start.1 = ((f32[64,3,16,128]{3,2,1,0:T(8,128)}), f32[64,3,16,128]{3,2,1,0:T(8,128)}, u32[]{:S(2)}, u32[]{:S(2)}) async-start(f32[64,3,16,128]{3,2,1,0:T(8,128)} %shard_map.86), calls=%async_computation.1 | async-start | bytes 3145728 | tf_op jit(solution)/shard_map/all_to_all | solution.py:161
  116.9 0.9 copy.31.gp_ref
  117.8 17.5 %shard_map.87 = f32[128,8192]{1,0:T(8,128)} custom-call(s32[768]{0:T(1024)} %reshape.113.cols_ref, s32[128]{0:T(128)} %cnt_ref.3, bf16[128,1024]{1,0:T(8,128)(2,1)} %copy.31.gp_ref, bf16[128,3,64,128]{3,2,1,0:T(8,128)(2,1)} %all-gather.2.cloned.1.call-done.bt_ref), custom_call_target="tpu_custom_call" | custom-call | tf_op jit(solution)/shard_map/pallas_call | solution.py:75
  135.3 3.0 %fusion.6 = f32[128]{0:T(128)S(1)} fusion(bf16[128,8192]{1,0:T(8,128)(2,1)S(1)} %copy-done.1, f32[128,8192]{1,0:T(8,128)} %shard_map.87, f32[8192]{0:T(1024)S(1)} %copy-done.2), kind=kLoop, calls=%fused_computation.10 | loop fusion | flops 4194176 | bytes 6324736 | tf_op jit(solution)/shard_map/reduce_sum | solution.py:171
  138.8 2.6 %fusion.5 = bf16[128,8192]{1,0:T(8,128)(2,1)} fusion(bf16[128,8192]{1,0:T(8,128)(2,1)S(1)} %copy-done.1, f32[128,8192]{1,0:T(8,128)S(1)} %copy-done, f32[128]{0:T(128)S(1)} %broadcast_multiply_fusion, f32[128]{0:T(128)S(1)} %get-tuple-element.10, f32[8192]{0:T(1024)S(1)} %copy-done.2, f32[128]{0:T(128)S(1)} %get-tuple-element.11), kind=kLoop, calls=%fused_computation.9 | loop fusion | flops 7340032 | bytes 8422912 | tf_op jit(solution)/shard_map/convert_element_type | solution.py:172
  141.4 16.7 %all-to-all-done.1 = f32[64,3,16,128]{3,2,1,0:T(8,128)} async-done(((f32[64,3,16,128]{3,2,1,0:T(8,128)}), f32[64,3,16,128]{3,2,1,0:T(8,128)}, u32[]{:S(2)}, u32[]{:S(2)}) %all-to-all-start.1) | async-done | bytes 1572896 | tf_op jit(solution)/shard_map/all_to_all | solution.py:161
  158.1 1.5 reduce_sum.29
  159.7 0.7 reshape.122
  (22 shorter events, 1.5 us)
Async XLA Ops:
  7.2 6.2 %copy-start.1 = (bf16[128,8192]{1,0:T(8,128)(2,1)S(1)}, bf16[128,8192]{1,0:T(8,128)(2,1)}, u32[]{:S(2)}) copy-start(bf16[128,8192]{1,0:T(8,128)(2,1)} %param.7) | copy-start | bytes 6291460
  7.2 6.2 %copy-start.2 = (f32[8192]{0:T(1024)S(1)}, f32[8192]{0:T(1024)}, u32[]{:S(2)}) copy-start(f32[8192]{0:T(1024)} %param.8) | copy-start | bytes 98308
  7.2 99.3 %all-gather.2.cloned.1.call-start = ((), (), s32[]{:S(2)}) async-start(), calls=%async_computation.2 | async-start | bytes 6389760 | tf_op jit(solution)/shard_map/all_gather | solution.py:140
  24.3 10.5 %copy-start.3 = (s32[128,6]{0,1:T(8,128)S(1)}, s32[128,6]{0,1:T(8,128)}, u32[]{:S(2)}) copy-start(s32[128,6]{0,1:T(8,128)} %param.11) | copy-start | bytes 9220
  24.3 58.1 %all-to-all-start = ((bf16[128,8,2048]{0,2,1:T(8,128)(2,1)}), bf16[128,8,2048]{0,2,1:T(8,128)(2,1)}, u32[]{:S(2)}, u32[]{:S(2)}) async-start(bf16[128,8,2048]{0,2,1:T(8,128)(2,1)} %pad_maximum_fusion), calls=%async_computation | async-start | bytes 8388608 | tf_op jit(solution)/shard_map/all_to_all | solution.py:150
  106.5 51.6 %all-to-all-start.1 = ((f32[64,3,16,128]{3,2,1,0:T(8,128)}), f32[64,3,16,128]{3,2,1,0:T(8,128)}, u32[]{:S(2)}, u32[]{:S(2)}) async-start(f32[64,3,16,128]{3,2,1,0:T(8,128)} %shard_map.86), calls=%async_computation.1 | async-start | bytes 3145728 | tf_op jit(solution)/shard_map/all_to_all | solution.py:161
  135.3 3.4 %copy-start = (f32[128,8192]{1,0:T(8,128)S(1)}, f32[128,8192]{1,0:T(8,128)}, u32[]{:S(2)}) copy-start(f32[128,8192]{1,0:T(8,128)} %shard_map.87) | copy-start | bytes 12582916
Sparse Core Ops, SparseCore 0:
  11.0 95.3 all-gather.1

commit v6 on v5

--- a/solution.py
+++ b/solution.py
@@ -98,7 +98,7 @@
         acc_t = (acc / divisor).T
         half = (k % 2) * BLK
         for d in range(dests):
-            out_ref[d, k // 2, :, half:half + BLK] = acc_t[d * sub:(d + 1) * sub, :]
+            out_ref[d, k // 2, :, half:half + BLK] = acc_t[d * sub:(d + 1) * sub, :].astype(out_ref.dtype)
 
 
 def pick_blocks(product_t, cols, counts, part_rows, divisor, devices):
@@ -115,7 +115,7 @@
     return pl.pallas_call(
         functools.partial(_pick_kernel, part_rows=part_rows, divisor=divisor),
         grid_spec=spec,
-        out_shape=jax.ShapeDtypeStruct((devices, MOSTR // 2, per_dev, 2 * BLK), jnp.float32),
+        out_shape=jax.ShapeDtypeStruct((devices, MOSTR // 2, per_dev, 2 * BLK), jnp.bfloat16),
         compiler_params=pltpu.CompilerParams(dimension_semantics=("arbitrary",)),
     )(cols.reshape(-1), counts, product_t)
 
@@ -158,7 +158,8 @@
     )
     partial = pick_blocks(product, kept_cols, kept_count, part_rows, divisor, dp_size)
     partial, piece = lax.optimization_barrier((partial, piece))
-    summed = lax.all_to_all(partial, ("z", "y"), split_axis=0, concat_axis=0, tiled=True).sum(axis=0)
+    summed = lax.all_to_all(partial, ("z", "y"), split_axis=0, concat_axis=0, tiled=True)
+    summed = summed.astype(jnp.float32).sum(axis=0)
     own_rows = summed.shape[1] // part_rows
     block_grad = (
         summed.reshape(MOSTR // 2, own_rows, part_rows, 2, BLK)

time: 170 us -> 171 us (level)
    all_to_all x1, waiting for transfers between devices: 16.7 us -> 19.2 us  [shards(): lax.all_to_all(partial, ('z', 'y'), split_axis=0, concat_axis=0, tiled=True)]
    convert_element_type x1, other arithmetic: 2.6 us -> 4.7 us  [shards(): return (grads.astype(jnp.bfloat16), block_grad)]
  transfers between devices with their start and end apart: 3 -> 3, of which waited for: 3 -> 3; matrix products, arithmetic and copies ran while one was open for 21% -> 20% of each run, Pallas kernels for 16% -> 6%
where the time goes in v6:
time: 171 us; the launch traced here: 169 us
  waiting for transfers between devices  66.3 us (39%)
  Pallas kernels  27.2 us (16%)
  starting transfers between devices  20.7 us (12%)
  local copies, waits for them, and re-layouts  18.7 us (11%)
  other arithmetic  15 us (9%)
  between operations  14.2 us (8%)
  matrix products  6.69 us (4%)
    all_to_all x1, waiting for transfers between devices, shards(): lax.all_to_all(sent, ('x', 'c'), split_axis=1, concat_axis=0, tiled=True)  46 us
    all_to_all x1, waiting for transfers between devices, shards(): lax.all_to_all(partial, ('z', 'y'), split_axis=0, concat_axis=0, tiled=True)  19.2 us
    pallas_call x1, Pallas kernels, normed_grad_of(): pl.pallas_call(_normed_grad_kernel, grid_spec=spec, out_shape=jax.ShapeDt...  17.5 us
    all_to_all x1, starting transfers between devices, shards(): lax.all_to_all(sent, ('x', 'c'), split_axis=1, concat_axis=0, tiled=True)  10.5 us
    all_to_all x1, starting transfers between devices, shards(): lax.all_to_all(partial, ('z', 'y'), split_axis=0, concat_axis=0, tiled=True)  10.1 us
    pallas_call x1, Pallas kernels, pick_blocks(): pl.pallas_call(functools.partial(_pick_kernel, part_rows=part_rows, divis...  9.68 us
    dot_general x1, matrix products, shards(): lax.dot_general(grad_all, slab, (((0,), (0,)), ((), ())), preferred_eleme...  6.69 us
    all_to_all x1, local copies, waits for them, and re-layouts, shards(): lax.all_to_all(sent, ('x', 'c'), split_axis=1, concat_axis=0, tiled=True)  6.55 us
  transfers between devices with their start and end apart: 3, of which 3 were waited for; matrix products, arithmetic and copies ran while one was open for 20% of the time, Pallas kernels for 6%

profile of v6, /device:TPU:6, one launch (start us, length us, event | category | flops | bytes accessed | tf_op | source)
XLA Modules:
  0.0 168.7 jit_solution(4333330515063503310)
XLA Ops:
  7.2 1.2 reshape.119
  8.6 0.8 reshape.120
  9.4 0.7 convert_element_type.27
  10.1 1.1 copy.26
  11.3 2.1 %fusion = f32[128]{0:T(128)S(1)} fusion(bf16[128,8192]{1,0:T(8,128)(2,1)} %param.7), kind=kLoop, calls=%fused_computation.4 | loop fusion | flops 3145600 | bytes 2097664 | tf_op jit(solution)/shard_map/reduce_sum | solution.py:131
  13.4 1.9 %fusion.2 = bf16[128,8192]{1,0:T(8,128)(2,1)} fusion(bf16[128,8192]{1,0:T(8,128)(2,1)S(1)} %copy-done, f32[8192]{0:T(1024)S(1)} %copy-done.1, f32[128]{0:T(128)S(1)} %get-tuple-element.11), kind=kLoop, calls=%fused_computation.6 | loop fusion | flops 4194304 | bytes 4227584 | tf_op jit(solution)/shard_map/convert_element_type | solution.py:132
  15.3 4.1 %copy.27 = bf16[128,8192]{0,1:T(8,128)(2,1)} copy(bf16[128,8192]{1,0:T(8,128)(2,1)} %fusion.2) | data formatting | bytes 4194304 | tf_op jit(solution)/shard_map/convert_element_type | solution.py:132
  19.4 2.0 %copy.34 = bf16[128,8,128,8]{0,3,2,1:T(8,128)(2,1)S(1)} copy(bf16[128,8,128,8]{0,3,1,2:T(8,128)(2,1)} %bitcast.21) | data formatting | bytes 4194304 | tf_op jit(solution)/shard_map/transpose | solution.py:144
  21.7 0.3 broadcast_in_dim.2
  22.0 2.3 %pad_maximum_fusion = bf16[128,8,2048]{0,2,1:T(8,128)(2,1)} fusion(bf16[128,8,1024]{0,2,1:T(8,128)(2,1)S(1)} %broadcast_in_dim.2, bf16[128,8,1024]{0,2,1:T(8,128)(2,1)S(1)} %bitcast.22), kind=kLoop, calls=%fused_computation.11 | loop fusion | flops 8388608 | bytes 8388608 | tf_op jit(solution)/shard_map/concatenate | solution.py:147
  24.3 10.5 %all-to-all-start = ((bf16[128,8,2048]{0,2,1:T(8,128)(2,1)}), bf16[128,8,2048]{0,2,1:T(8,128)(2,1)}, u32[]{:S(2)}, u32[]{:S(2)}) async-start(bf16[128,8,2048]{0,2,1:T(8,128)(2,1)} %pad_maximum_fusion), calls=%async_computation | async-start | bytes 8388608 | tf_op jit(solution)/shard_map/all_to_all | solution.py:150
  34.8 0.8 copy.31.gp_ref
  35.7 0.7 reshape.113.cols_ref
  36.5 46.0 %all-to-all-done = bf16[128,8,2048]{0,2,1:T(8,128)(2,1)} async-done(((bf16[128,8,2048]{0,2,1:T(8,128)(2,1)}), bf16[128,8,2048]{0,2,1:T(8,128)(2,1)}, u32[]{:S(2)}, u32[]{:S(2)}) %all-to-all-start) | async-done | bytes 4194336 | tf_op jit(solution)/shard_map/all_to_all | solution.py:150
  82.5 6.5 %copy.29 = bf16[8,128,1,2048]{3,1,0,2:T(8,128)(2,1)} copy(bf16[8,128,1,2048]{1,3,0,2:T(8,128)(2,1)} %bitcast.7) | data formatting | bytes 8388608 | tf_op jit(solution)/shard_map/all_to_all | solution.py:150
  89.0 6.7 %fusion.7.pt_ref = f32[1024,1024]{1,0:T(8,128)} fusion(bf16[1024,2048]{1,0:T(8,128)(2,1)} %bitcast.23), kind=kOutput, calls=%fused_computation.12 | convolution fusion | flops 2147483648 | bytes 8388608 | tf_op jit(solution)/shard_map/dot_general | solution.py:156
  95.7 9.7 %shard_map.86 = bf16[64,3,16,128]{3,2,1,0:T(8,128)(2,1)} custom-call(s32[768]{0:T(1024)} %reshape.113.cols_ref, s32[128]{0:T(128)} %cnt_ref.3, f32[1024,1024]{1,0:T(8,128)} %fusion.7.pt_ref), custom_call_target="tpu_custom_call" | custom-call | tf_op jit(solution)/shard_map/pallas_call | solution.py:115
  105.4 1.1 all-gather.2.cloned.1.call-done.bt_ref
  106.5 17.5 %shard_map.87 = f32[128,8192]{1,0:T(8,128)} custom-call(s32[768]{0:T(1024)} %reshape.113.cols_ref, s32[128]{0:T(128)} %cnt_ref.3, bf16[128,1024]{1,0:T(8,128)(2,1)} %copy.31.gp_ref, bf16[128,3,64,128]{3,2,1,0:T(8,128)(2,1)} %all-gather.2.cloned.1.call-done.bt_ref), custom_call_target="tpu_custom_call" | custom-call | tf_op jit(solution)/shard_map/pallas_call | solution.py:75
  124.0 2.8 %fusion.6 = f32[128]{0:T(128)S(1)} fusion(bf16[128,8192]{1,0:T(8,128)(2,1)S(1)} %copy-done, f32[128,8192]{1,0:T(8,128)} %shard_map.87, f32[8192]{0:T(1024)S(1)} %copy-done.1), kind=kLoop, calls=%fused_computation.10 | loop fusion | flops 4194176 | bytes 6324736 | tf_op jit(solution)/shard_map/reduce_sum | solution.py:172
  126.8 10.1 %all-to-all-start.1 = ((bf16[64,3,16,128]{3,2,1,0:T(8,128)(2,1)}), bf16[64,3,16,128]{3,2,1,0:T(8,128)(2,1)S(1)}, u32[]{:S(2)}, u32[]{:S(2)}) async-start(bf16[64,3,16,128]{3,2,1,0:T(8,128)(2,1)} %shard_map.86), calls=%async_computation.1 | async-start | bytes 1572864 | tf_op jit(solution)/shard_map/all_to_all | solution.py:161
  137.0 4.7 %fusion.5 = bf16[128,8192]{1,0:T(8,128)(2,1)} fusion(bf16[128,8192]{1,0:T(8,128)(2,1)S(1)} %copy-done, f32[128,8192]{1,0:T(8,128)} %shard_map.87, f32[128]{0:T(128)S(1)} %broadcast_multiply_fusion, f32[128]{0:T(128)S(1)} %get-tuple-element.10, f32[8192]{0:T(1024)S(1)} %copy-done.1, f32[128]{0:T(128)S(1)} %get-tuple-element.11), kind=kLoop, calls=%fused_computation.9 | loop fusion | flops 7340032 | bytes 8422912 | tf_op jit(solution)/shard_map/convert_element_type | solution.py:173
  141.7 19.2 %all-to-all-done.1 = bf16[64,3,16,128]{3,2,1,0:T(8,128)(2,1)S(1)} async-done(((bf16[64,3,16,128]{3,2,1,0:T(8,128)(2,1)}), bf16[64,3,16,128]{3,2,1,0:T(8,128)(2,1)S(1)}, u32[]{:S(2)}, u32[]{:S(2)}) %all-to-all-start.1) | async-done | bytes 786464 | tf_op jit(solution)/shard_map/all_to_all | solution.py:161
  161.2 0.7 reshape.122
  (20 shorter events, 0.9 us)
Async XLA Ops:
  7.2 6.2 %copy-start = (bf16[128,8192]{1,0:T(8,128)(2,1)S(1)}, bf16[128,8192]{1,0:T(8,128)(2,1)}, u32[]{:S(2)}) copy-start(bf16[128,8192]{1,0:T(8,128)(2,1)} %param.7) | copy-start | bytes 6291460
  7.2 6.2 %copy-start.1 = (f32[8192]{0:T(1024)S(1)}, f32[8192]{0:T(1024)}, u32[]{:S(2)}) copy-start(f32[8192]{0:T(1024)} %param.8) | copy-start | bytes 98308
  7.2 99.3 %all-gather.2.cloned.1.call-start = ((), (), s32[]{:S(2)}) async-start(), calls=%async_computation.2 | async-start | bytes 6389760 | tf_op jit(solution)/shard_map/all_gather | solution.py:140
  24.3 11.3 %copy-start.2 = (s32[128,6]{0,1:T(8,128)S(1)}, s32[128,6]{0,1:T(8,128)}, u32[]{:S(2)}) copy-start(s32[128,6]{0,1:T(8,128)} %param.11) | copy-start | bytes 9220
  24.3 58.2 %all-to-all-start = ((bf16[128,8,2048]{0,2,1:T(8,128)(2,1)}), bf16[128,8,2048]{0,2,1:T(8,128)(2,1)}, u32[]{:S(2)}, u32[]{:S(2)}) async-start(bf16[128,8,2048]{0,2,1:T(8,128)(2,1)} %pad_maximum_fusion), calls=%async_computation | async-start | bytes 8388608 | tf_op jit(solution)/shard_map/all_to_all | solution.py:150
  126.8 34.1 %all-to-all-start.1 = ((bf16[64,3,16,128]{3,2,1,0:T(8,128)(2,1)}), bf16[64,3,16,128]{3,2,1,0:T(8,128)(2,1)S(1)}, u32[]{:S(2)}, u32[]{:S(2)}) async-start(bf16[64,3,16,128]{3,2,1,0:T(8,128)(2,1)} %shard_map.86), calls=%async_computation.1 | async-start | bytes 1572864 | tf_op jit(solution)/shard_map/all_to_all | solution.py:161
Sparse Core Ops, SparseCore 0:
  11.0 95.3 all-gather.1

commit v7 on v6

--- a/solution.py
+++ b/solution.py
@@ -32,8 +32,11 @@
     return jnp.stack([first, second], axis=2).reshape(-1, KVW).astype(jnp.bfloat16)
 
 
-def _normed_grad_kernel(cols_ref, cnt_ref, gp_ref, bt_ref, out_ref, w_ref):
+def _normed_grad_kernel(cols_ref, cnt_ref, core_ref, gp_ref, own_ref, other_ref, out_ref, w_ref):
     step = pl.program_id(0)
+    rows = own_ref.shape[2]
+    own_at = core_ref[0] * rows
+    other_at = (1 - core_ref[0]) * rows
 
     @pl.when(step == 0)
     def _():
@@ -43,33 +46,35 @@
         for rr in range(ROWS_PER_STEP):
             row = step * ROWS_PER_STEP + rr
             live = cnt_ref[row]
+            lanes = slice(rr * BLK, (rr + 1) * BLK)
             for k in range(MOSTR):
-                start = pl.multiple_of(cols_ref[row * MOSTR + k] * BLK, BLK)
+                start = cols_ref[row * MOSTR + k] * BLK
                 if fill:
                     half = (k % 2) * BLK
-                    value = bt_ref[rr, k // 2, :, half:half + BLK]
-                    value = jnp.where(k < live, value, jnp.zeros_like(value))
+                    for at, ref in ((own_at, own_ref), (other_at, other_ref)):
+                        value = ref[rr, k // 2, :, half:half + BLK]
+                        value = jnp.where(k < live, value, jnp.zeros_like(value))
+                        w_ref[pl.ds(pl.multiple_of(start + at, rows), rows), lanes] = value
                 else:
-                    value = jnp.zeros((BLK, BLK), w_ref.dtype)
-                w_ref[pl.ds(start, BLK), rr * BLK:(rr + 1) * BLK] = value
+                    zero = jnp.zeros((BLK, BLK), w_ref.dtype)
+                    w_ref[pl.ds(pl.multiple_of(start, BLK), BLK), lanes] = zero
 
     place(True)
     out_ref[...] = jnp.dot(gp_ref[...], w_ref[...], preferred_element_type=jnp.float32)
     place(False)
 
 
-def normed_grad_of(grad_pre, blocks_t, cols, counts):
+def normed_grad_of(grad_pre, own, other, core, cols, counts):
     tok = grad_pre.shape[0]
-    row_blocks = blocks_t.shape[0]
+    row_blocks = own.shape[0]
+    rows = own.shape[2]
     width = ROWS_PER_STEP * BLK
+    half_spec = pl.BlockSpec((ROWS_PER_STEP, MOSTR // 2, rows, 2 * BLK), lambda g, c, n, h: (g, 0, 0, 0))
     spec = pltpu.PrefetchScalarGridSpec(
-        num_scalar_prefetch=2,
+        num_scalar_prefetch=3,
         grid=(row_blocks // ROWS_PER_STEP,),
-        in_specs=[
-            pl.BlockSpec((tok, KVW), lambda g, c, n: (0, 0)),
-            pl.BlockSpec((ROWS_PER_STEP, MOSTR // 2, BLK, 2 * BLK), lambda g, c, n: (g, 0, 0, 0)),
-        ],
-        out_specs=pl.BlockSpec((tok, width), lambda g, c, n: (0, g)),
+        in_specs=[pl.BlockSpec((tok, KVW), lambda g, c, n, h: (0, 0)), half_spec, half_spec],
+        out_specs=pl.BlockSpec((tok, width), lambda g, c, n, h: (0, g)),
         scratch_shapes=[pltpu.VMEM((KVW, width), jnp.bfloat16)],
     )
     return pl.pallas_call(
@@ -77,7 +82,7 @@
         grid_spec=spec,
         out_shape=jax.ShapeDtypeStruct((tok, row_blocks * BLK), jnp.float32),
         compiler_params=pltpu.CompilerParams(dimension_semantics=("arbitrary",)),
-    )(cols.reshape(-1), counts, grad_pre, blocks_t)
+    )(cols.reshape(-1), counts, core, grad_pre, own, other)
 
 
 def _pick_kernel(cols_ref, cnt_ref, pt_ref, out_ref, *, part_rows, divisor):
@@ -137,7 +142,12 @@
         .transpose(0, 1, 4, 2, 3)
         .reshape(key_blocks.shape[0], MOSTR // 2, BLK, 2 * BLK)
     )
-    piece = lax.all_gather(local_t, ("z", "y"), axis=0, tiled=True)
+    cores = lax.axis_size("c")
+    core = lax.axis_index("c")
+    half_rows = BLK // cores
+    local_h = lax.dynamic_slice_in_dim(local_t, core * half_rows, half_rows, axis=2)
+    own = lax.all_gather(local_h, ("z", "y"), axis=0, tiled=True)
+    other = lax.ppermute(own, "c", perm=[(i, (i + 1) % cores) for i in range(cores)])
 
     split_normed = (
         normed.reshape(tok_rows, row_blocks, groups, part_rows)
@@ -149,6 +159,8 @@
     )
     received = lax.all_to_all(sent, ("x", "c"), split_axis=1, concat_axis=0, tiled=True)
     received = received.reshape(groups * tok_rows, row_blocks * part_rows + KVW)
+    normed_grad = normed_grad_of(grad_pre, own, other, core.reshape(1), kept_cols, kept_count)
+    normed_grad, received = lax.optimization_barrier((normed_grad, received))
     grad_all = received[:, row_blocks * part_rows:]
     normed_rows = received[:, : row_blocks * part_rows].reshape(groups * tok_rows, row_blocks, part_rows)
     divisor = math.sqrt(tok_rows * groups * dp_size)
@@ -157,7 +169,6 @@
         grad_all, slab, (((0,), (0,)), ((), ())), preferred_element_type=jnp.float32
     )
     partial = pick_blocks(product, kept_cols, kept_count, part_rows, divisor, dp_size)
-    partial, piece = lax.optimization_barrier((partial, piece))
     summed = lax.all_to_all(partial, ("z", "y"), split_axis=0, concat_axis=0, tiled=True)
     summed = summed.astype(jnp.float32).sum(axis=0)
     own_rows = summed.shape[1] // part_rows
@@ -167,7 +178,6 @@
         .reshape(own_rows, MOSTR, part_rows * BLK)
     )
 
-    normed_grad = normed_grad_of(grad_pre, piece, kept_cols, kept_count)
     scaled = norm_gain * normed_grad
     grads = inv_rms * scaled - inv_rms**3 * xf * jnp.mean(scaled * xf, axis=1, keepdims=True)
     return (grads.astype(jnp.bfloat16), block_grad)

time: 171 us -> 189 us (1.11)
  waiting for transfers between devices: 66.3 us -> 86.8 us
  matrix products: 6.69 us -> 4.35 us
    all_gather x1, waiting for transfers between devices: 1.09 us -> 66.7 us  [shards(): own = lax.all_gather(local_h, ('z', 'y'), axis=0, tiled=True)]
    all_to_all x1, waiting for transfers between devices: 46 us -> 0.01 us  [shards(): lax.all_to_all(sent, ('x', 'c'), split_axis=1, concat_axis=0, tiled=True)]
    dot_general x1, matrix products: 6.69 us -> 4.35 us  [shards(): lax.dot_general(grad_all, slab, (((0,), (0,)), ((), ())), preferred_eleme...]
    ppermute x0 -> x1, starting transfers between devices: none -> 1.91 us  [shards(): lax.ppermute(own, 'c', perm=[(i, (i + 1) % cores) for i in range(cores)])]
  transfers between devices with their start and end apart: 3 -> 4, of which waited for: 3 -> 2; matrix products, arithmetic and copies ran while one was open for 20% -> 15% of each run, Pallas kernels for 6% -> 0%
where the time goes in v7:
time: 189 us; the launch traced here: 187 us
  waiting for transfers between devices  86.8 us (46%)
  Pallas kernels  26.9 us (14%)
  starting transfers between devices  20.9 us (11%)
  local copies, waits for them, and re-layouts  19.1 us (10%)
  other arithmetic  15 us (8%)
  between operations  14.2 us (8%)
  matrix products  4.35 us (2%)
    all_gather x1, waiting for transfers between devices, shards(): own = lax.all_gather(local_h, ('z', 'y'), axis=0, tiled=True)  66.7 us
    all_to_all x1, waiting for transfers between devices, shards(): lax.all_to_all(partial, ('z', 'y'), split_axis=0, concat_axis=0, tiled=True)  20.1 us
    pallas_call x1, Pallas kernels, normed_grad_of(): pl.pallas_call(_normed_grad_kernel, grid_spec=spec, out_shape=jax.ShapeDt...  17.3 us
    all_to_all x1, starting transfers between devices, shards(): lax.all_to_all(sent, ('x', 'c'), split_axis=1, concat_axis=0, tiled=True)  10.4 us
    pallas_call x1, Pallas kernels, pick_blocks(): pl.pallas_call(functools.partial(_pick_kernel, part_rows=part_rows, divis...  9.66 us
    all_to_all x1, starting transfers between devices, shards(): lax.all_to_all(partial, ('z', 'y'), split_axis=0, concat_axis=0, tiled=True)  8.53 us
    all_to_all x1, local copies, waits for them, and re-layouts, shards(): lax.all_to_all(sent, ('x', 'c'), split_axis=1, concat_axis=0, tiled=True)  6.52 us
    convert_element_type x1, other arithmetic, shards(): return (grads.astype(jnp.bfloat16), block_grad)  4.7 us
  transfers between devices with their start and end apart: 4, of which 2 were waited for; matrix products, arithmetic and copies ran while one was open for 15% of the time, Pallas kernels for 0%

profile of v7, /device:TPU:6, one launch (start us, length us, event | category | flops | bytes accessed | tf_op | source)
XLA Modules:
  0.0 187.3 jit_solution(18181954370183746252)
XLA Ops:
  7.2 1.2 reshape.120
  8.7 0.6 constant_dynamic-slice_fusion
  9.4 0.7 convert_element_type.27
  10.1 1.1 copy.26
  11.2 2.1 %fusion = f32[128]{0:T(128)S(1)} fusion(bf16[128,8192]{1,0:T(8,128)(2,1)} %param.7), kind=kLoop, calls=%fused_computation.4 | loop fusion | flops 3145600 | bytes 2097664 | tf_op jit(solution)/shard_map/reduce_sum | solution.py:136
  13.3 1.9 %fusion.2 = bf16[128,8192]{1,0:T(8,128)(2,1)} fusion(bf16[128,8192]{1,0:T(8,128)(2,1)S(1)} %copy-done, f32[8192]{0:T(1024)S(1)} %copy-done.2, f32[128]{0:T(128)S(1)} %get-tuple-element.11), kind=kLoop, calls=%fused_computation.6 | loop fusion | flops 4194304 | bytes 4227584 | tf_op jit(solution)/shard_map/convert_element_type | solution.py:137
  15.2 4.1 %copy.29 = bf16[128,8192]{0,1:T(8,128)(2,1)} copy(bf16[128,8192]{1,0:T(8,128)(2,1)} %fusion.2) | data formatting | bytes 4194304 | tf_op jit(solution)/shard_map/convert_element_type | solution.py:137
  19.3 2.0 %copy.34 = bf16[128,8,128,8]{0,3,2,1:T(8,128)(2,1)S(1)} copy(bf16[128,8,128,8]{0,3,1,2:T(8,128)(2,1)} %bitcast.22) | data formatting | bytes 4194304 | tf_op jit(solution)/shard_map/transpose | solution.py:154
  21.9 2.2 %pad_maximum_fusion = bf16[128,8,2048]{0,2,1:T(8,128)(2,1)} fusion(bf16[128,8,1024]{0,2,1:T(8,128)(2,1)S(1)} %broadcast_in_dim.2, bf16[128,8,1024]{0,2,1:T(8,128)(2,1)S(1)} %bitcast.23), kind=kLoop, calls=%fused_computation.11 | loop fusion | flops 8388608 | bytes 8388608 | tf_op jit(solution)/shard_map/concatenate | solution.py:157
  24.2 10.4 %all-to-all-start = ((bf16[128,8,2048]{0,2,1:T(8,128)(2,1)}), bf16[128,8,2048]{0,2,1:T(8,128)(2,1)}, u32[]{:S(2)}, u32[]{:S(2)}) async-start(bf16[128,8,2048]{0,2,1:T(8,128)(2,1)} %pad_maximum_fusion), calls=%async_computation | async-start | bytes 8388608 | tf_op jit(solution)/shard_map/all_to_all | solution.py:160
  34.6 66.7 %all-gather.2.cloned.1.call-done.own_ref = bf16[128,3,32,128]{3,2,1,0:T(8,128)(2,1)} async-done(((bf16[2,3,32,128]{3,2,1,0:T(8,128)(2,1)}), bf16[128,3,32,128]{3,2,1,0:T(8,128)(2,1)}) %all-gather.2.cloned.1.call-update) | async-done | bytes 3145744 | tf_op jit(solution)/shard_map/all_gather | solution.py:149
  101.3 1.9 %collective-permute-start = (bf16[128,3,32,128]{3,2,1,0:T(8,128)(2,1)}, bf16[128,3,32,128]{3,2,1,0:T(8,128)(2,1)}, u32[]{:S(2)}, u32[]{:S(2)}) collective-permute-start(bf16[128,3,32,128]{3,2,1,0:T(8,128)(2,1)} %all-gather.2.cloned.1.call-done.own_ref), channel_id=1, source_target_pairs={{0,1},{1,0},{2,3},{3,2},{4,5},{5,4},{6,7},{7,6},{8,9},{9,8},{10,11... | collective-permute-start | bytes 9437192 | tf_op jit(solution)/shard_map/ppermute | solution.py:150
  103.2 0.9 copy.28.gp_ref
  104.2 0.7 reshape.116.cols_ref
  104.9 6.5 %copy.31 = bf16[8,128,1,2048]{3,1,0,2:T(8,128)(2,1)} copy(bf16[8,128,1,2048]{1,3,0,2:T(8,128)(2,1)} %bitcast.9) | data formatting | bytes 8388608 | tf_op jit(solution)/shard_map/all_to_all | solution.py:160
  111.4 17.3 %shard_map.86 = f32[128,8192]{1,0:T(8,128)} custom-call(s32[768]{0:T(1024)} %reshape.116.cols_ref, s32[128]{0:T(128)} %cnt_ref.3, s32[1]{0:T(128)} %bitcast.core_ref, bf16[128,1024]{1,0:T(8,128)(2,1)} %copy.28.gp_ref, bf16[128,3,32,128]{3,2,1,0:T(8,128)(2,1)} %all-gather.2.cloned.1.call-done.own_ref, bf16[128,3,32,128]{3,2,1,0:T(8,128)(2,1)} %collective-permute-done.other_ref), custom_call_target="tpu_custom_call" | custom-call | tf_op jit(solution)/shard_map/pallas_call | solution.py:80
  128.7 3.0 %fusion.6 = f32[128]{0:T(128)S(1)} fusion(bf16[128,8192]{1,0:T(8,128)(2,1)S(1)} %copy-done, f32[128,8192]{1,0:T(8,128)} %shard_map.86, f32[8192]{0:T(1024)S(1)} %copy-done.2), kind=kLoop, calls=%fused_computation.10 | loop fusion | flops 4194176 | bytes 6324736 | tf_op jit(solution)/shard_map/reduce_sum | solution.py:182
  131.7 0.5 copy-done.1
  132.2 4.4 %fusion.7.pt_ref = f32[1024,1024]{1,0:T(8,128)} fusion(bf16[1024,2048]{1,0:T(8,128)(2,1)S(1)} %bitcast.24), kind=kOutput, calls=%fused_computation.13 | convolution fusion | flops 2147483648 | bytes 8388608 | tf_op jit(solution)/shard_map/dot_general | solution.py:168
  136.5 9.7 %shard_map.87 = bf16[64,3,16,128]{3,2,1,0:T(8,128)(2,1)} custom-call(s32[768]{0:T(1024)} %reshape.116.cols_ref, s32[128]{0:T(128)} %cnt_ref.3, f32[1024,1024]{1,0:T(8,128)} %fusion.7.pt_ref), custom_call_target="tpu_custom_call" | custom-call | tf_op jit(solution)/shard_map/pallas_call | solution.py:120
  146.2 8.5 %all-to-all-start.1 = ((bf16[64,3,16,128]{3,2,1,0:T(8,128)(2,1)}), bf16[64,3,16,128]{3,2,1,0:T(8,128)(2,1)S(1)}, u32[]{:S(2)}, u32[]{:S(2)}) async-start(bf16[64,3,16,128]{3,2,1,0:T(8,128)(2,1)} %shard_map.87), calls=%async_computation.1 | async-start | bytes 1572864 | tf_op jit(solution)/shard_map/all_to_all | solution.py:172
  154.7 4.7 %fusion.5 = bf16[128,8192]{1,0:T(8,128)(2,1)} fusion(bf16[128,8192]{1,0:T(8,128)(2,1)S(1)} %copy-done, f32[128,8192]{1,0:T(8,128)} %shard_map.86, f32[128]{0:T(128)S(1)} %broadcast_multiply_fusion, f32[128]{0:T(128)S(1)} %get-tuple-element.10, f32[8192]{0:T(1024)S(1)} %copy-done.2, f32[128]{0:T(128)S(1)} %get-tuple-element.11), kind=kLoop, calls=%fused_computation.9 | loop fusion | flops 7340032 | bytes 8422912 | tf_op jit(solution)/shard_map/convert_element_type | solution.py:183
  159.4 20.1 %all-to-all-done.1 = bf16[64,3,16,128]{3,2,1,0:T(8,128)(2,1)S(1)} async-done(((bf16[64,3,16,128]{3,2,1,0:T(8,128)(2,1)}), bf16[64,3,16,128]{3,2,1,0:T(8,128)(2,1)S(1)}, u32[]{:S(2)}, u32[]{:S(2)}) %all-to-all-start.1) | async-done | bytes 786464 | tf_op jit(solution)/shard_map/all_to_all | solution.py:172
  179.8 0.7 reshape.126
  (25 shorter events, 1.3 us)
Async XLA Ops:
  7.2 6.2 %copy-start = (bf16[128,8192]{1,0:T(8,128)(2,1)S(1)}, bf16[128,8192]{1,0:T(8,128)(2,1)}, u32[]{:S(2)}) copy-start(bf16[128,8192]{1,0:T(8,128)(2,1)} %param.7) | copy-start | bytes 6291460
  7.2 6.2 %copy-start.2 = (f32[8192]{0:T(1024)S(1)}, f32[8192]{0:T(1024)}, u32[]{:S(2)}) copy-start(f32[8192]{0:T(1024)} %param.8) | copy-start | bytes 98308
  7.2 94.1 %all-gather.2.cloned.1.call-start = ((), (), s32[]{:S(2)}) async-start(), calls=%async_computation.2 | async-start | bytes 3194880 | tf_op jit(solution)/shard_map/all_gather | solution.py:149
  24.2 79.9 %copy-start.3 = (s32[128,6]{0,1:T(8,128)S(1)}, s32[128,6]{0,1:T(8,128)}, u32[]{:S(2)}) copy-start(s32[128,6]{0,1:T(8,128)} %param.11) | copy-start | bytes 9220
  24.2 80.8 %all-to-all-start = ((bf16[128,8,2048]{0,2,1:T(8,128)(2,1)}), bf16[128,8,2048]{0,2,1:T(8,128)(2,1)}, u32[]{:S(2)}, u32[]{:S(2)}) async-start(bf16[128,8,2048]{0,2,1:T(8,128)(2,1)} %pad_maximum_fusion), calls=%async_computation | async-start | bytes 8388608 | tf_op jit(solution)/shard_map/all_to_all | solution.py:160
  101.3 10.1 %collective-permute-start = (bf16[128,3,32,128]{3,2,1,0:T(8,128)(2,1)}, bf16[128,3,32,128]{3,2,1,0:T(8,128)(2,1)}, u32[]{:S(2)}, u32[]{:S(2)}) collective-permute-start(bf16[128,3,32,128]{3,2,1,0:T(8,128)(2,1)} %all-gather.2.cloned.1.call-done.own_ref), channel_id=1, source_target_pairs={{0,1},{1,0},{2,3},{3,2},{4,5},{5,4},{6,7},{7,6},{8,9},{9,8},{10,11... | collective-permute-start | bytes 9437192 | tf_op jit(solution)/shard_map/ppermute | solution.py:150
  128.7 3.4 %copy-start.1 = (bf16[8,128,1,2048]{3,1,0,2:T(8,128)(2,1)S(1)}, bf16[8,128,1,2048]{3,1,0,2:T(8,128)(2,1)}, u32[]{:S(2)}) copy-start(bf16[8,128,1,2048]{3,1,0,2:T(8,128)(2,1)} %copy.31) | copy-start | bytes 12582916
  146.2 33.3 %all-to-all-start.1 = ((bf16[64,3,16,128]{3,2,1,0:T(8,128)(2,1)}), bf16[64,3,16,128]{3,2,1,0:T(8,128)(2,1)S(1)}, u32[]{:S(2)}, u32[]{:S(2)}) async-start(bf16[64,3,16,128]{3,2,1,0:T(8,128)(2,1)} %shard_map.87), calls=%async_computation.1 | async-start | bytes 1572864 | tf_op jit(solution)/shard_map/all_to_all | solution.py:172
Sparse Core Ops, SparseCore 0:
  11.0 90.2 all-gather.1

commit v8 on v6

--- a/solution.py
+++ b/solution.py
@@ -159,6 +159,11 @@
     partial = pick_blocks(product, kept_cols, kept_count, part_rows, divisor, dp_size)
     partial, piece = lax.optimization_barrier((partial, piece))
     summed = lax.all_to_all(partial, ("z", "y"), split_axis=0, concat_axis=0, tiled=True)
+    normed_grad = normed_grad_of(grad_pre, piece, kept_cols, kept_count)
+    scaled = norm_gain * normed_grad
+    grads = inv_rms * scaled - inv_rms**3 * xf * jnp.mean(scaled * xf, axis=1, keepdims=True)
+    grads = grads.astype(jnp.bfloat16)
+    summed, grads = lax.optimization_barrier((summed, grads))
     summed = summed.astype(jnp.float32).sum(axis=0)
     own_rows = summed.shape[1] // part_rows
     block_grad = (
@@ -167,10 +172,7 @@
         .reshape(own_rows, MOSTR, part_rows * BLK)
     )
 
-    normed_grad = normed_grad_of(grad_pre, piece, kept_cols, kept_count)
-    scaled = norm_gain * normed_grad
-    grads = inv_rms * scaled - inv_rms**3 * xf * jnp.mean(scaled * xf, axis=1, keepdims=True)
-    return (grads.astype(jnp.bfloat16), block_grad)
+    return (grads, block_grad)
 
 
 def _split_mesh(mesh):

time: 171 us -> 151 us (0.88)
  waiting for transfers between devices: 66.3 us -> 47.4 us
  other arithmetic: 15 us -> 13 us
    all_to_all x1, waiting for transfers between devices: 19.2 us -> 0.34 us  [shards(): lax.all_to_all(partial, ('z', 'y'), split_axis=0, concat_axis=0, tiled=True)]
    convert_element_type x1, other arithmetic: 4.7 us -> 2.6 us  [shards(): grads = grads.astype(jnp.bfloat16)]
  transfers between devices with their start and end apart: 3 -> 3, of which waited for: 3 -> 3; matrix products, arithmetic and copies ran while one was open for 20% -> 24% of each run, Pallas kernels for 6% -> 18%
where the time goes in v8:
time: 151 us; the launch traced here: 148 us
  waiting for transfers between devices  47.4 us (31%)
  Pallas kernels  27.2 us (18%)
  starting transfers between devices  20.7 us (14%)
  local copies, waits for them, and re-layouts  19.2 us (13%)
  between operations  14.2 us (9%)
  other arithmetic  13 us (9%)
  matrix products  6.7 us (4%)
    all_to_all x1, waiting for transfers between devices, shards(): lax.all_to_all(sent, ('x', 'c'), split_axis=1, concat_axis=0, tiled=True)  46 us
    pallas_call x1, Pallas kernels, normed_grad_of(): pl.pallas_call(_normed_grad_kernel, grid_spec=spec, out_shape=jax.ShapeDt...  17.5 us
    all_to_all x1, starting transfers between devices, shards(): lax.all_to_all(sent, ('x', 'c'), split_axis=1, concat_axis=0, tiled=True)  10.5 us
    all_to_all x1, starting transfers between devices, shards(): lax.all_to_all(partial, ('z', 'y'), split_axis=0, concat_axis=0, tiled=True)  10.2 us
    pallas_call x1, Pallas kernels, pick_blocks(): pl.pallas_call(functools.partial(_pick_kernel, part_rows=part_rows, divis...  9.67 us
    dot_general x1, matrix products, shards(): lax.dot_general(grad_all, slab, (((0,), (0,)), ((), ())), preferred_eleme...  6.7 us
    all_to_all x1, local copies, waits for them, and re-layouts, shards(): lax.all_to_all(sent, ('x', 'c'), split_axis=1, concat_axis=0, tiled=True)  6.57 us
    convert_element_type x1, local copies, waits for them, and re-layouts, shards(): normed = (xf * inv_rms * norm_gain).astype(jnp.bfloat16)  4.12 us
  transfers between devices with their start and end apart: 3, of which 3 were waited for; matrix products, arithmetic and copies ran while one was open for 24% of the time, Pallas kernels for 18%

profile of v8, /device:TPU:6, one launch (start us, length us, event | category | flops | bytes accessed | tf_op | source)
XLA Modules:
  0.0 148.4 jit_solution(6696906700878177314)
XLA Ops:
  7.2 1.2 reshape.119
  8.6 0.8 reshape.120
  9.4 1.1 copy.28
  10.6 0.7 convert_element_type.28
  11.3 2.1 %fusion = f32[128]{0:T(128)S(1)} fusion(bf16[128,8192]{1,0:T(8,128)(2,1)} %param.7), kind=kLoop, calls=%fused_computation.4 | loop fusion | flops 3145600 | bytes 2097664 | tf_op jit(solution)/shard_map/reduce_sum | solution.py:131
  13.4 1.9 %fusion.2 = bf16[128,8192]{1,0:T(8,128)(2,1)} fusion(bf16[128,8192]{1,0:T(8,128)(2,1)S(1)} %copy-done.1, f32[8192]{0:T(1024)S(1)} %copy-done.2, f32[128]{0:T(128)S(1)} %get-tuple-element.15), kind=kLoop, calls=%fused_computation.6 | loop fusion | flops 4194304 | bytes 4227584 | tf_op jit(solution)/shard_map/convert_element_type | solution.py:132
  15.3 4.1 %copy.26 = bf16[128,8192]{0,1:T(8,128)(2,1)} copy(bf16[128,8192]{1,0:T(8,128)(2,1)} %fusion.2) | data formatting | bytes 4194304 | tf_op jit(solution)/shard_map/convert_element_type | solution.py:132
  19.4 2.0 %copy.34 = bf16[128,8,128,8]{0,3,2,1:T(8,128)(2,1)S(1)} copy(bf16[128,8,128,8]{0,3,1,2:T(8,128)(2,1)} %bitcast.21) | data formatting | bytes 4194304 | tf_op jit(solution)/shard_map/transpose | solution.py:144
  22.0 2.3 %pad_maximum_fusion = bf16[128,8,2048]{0,2,1:T(8,128)(2,1)} fusion(bf16[128,8,1024]{0,2,1:T(8,128)(2,1)S(1)} %broadcast_in_dim.2, bf16[128,8,1024]{0,2,1:T(8,128)(2,1)S(1)} %bitcast.22), kind=kLoop, calls=%fused_computation.11 | loop fusion | flops 8388608 | bytes 8388608 | tf_op jit(solution)/shard_map/concatenate | solution.py:147
  24.3 10.5 %all-to-all-start = ((bf16[128,8,2048]{0,2,1:T(8,128)(2,1)}), bf16[128,8,2048]{0,2,1:T(8,128)(2,1)}, u32[]{:S(2)}, u32[]{:S(2)}) async-start(bf16[128,8,2048]{0,2,1:T(8,128)(2,1)} %pad_maximum_fusion), calls=%async_computation | async-start | bytes 8388608 | tf_op jit(solution)/shard_map/all_to_all | solution.py:150
  34.8 0.8 copy.31.gp_ref
  35.7 0.7 reshape.113.cols_ref
  36.5 46.0 %all-to-all-done = bf16[128,8,2048]{0,2,1:T(8,128)(2,1)} async-done(((bf16[128,8,2048]{0,2,1:T(8,128)(2,1)}), bf16[128,8,2048]{0,2,1:T(8,128)(2,1)}, u32[]{:S(2)}, u32[]{:S(2)}) %all-to-all-start) | async-done | bytes 4194336 | tf_op jit(solution)/shard_map/all_to_all | solution.py:150
  82.5 6.6 %copy.29 = bf16[8,128,1,2048]{3,1,0,2:T(8,128)(2,1)} copy(bf16[8,128,1,2048]{1,3,0,2:T(8,128)(2,1)} %bitcast.7) | data formatting | bytes 8388608 | tf_op jit(solution)/shard_map/all_to_all | solution.py:150
  89.0 6.7 %fusion.7.pt_ref = f32[1024,1024]{1,0:T(8,128)} fusion(bf16[1024,2048]{1,0:T(8,128)(2,1)} %bitcast.23), kind=kOutput, calls=%fused_computation.12 | convolution fusion | flops 2147483648 | bytes 8388608 | tf_op jit(solution)/shard_map/dot_general | solution.py:156
  95.7 9.7 %shard_map.86 = bf16[64,3,16,128]{3,2,1,0:T(8,128)(2,1)} custom-call(s32[768]{0:T(1024)} %reshape.113.cols_ref, s32[128]{0:T(128)} %cnt_ref.3, f32[1024,1024]{1,0:T(8,128)} %fusion.7.pt_ref), custom_call_target="tpu_custom_call" | custom-call | tf_op jit(solution)/shard_map/pallas_call | solution.py:115
  105.4 1.1 all-gather.2.cloned.1.call-done.bt_ref
  106.5 10.2 %all-to-all-start.1 = ((bf16[64,3,16,128]{3,2,1,0:T(8,128)(2,1)}), bf16[64,3,16,128]{3,2,1,0:T(8,128)(2,1)S(1)}, u32[]{:S(2)}, u32[]{:S(2)}) async-start(bf16[64,3,16,128]{3,2,1,0:T(8,128)(2,1)} %shard_map.86), calls=%async_computation.1 | async-start | bytes 1572864 | tf_op jit(solution)/shard_map/all_to_all | solution.py:161
  116.6 17.5 %shard_map.87 = f32[128,8192]{1,0:T(8,128)} custom-call(s32[768]{0:T(1024)} %reshape.113.cols_ref, s32[128]{0:T(128)} %cnt_ref.3, bf16[128,1024]{1,0:T(8,128)(2,1)} %copy.31.gp_ref, bf16[128,3,64,128]{3,2,1,0:T(8,128)(2,1)} %all-gather.2.cloned.1.call-done.bt_ref), custom_call_target="tpu_custom_call" | custom-call | tf_op jit(solution)/shard_map/pallas_call | solution.py:75
  134.2 3.0 %fusion.6 = f32[128]{0:T(128)S(1)} fusion(bf16[128,8192]{1,0:T(8,128)(2,1)S(1)} %copy-done.1, f32[128,8192]{1,0:T(8,128)} %shard_map.87, f32[8192]{0:T(1024)S(1)} %copy-done.2), kind=kLoop, calls=%fused_computation.10 | loop fusion | flops 4194176 | bytes 6324736 | tf_op jit(solution)/shard_map/reduce_sum | solution.py:164
  137.2 0.5 copy-done
  137.6 2.6 %fusion.5 = bf16[128,8192]{1,0:T(8,128)(2,1)} fusion(bf16[128,8192]{1,0:T(8,128)(2,1)S(1)} %copy-done.1, f32[128,8192]{1,0:T(8,128)S(1)} %copy-done, f32[128]{0:T(128)S(1)} %broadcast_multiply_fusion, f32[128]{0:T(128)S(1)} %get-tuple-element.14, f32[8192]{0:T(1024)S(1)} %copy-done.2, f32[128]{0:T(128)S(1)} %get-tuple-element.15), kind=kLoop, calls=%fused_computation.9 | loop fusion | flops 7340032 | bytes 8422912 | tf_op jit(solution)/shard_map/convert_element_type | solution.py:165
  140.2 0.3 all-to-all-done.1
  140.8 0.7 reshape.122
  (22 shorter events, 1.2 us)
Async XLA Ops:
  7.2 6.2 %copy-start.1 = (bf16[128,8192]{1,0:T(8,128)(2,1)S(1)}, bf16[128,8192]{1,0:T(8,128)(2,1)}, u32[]{:S(2)}) copy-start(bf16[128,8192]{1,0:T(8,128)(2,1)} %param.7) | copy-start | bytes 6291460
  7.2 6.2 %copy-start.2 = (f32[8192]{0:T(1024)S(1)}, f32[8192]{0:T(1024)}, u32[]{:S(2)}) copy-start(f32[8192]{0:T(1024)} %param.8) | copy-start | bytes 98308
  7.2 99.3 %all-gather.2.cloned.1.call-start = ((), (), s32[]{:S(2)}) async-start(), calls=%async_computation.2 | async-start | bytes 6389760 | tf_op jit(solution)/shard_map/all_gather | solution.py:140
  24.3 11.3 %copy-start.3 = (s32[128,6]{0,1:T(8,128)S(1)}, s32[128,6]{0,1:T(8,128)}, u32[]{:S(2)}) copy-start(s32[128,6]{0,1:T(8,128)} %param.11) | copy-start | bytes 9220
  24.3 58.1 %all-to-all-start = ((bf16[128,8,2048]{0,2,1:T(8,128)(2,1)}), bf16[128,8,2048]{0,2,1:T(8,128)(2,1)}, u32[]{:S(2)}, u32[]{:S(2)}) async-start(bf16[128,8,2048]{0,2,1:T(8,128)(2,1)} %pad_maximum_fusion), calls=%async_computation | async-start | bytes 8388608 | tf_op jit(solution)/shard_map/all_to_all | solution.py:150
  106.5 34.1 %all-to-all-start.1 = ((bf16[64,3,16,128]{3,2,1,0:T(8,128)(2,1)}), bf16[64,3,16,128]{3,2,1,0:T(8,128)(2,1)S(1)}, u32[]{:S(2)}, u32[]{:S(2)}) async-start(bf16[64,3,16,128]{3,2,1,0:T(8,128)(2,1)} %shard_map.86), calls=%async_computation.1 | async-start | bytes 1572864 | tf_op jit(solution)/shard_map/all_to_all | solution.py:161
  134.2 3.4 %copy-start = (f32[128,8192]{1,0:T(8,128)S(1)}, f32[128,8192]{1,0:T(8,128)}, u32[]{:S(2)}) copy-start(f32[128,8192]{1,0:T(8,128)} %shard_map.87) | copy-start | bytes 12582916
Sparse Core Ops, SparseCore 0:
  11.0 95.3 all-gather.1

commit v9 on v8

--- a/solution.py
+++ b/solution.py
@@ -16,7 +16,7 @@
 BLK = 64
 MOSTR = 6
 SEQ_LEN = 1024
-ROWS_PER_STEP = 8
+ROWS_PER_STEP = 16
 
 
 def rope_back(grad, positions):
@@ -92,9 +92,7 @@
         for rr in range(per_step):
             row = step * per_step + rr
             start = pl.multiple_of(cols_ref[row * MOSTR + k] * BLK, BLK)
-            value = pt_ref[pl.ds(start, BLK), :]
-            value = jnp.where(k < cnt_ref[row], value, jnp.zeros_like(value))
-            acc = jnp.where(group == rr, value, acc)
+            acc = jnp.where(group == rr, pt_ref[pl.ds(start, BLK), :], acc)
         acc_t = (acc / divisor).T
         half = (k % 2) * BLK
         for d in range(dests):
@@ -171,6 +169,9 @@
         .transpose(1, 0, 3, 2, 4)
         .reshape(own_rows, MOSTR, part_rows * BLK)
     )
+    own_count = lax.dynamic_slice_in_dim(kept_count, lax.axis_index(("z", "y")) * own_rows, own_rows)
+    own_live = lax.broadcasted_iota(jnp.int32, (own_rows, MOSTR), 1) < own_count[:, None]
+    block_grad = jnp.where(own_live[:, :, None], block_grad, jnp.float32(0.0))
 
     return (grads, block_grad)
 

time: 151 us -> 149 us (0.987)
  waiting for transfers between devices: 47.4 us -> 52 us
  Pallas kernels: 27.2 us -> 22.7 us
  starting transfers between devices: 20.7 us -> 19.1 us
    all_to_all x1, waiting for transfers between devices: 0.34 us -> 3.31 us  [shards(): lax.all_to_all(partial, ('z', 'y'), split_axis=0, concat_axis=0, tiled=True)]
    pallas_call x1, Pallas kernels: 17.5 us -> 14.8 us  [normed_grad_of(): pl.pallas_call(_normed_grad_kernel, grid_spec=spec, out_shape=jax.ShapeDt...]
    all_gather x1, waiting for transfers between devices: 1.07 us -> 2.81 us  [shards(): piece = lax.all_gather(local_t, ('z', 'y'), axis=0, tiled=True)]
    pallas_call x1, Pallas kernels: 9.67 us -> 7.95 us  [pick_blocks(): pl.pallas_call(functools.partial(_pick_kernel, part_rows=part_rows, divis...]
    all_to_all x1, starting transfers between devices: 10.2 us -> 8.6 us  [shards(): lax.all_to_all(partial, ('z', 'y'), split_axis=0, concat_axis=0, tiled=True)]
  transfers between devices with their start and end apart: 3 -> 3, of which waited for: 3 -> 3; matrix products, arithmetic and copies ran while one was open for 24% -> 24% of each run, Pallas kernels for 18% -> 15%
where the time goes in v9:
time: 149 us; the launch traced here: 147 us
  waiting for transfers between devices  52 us (35%)
  Pallas kernels  22.7 us (15%)
  starting transfers between devices  19.1 us (13%)
  local copies, waits for them, and re-layouts  18.6 us (12%)
  between operations  14.2 us (10%)
  other arithmetic  13.7 us (9%)
  matrix products  6.7 us (4%)
    all_to_all x1, waiting for transfers between devices, shards(): lax.all_to_all(sent, ('x', 'c'), split_axis=1, concat_axis=0, tiled=True)  45.9 us
    pallas_call x1, Pallas kernels, normed_grad_of(): pl.pallas_call(_normed_grad_kernel, grid_spec=spec, out_shape=jax.ShapeDt...  14.8 us
    all_to_all x1, starting transfers between devices, shards(): lax.all_to_all(sent, ('x', 'c'), split_axis=1, concat_axis=0, tiled=True)  10.5 us
    all_to_all x1, starting transfers between devices, shards(): lax.all_to_all(partial, ('z', 'y'), split_axis=0, concat_axis=0, tiled=True)  8.6 us
    pallas_call x1, Pallas kernels, pick_blocks(): pl.pallas_call(functools.partial(_pick_kernel, part_rows=part_rows, divis...  7.95 us
    dot_general x1, matrix products, shards(): lax.dot_general(grad_all, slab, (((0,), (0,)), ((), ())), preferred_eleme...  6.7 us
    all_to_all x1, local copies, waits for them, and re-layouts, shards(): lax.all_to_all(sent, ('x', 'c'), split_axis=1, concat_axis=0, tiled=True)  6.54 us
    convert_element_type x1, local copies, waits for them, and re-layouts, shards(): normed = (xf * inv_rms * norm_gain).astype(jnp.bfloat16)  4.11 us
  transfers between devices with their start and end apart: 3, of which 3 were waited for; matrix products, arithmetic and copies ran while one was open for 24% of the time, Pallas kernels for 15%

profile of v9, /device:TPU:6, one launch (start us, length us, event | category | flops | bytes accessed | tf_op | source)
XLA Modules:
  0.0 147.1 jit_solution(4496870443138302441)
XLA Ops:
  7.2 1.2 reshape.138
  8.6 0.8 reshape.139
  9.4 1.1 copy.28
  10.6 0.7 convert_element_type.28
  11.3 2.1 %fusion = f32[128]{0:T(128)S(1)} fusion(bf16[128,8192]{1,0:T(8,128)(2,1)} %param.7), kind=kLoop, calls=%fused_computation.4 | loop fusion | flops 3145600 | bytes 2097664 | tf_op jit(solution)/shard_map/reduce_sum | solution.py:129
  13.4 1.9 %fusion.2 = bf16[128,8192]{1,0:T(8,128)(2,1)} fusion(bf16[128,8192]{1,0:T(8,128)(2,1)S(1)} %copy-done.1, f32[8192]{0:T(1024)S(1)} %copy-done.2, f32[128]{0:T(128)S(1)} %get-tuple-element.15), kind=kLoop, calls=%fused_computation.6 | loop fusion | flops 4194304 | bytes 4227584 | tf_op jit(solution)/shard_map/convert_element_type | solution.py:130
  15.3 4.1 %copy.26 = bf16[128,8192]{0,1:T(8,128)(2,1)} copy(bf16[128,8192]{1,0:T(8,128)(2,1)} %fusion.2) | data formatting | bytes 4194304 | tf_op jit(solution)/shard_map/convert_element_type | solution.py:130
  19.4 2.0 %copy.34 = bf16[128,8,128,8]{0,3,2,1:T(8,128)(2,1)S(1)} copy(bf16[128,8,128,8]{0,3,1,2:T(8,128)(2,1)} %bitcast.21) | data formatting | bytes 4194304 | tf_op jit(solution)/shard_map/transpose | solution.py:142
  22.0 2.3 %pad_maximum_fusion = bf16[128,8,2048]{0,2,1:T(8,128)(2,1)} fusion(bf16[128,8,1024]{0,2,1:T(8,128)(2,1)S(1)} %broadcast_in_dim.10, bf16[128,8,1024]{0,2,1:T(8,128)(2,1)S(1)} %bitcast.22), kind=kLoop, calls=%fused_computation.11 | loop fusion | flops 8388608 | bytes 8388608 | tf_op jit(solution)/shard_map/concatenate | solution.py:145
  24.3 10.5 %all-to-all-start = ((bf16[128,8,2048]{0,2,1:T(8,128)(2,1)}), bf16[128,8,2048]{0,2,1:T(8,128)(2,1)}, u32[]{:S(2)}, u32[]{:S(2)}) async-start(bf16[128,8,2048]{0,2,1:T(8,128)(2,1)} %pad_maximum_fusion), calls=%async_computation | async-start | bytes 8388608 | tf_op jit(solution)/shard_map/all_to_all | solution.py:148
  34.8 0.8 copy.31.gp_ref
  35.7 0.7 reshape.132.cols_ref
  36.6 45.9 %all-to-all-done = bf16[128,8,2048]{0,2,1:T(8,128)(2,1)} async-done(((bf16[128,8,2048]{0,2,1:T(8,128)(2,1)}), bf16[128,8,2048]{0,2,1:T(8,128)(2,1)}, u32[]{:S(2)}, u32[]{:S(2)}) %all-to-all-start) | async-done | bytes 4194336 | tf_op jit(solution)/shard_map/all_to_all | solution.py:148
  82.5 6.5 %copy.29 = bf16[8,128,1,2048]{3,1,0,2:T(8,128)(2,1)} copy(bf16[8,128,1,2048]{1,3,0,2:T(8,128)(2,1)} %bitcast.7) | data formatting | bytes 8388608 | tf_op jit(solution)/shard_map/all_to_all | solution.py:148
  89.0 6.7 %fusion.7.pt_ref = f32[1024,1024]{1,0:T(8,128)} fusion(bf16[1024,2048]{1,0:T(8,128)(2,1)} %bitcast.23), kind=kOutput, calls=%fused_computation.12 | convolution fusion | flops 2147483648 | bytes 8388608 | tf_op jit(solution)/shard_map/dot_general | solution.py:154
  95.7 8.0 %shard_map.86 = bf16[64,3,16,128]{3,2,1,0:T(8,128)(2,1)} custom-call(s32[768]{0:T(1024)} %reshape.132.cols_ref, s32[128]{0:T(128)} %cnt_ref.3, f32[1024,1024]{1,0:T(8,128)} %fusion.7.pt_ref), custom_call_target="tpu_custom_call" | custom-call | tf_op jit(solution)/shard_map/pallas_call | solution.py:113
  103.7 2.8 %all-gather.2.cloned.1.call-done.bt_ref = bf16[128,3,64,128]{3,2,1,0:T(8,128)(2,1)} async-done(((bf16[2,3,64,128]{3,2,1,0:T(8,128)(2,1)}), bf16[128,3,64,128]{3,2,1,0:T(8,128)(2,1)}) %all-gather.2.cloned.1.call-update) | async-done | bytes 6291472 | tf_op jit(solution)/shard_map/all_gather | solution.py:138
  106.5 8.6 %all-to-all-start.1 = ((bf16[64,3,16,128]{3,2,1,0:T(8,128)(2,1)}), bf16[64,3,16,128]{3,2,1,0:T(8,128)(2,1)S(1)}, u32[]{:S(2)}, u32[]{:S(2)}) async-start(bf16[64,3,16,128]{3,2,1,0:T(8,128)(2,1)} %shard_map.86), calls=%async_computation.1 | async-start | bytes 1572864 | tf_op jit(solution)/shard_map/all_to_all | solution.py:159
  115.1 14.8 %shard_map.87 = f32[128,8192]{1,0:T(8,128)} custom-call(s32[768]{0:T(1024)} %reshape.132.cols_ref, s32[128]{0:T(128)} %cnt_ref.3, bf16[128,1024]{1,0:T(8,128)(2,1)} %copy.31.gp_ref, bf16[128,3,64,128]{3,2,1,0:T(8,128)(2,1)} %all-gather.2.cloned.1.call-done.bt_ref), custom_call_target="tpu_custom_call" | custom-call | tf_op jit(solution)/shard_map/pallas_call | solution.py:75
  129.9 3.0 %fusion.6 = f32[128]{0:T(128)S(1)} fusion(bf16[128,8192]{1,0:T(8,128)(2,1)S(1)} %copy-done.1, f32[128,8192]{1,0:T(8,128)} %shard_map.87, f32[8192]{0:T(1024)S(1)} %copy-done.2), kind=kLoop, calls=%fused_computation.10 | loop fusion | flops 4194176 | bytes 6324736 | tf_op jit(solution)/shard_map/reduce_sum | solution.py:162
  132.8 0.5 copy-done
  133.3 2.6 %fusion.5 = bf16[128,8192]{1,0:T(8,128)(2,1)} fusion(bf16[128,8192]{1,0:T(8,128)(2,1)S(1)} %copy-done.1, f32[128,8192]{1,0:T(8,128)S(1)} %copy-done, f32[128]{0:T(128)S(1)} %broadcast_multiply_fusion, f32[128]{0:T(128)S(1)} %get-tuple-element.14, f32[8192]{0:T(1024)S(1)} %copy-done.2, f32[128]{0:T(128)S(1)} %get-tuple-element.15), kind=kLoop, calls=%fused_computation.9 | loop fusion | flops 7340032 | bytes 8422912 | tf_op jit(solution)/shard_map/convert_element_type | solution.py:163
  135.9 3.3 %all-to-all-done.1 = bf16[64,3,16,128]{3,2,1,0:T(8,128)(2,1)S(1)} async-done(((bf16[64,3,16,128]{3,2,1,0:T(8,128)(2,1)}), bf16[64,3,16,128]{3,2,1,0:T(8,128)(2,1)S(1)}, u32[]{:S(2)}, u32[]{:S(2)}) %all-to-all-start.1) | async-done | bytes 786464 | tf_op jit(solution)/shard_map/all_to_all | solution.py:159
  139.6 0.7 broadcast_select_fusion
  (27 shorter events, 1.4 us)
Async XLA Ops:
  7.2 6.2 %copy-start.1 = (bf16[128,8192]{1,0:T(8,128)(2,1)S(1)}, bf16[128,8192]{1,0:T(8,128)(2,1)}, u32[]{:S(2)}) copy-start(bf16[128,8192]{1,0:T(8,128)(2,1)} %param.7) | copy-start | bytes 6291460
  7.2 6.2 %copy-start.2 = (f32[8192]{0:T(1024)S(1)}, f32[8192]{0:T(1024)}, u32[]{:S(2)}) copy-start(f32[8192]{0:T(1024)} %param.8) | copy-start | bytes 98308
  7.2 99.3 %all-gather.2.cloned.1.call-start = ((), (), s32[]{:S(2)}) async-start(), calls=%async_computation.2 | async-start | bytes 6389760 | tf_op jit(solution)/shard_map/all_gather | solution.py:138
  24.3 11.3 %copy-start.3 = (s32[128,6]{0,1:T(8,128)S(1)}, s32[128,6]{0,1:T(8,128)}, u32[]{:S(2)}) copy-start(s32[128,6]{0,1:T(8,128)} %param.11) | copy-start | bytes 9220
  24.3 12.2 %copy-start.4 = (s32[128]{0:T(128)S(1)}, s32[128]{0:T(128)}, u32[]{:S(2)}) copy-start(s32[128]{0:T(128)} %cnt_ref.3) | copy-start | bytes 1540
  24.3 58.2 %all-to-all-start = ((bf16[128,8,2048]{0,2,1:T(8,128)(2,1)}), bf16[128,8,2048]{0,2,1:T(8,128)(2,1)}, u32[]{:S(2)}, u32[]{:S(2)}) async-start(bf16[128,8,2048]{0,2,1:T(8,128)(2,1)} %pad_maximum_fusion), calls=%async_computation | async-start | bytes 8388608 | tf_op jit(solution)/shard_map/all_to_all | solution.py:148
  106.5 32.8 %all-to-all-start.1 = ((bf16[64,3,16,128]{3,2,1,0:T(8,128)(2,1)}), bf16[64,3,16,128]{3,2,1,0:T(8,128)(2,1)S(1)}, u32[]{:S(2)}, u32[]{:S(2)}) async-start(bf16[64,3,16,128]{3,2,1,0:T(8,128)(2,1)} %shard_map.86), calls=%async_computation.1 | async-start | bytes 1572864 | tf_op jit(solution)/shard_map/all_to_all | solution.py:159
  129.9 3.4 %copy-start = (f32[128,8192]{1,0:T(8,128)S(1)}, f32[128,8192]{1,0:T(8,128)}, u32[]{:S(2)}) copy-start(f32[128,8192]{1,0:T(8,128)} %shard_map.87) | copy-start | bytes 12582916
Sparse Core Ops, SparseCore 0:
  11.0 95.3 all-gather.1

commit v10 on v9

--- a/solution.py
+++ b/solution.py
@@ -16,7 +16,7 @@
 BLK = 64
 MOSTR = 6
 SEQ_LEN = 1024
-ROWS_PER_STEP = 16
+ROWS_PER_STEP = 32
 
 
 def rope_back(grad, positions):
@@ -101,7 +101,7 @@
 
 def pick_blocks(product_t, cols, counts, part_rows, divisor, devices):
     per_dev = product_t.shape[1] // devices
-    width = max(128, per_dev)
+    width = max(256, per_dev)
     dests = width // per_dev
     chunks = product_t.shape[1] // width
     spec = pltpu.PrefetchScalarGridSpec(

time: 149 us -> 148 us (level)
  no operation moved by 1% of the time
where the time goes in v10:
time: 148 us; the launch traced here: 147 us
  waiting for transfers between devices  53.1 us (36%)
  Pallas kernels  21.5 us (15%)
  starting transfers between devices  19.3 us (13%)
  local copies, waits for them, and re-layouts  18.6 us (13%)
  between operations  14.2 us (10%)
  other arithmetic  13.7 us (9%)
  matrix products  6.7 us (5%)
    all_to_all x1, waiting for transfers between devices, shards(): lax.all_to_all(sent, ('x', 'c'), split_axis=1, concat_axis=0, tiled=True)  45.9 us
    pallas_call x1, Pallas kernels, normed_grad_of(): pl.pallas_call(_normed_grad_kernel, grid_spec=spec, out_shape=jax.ShapeDt...  14.4 us
    all_to_all x1, starting transfers between devices, shards(): lax.all_to_all(sent, ('x', 'c'), split_axis=1, concat_axis=0, tiled=True)  10.5 us
    all_to_all x1, starting transfers between devices, shards(): lax.all_to_all(partial, ('z', 'y'), split_axis=0, concat_axis=0, tiled=True)  8.78 us
    pallas_call x1, Pallas kernels, pick_blocks(): pl.pallas_call(functools.partial(_pick_kernel, part_rows=part_rows, divis...  7.06 us
    dot_general x1, matrix products, shards(): lax.dot_general(grad_all, slab, (((0,), (0,)), ((), ())), preferred_eleme...  6.7 us
    all_to_all x1, local copies, waits for them, and re-layouts, shards(): lax.all_to_all(sent, ('x', 'c'), split_axis=1, concat_axis=0, tiled=True)  6.54 us
    convert_element_type x1, local copies, waits for them, and re-layouts, shards(): normed = (xf * inv_rms * norm_gain).astype(jnp.bfloat16)  4.11 us
  transfers between devices with their start and end apart: 3, of which 3 were waited for; matrix products, arithmetic and copies ran while one was open for 24% of the time, Pallas kernels for 15%

profile of v10, /device:TPU:6, one launch (start us, length us, event | category | flops | bytes accessed | tf_op | source)
XLA Modules:
  0.0 147.1 jit_solution(5328748638545350663)
XLA Ops:
  7.2 1.2 reshape.138
  8.6 0.8 reshape.139
  9.4 1.1 copy.28
  10.6 0.7 convert_element_type.28
  11.3 2.1 %fusion = f32[128]{0:T(128)S(1)} fusion(bf16[128,8192]{1,0:T(8,128)(2,1)} %param.7), kind=kLoop, calls=%fused_computation.4 | loop fusion | flops 3145600 | bytes 2097664 | tf_op jit(solution)/shard_map/reduce_sum | solution.py:129
  13.4 1.9 %fusion.2 = bf16[128,8192]{1,0:T(8,128)(2,1)} fusion(bf16[128,8192]{1,0:T(8,128)(2,1)S(1)} %copy-done.1, f32[8192]{0:T(1024)S(1)} %copy-done.2, f32[128]{0:T(128)S(1)} %get-tuple-element.15), kind=kLoop, calls=%fused_computation.6 | loop fusion | flops 4194304 | bytes 4227584 | tf_op jit(solution)/shard_map/convert_element_type | solution.py:130
  15.3 4.1 %copy.26 = bf16[128,8192]{0,1:T(8,128)(2,1)} copy(bf16[128,8192]{1,0:T(8,128)(2,1)} %fusion.2) | data formatting | bytes 4194304 | tf_op jit(solution)/shard_map/convert_element_type | solution.py:130
  19.4 2.0 %copy.34 = bf16[128,8,128,8]{0,3,2,1:T(8,128)(2,1)S(1)} copy(bf16[128,8,128,8]{0,3,1,2:T(8,128)(2,1)} %bitcast.21) | data formatting | bytes 4194304 | tf_op jit(solution)/shard_map/transpose | solution.py:142
  22.0 2.3 %pad_maximum_fusion = bf16[128,8,2048]{0,2,1:T(8,128)(2,1)} fusion(bf16[128,8,1024]{0,2,1:T(8,128)(2,1)S(1)} %broadcast_in_dim.10, bf16[128,8,1024]{0,2,1:T(8,128)(2,1)S(1)} %bitcast.22), kind=kLoop, calls=%fused_computation.11 | loop fusion | flops 8388608 | bytes 8388608 | tf_op jit(solution)/shard_map/concatenate | solution.py:145
  24.3 10.5 %all-to-all-start = ((bf16[128,8,2048]{0,2,1:T(8,128)(2,1)}), bf16[128,8,2048]{0,2,1:T(8,128)(2,1)}, u32[]{:S(2)}, u32[]{:S(2)}) async-start(bf16[128,8,2048]{0,2,1:T(8,128)(2,1)} %pad_maximum_fusion), calls=%async_computation | async-start | bytes 8388608 | tf_op jit(solution)/shard_map/all_to_all | solution.py:148
  34.8 0.8 copy.31.gp_ref
  35.7 0.7 reshape.132.cols_ref
  36.6 45.9 %all-to-all-done = bf16[128,8,2048]{0,2,1:T(8,128)(2,1)} async-done(((bf16[128,8,2048]{0,2,1:T(8,128)(2,1)}), bf16[128,8,2048]{0,2,1:T(8,128)(2,1)}, u32[]{:S(2)}, u32[]{:S(2)}) %all-to-all-start) | async-done | bytes 4194336 | tf_op jit(solution)/shard_map/all_to_all | solution.py:148
  82.5 6.5 %copy.29 = bf16[8,128,1,2048]{3,1,0,2:T(8,128)(2,1)} copy(bf16[8,128,1,2048]{1,3,0,2:T(8,128)(2,1)} %bitcast.7) | data formatting | bytes 8388608 | tf_op jit(solution)/shard_map/all_to_all | solution.py:148
  89.0 6.7 %fusion.7.pt_ref = f32[1024,1024]{1,0:T(8,128)} fusion(bf16[1024,2048]{1,0:T(8,128)(2,1)} %bitcast.23), kind=kOutput, calls=%fused_computation.12 | convolution fusion | flops 2147483648 | bytes 8388608 | tf_op jit(solution)/shard_map/dot_general | solution.py:154
  95.7 7.1 %shard_map.86 = bf16[64,3,16,128]{3,2,1,0:T(8,128)(2,1)} custom-call(s32[768]{0:T(1024)} %reshape.132.cols_ref, s32[128]{0:T(128)} %cnt_ref.3, f32[1024,1024]{1,0:T(8,128)} %fusion.7.pt_ref), custom_call_target="tpu_custom_call" | custom-call | tf_op jit(solution)/shard_map/pallas_call | solution.py:113
  102.8 3.7 %all-gather.2.cloned.1.call-done.bt_ref = bf16[128,3,64,128]{3,2,1,0:T(8,128)(2,1)} async-done(((bf16[2,3,64,128]{3,2,1,0:T(8,128)(2,1)}), bf16[128,3,64,128]{3,2,1,0:T(8,128)(2,1)}) %all-gather.2.cloned.1.call-update) | async-done | bytes 6291472 | tf_op jit(solution)/shard_map/all_gather | solution.py:138
  106.5 8.8 %all-to-all-start.1 = ((bf16[64,3,16,128]{3,2,1,0:T(8,128)(2,1)}), bf16[64,3,16,128]{3,2,1,0:T(8,128)(2,1)S(1)}, u32[]{:S(2)}, u32[]{:S(2)}) async-start(bf16[64,3,16,128]{3,2,1,0:T(8,128)(2,1)} %shard_map.86), calls=%async_computation.1 | async-start | bytes 1572864 | tf_op jit(solution)/shard_map/all_to_all | solution.py:159
  115.3 14.4 %shard_map.87 = f32[128,8192]{1,0:T(8,128)} custom-call(s32[768]{0:T(1024)} %reshape.132.cols_ref, s32[128]{0:T(128)} %cnt_ref.3, bf16[128,1024]{1,0:T(8,128)(2,1)} %copy.31.gp_ref, bf16[128,3,64,128]{3,2,1,0:T(8,128)(2,1)} %all-gather.2.cloned.1.call-done.bt_ref), custom_call_target="tpu_custom_call" | custom-call | tf_op jit(solution)/shard_map/pallas_call | solution.py:75
  129.7 3.0 %fusion.6 = f32[128]{0:T(128)S(1)} fusion(bf16[128,8192]{1,0:T(8,128)(2,1)S(1)} %copy-done.1, f32[128,8192]{1,0:T(8,128)} %shard_map.87, f32[8192]{0:T(1024)S(1)} %copy-done.2), kind=kLoop, calls=%fused_computation.10 | loop fusion | flops 4194176 | bytes 6324736 | tf_op jit(solution)/shard_map/reduce_sum | solution.py:162
  132.7 0.5 copy-done
  133.2 2.6 %fusion.5 = bf16[128,8192]{1,0:T(8,128)(2,1)} fusion(bf16[128,8192]{1,0:T(8,128)(2,1)S(1)} %copy-done.1, f32[128,8192]{1,0:T(8,128)S(1)} %copy-done, f32[128]{0:T(128)S(1)} %broadcast_multiply_fusion, f32[128]{0:T(128)S(1)} %get-tuple-element.14, f32[8192]{0:T(1024)S(1)} %copy-done.2, f32[128]{0:T(128)S(1)} %get-tuple-element.15), kind=kLoop, calls=%fused_computation.9 | loop fusion | flops 7340032 | bytes 8422912 | tf_op jit(solution)/shard_map/convert_element_type | solution.py:163
  135.8 3.4 %all-to-all-done.1 = bf16[64,3,16,128]{3,2,1,0:T(8,128)(2,1)S(1)} async-done(((bf16[64,3,16,128]{3,2,1,0:T(8,128)(2,1)}), bf16[64,3,16,128]{3,2,1,0:T(8,128)(2,1)S(1)}, u32[]{:S(2)}, u32[]{:S(2)}) %all-to-all-start.1) | async-done | bytes 786464 | tf_op jit(solution)/shard_map/all_to_all | solution.py:159
  139.5 0.7 broadcast_select_fusion
  (27 shorter events, 1.4 us)
Async XLA Ops:
  7.2 6.2 %copy-start.1 = (bf16[128,8192]{1,0:T(8,128)(2,1)S(1)}, bf16[128,8192]{1,0:T(8,128)(2,1)}, u32[]{:S(2)}) copy-start(bf16[128,8192]{1,0:T(8,128)(2,1)} %param.7) | copy-start | bytes 6291460
  7.2 6.2 %copy-start.2 = (f32[8192]{0:T(1024)S(1)}, f32[8192]{0:T(1024)}, u32[]{:S(2)}) copy-start(f32[8192]{0:T(1024)} %param.8) | copy-start | bytes 98308
  7.2 99.3 %all-gather.2.cloned.1.call-start = ((), (), s32[]{:S(2)}) async-start(), calls=%async_computation.2 | async-start | bytes 6389760 | tf_op jit(solution)/shard_map/all_gather | solution.py:138
  24.3 11.3 %copy-start.3 = (s32[128,6]{0,1:T(8,128)S(1)}, s32[128,6]{0,1:T(8,128)}, u32[]{:S(2)}) copy-start(s32[128,6]{0,1:T(8,128)} %param.11) | copy-start | bytes 9220
  24.3 12.2 %copy-start.4 = (s32[128]{0:T(128)S(1)}, s32[128]{0:T(128)}, u32[]{:S(2)}) copy-start(s32[128]{0:T(128)} %cnt_ref.3) | copy-start | bytes 1540
  24.3 58.2 %all-to-all-start = ((bf16[128,8,2048]{0,2,1:T(8,128)(2,1)}), bf16[128,8,2048]{0,2,1:T(8,128)(2,1)}, u32[]{:S(2)}, u32[]{:S(2)}) async-start(bf16[128,8,2048]{0,2,1:T(8,128)(2,1)} %pad_maximum_fusion), calls=%async_computation | async-start | bytes 8388608 | tf_op jit(solution)/shard_map/all_to_all | solution.py:148
  106.5 32.7 %all-to-all-start.1 = ((bf16[64,3,16,128]{3,2,1,0:T(8,128)(2,1)}), bf16[64,3,16,128]{3,2,1,0:T(8,128)(2,1)S(1)}, u32[]{:S(2)}, u32[]{:S(2)}) async-start(bf16[64,3,16,128]{3,2,1,0:T(8,128)(2,1)} %shard_map.86), calls=%async_computation.1 | async-start | bytes 1572864 | tf_op jit(solution)/shard_map/all_to_all | solution.py:159
  129.7 3.4 %copy-start = (f32[128,8192]{1,0:T(8,128)S(1)}, f32[128,8192]{1,0:T(8,128)}, u32[]{:S(2)}) copy-start(f32[128,8192]{1,0:T(8,128)} %shard_map.87) | copy-start | bytes 12582916
Sparse Core Ops, SparseCore 0:
  11.0 95.3 all-gather.1

commit v11 on v10

--- a/solution.py
+++ b/solution.py
@@ -32,12 +32,13 @@
     return jnp.stack([first, second], axis=2).reshape(-1, KVW).astype(jnp.bfloat16)
 
 
-def _normed_grad_kernel(cols_ref, cnt_ref, gp_ref, bt_ref, out_ref, w_ref):
+def _normed_grad_kernel(cols_ref, cnt_ref, gp_ref, bt_ref, x_ref, gain_ref, out_ref, dot_ref, w_ref):
     step = pl.program_id(0)
 
     @pl.when(step == 0)
     def _():
         w_ref[...] = jnp.zeros(w_ref.shape, w_ref.dtype)
+        dot_ref[...] = jnp.zeros(dot_ref.shape, dot_ref.dtype)
 
     def place(fill):
         for rr in range(ROWS_PER_STEP):
@@ -54,11 +55,14 @@
                 w_ref[pl.ds(start, BLK), rr * BLK:(rr + 1) * BLK] = value
 
     place(True)
-    out_ref[...] = jnp.dot(gp_ref[...], w_ref[...], preferred_element_type=jnp.float32)
+    result = jnp.dot(gp_ref[...], w_ref[...], preferred_element_type=jnp.float32)
+    out_ref[...] = result
+    part = jnp.sum(gain_ref[...] * result * x_ref[...].astype(jnp.float32), axis=1, keepdims=True)
+    dot_ref[...] += jnp.broadcast_to(part, dot_ref.shape)
     place(False)
 
 
-def normed_grad_of(grad_pre, blocks_t, cols, counts):
+def normed_grad_of(grad_pre, blocks_t, cols, counts, checkpoint, norm_gain):
     tok = grad_pre.shape[0]
     row_blocks = blocks_t.shape[0]
     width = ROWS_PER_STEP * BLK
@@ -68,16 +72,24 @@
         in_specs=[
             pl.BlockSpec((tok, KVW), lambda g, c, n: (0, 0)),
             pl.BlockSpec((ROWS_PER_STEP, MOSTR // 2, BLK, 2 * BLK), lambda g, c, n: (g, 0, 0, 0)),
+            pl.BlockSpec((tok, width), lambda g, c, n: (0, g)),
+            pl.BlockSpec((1, width), lambda g, c, n: (0, g)),
         ],
-        out_specs=pl.BlockSpec((tok, width), lambda g, c, n: (0, g)),
+        out_specs=[
+            pl.BlockSpec((tok, width), lambda g, c, n: (0, g)),
+            pl.BlockSpec((tok, 128), lambda g, c, n: (0, 0)),
+        ],
         scratch_shapes=[pltpu.VMEM((KVW, width), jnp.bfloat16)],
     )
     return pl.pallas_call(
         _normed_grad_kernel,
         grid_spec=spec,
-        out_shape=jax.ShapeDtypeStruct((tok, row_blocks * BLK), jnp.float32),
+        out_shape=(
+            jax.ShapeDtypeStruct((tok, row_blocks * BLK), jnp.float32),
+            jax.ShapeDtypeStruct((tok, 128), jnp.float32),
+        ),
         compiler_params=pltpu.CompilerParams(dimension_semantics=("arbitrary",)),
-    )(cols.reshape(-1), counts, grad_pre, blocks_t)
+    )(cols.reshape(-1), counts, grad_pre, blocks_t, checkpoint, norm_gain.reshape(1, -1))
 
 
 def _pick_kernel(cols_ref, cnt_ref, pt_ref, out_ref, *, part_rows, divisor):
@@ -157,9 +169,9 @@
     partial = pick_blocks(product, kept_cols, kept_count, part_rows, divisor, dp_size)
     partial, piece = lax.optimization_barrier((partial, piece))
     summed = lax.all_to_all(partial, ("z", "y"), split_axis=0, concat_axis=0, tiled=True)
-    normed_grad = normed_grad_of(grad_pre, piece, kept_cols, kept_count)
+    normed_grad, row_dot = normed_grad_of(grad_pre, piece, kept_cols, kept_count, checkpoint, norm_gain)
     scaled = norm_gain * normed_grad
-    grads = inv_rms * scaled - inv_rms**3 * xf * jnp.mean(scaled * xf, axis=1, keepdims=True)
+    grads = inv_rms * scaled - inv_rms**3 * xf * (row_dot[:, :1] / D)
     grads = grads.astype(jnp.bfloat16)
     summed, grads = lax.optimization_barrier((summed, grads))
     summed = summed.astype(jnp.float32).sum(axis=0)

time: 148 us -> 148 us (level)
  local copies, waits for them, and re-layouts: 18.6 us -> 15.6 us
  waiting for transfers between devices: 53.1 us -> 55 us
    reduce_sum x1 -> x0, other arithmetic: 2.96 us -> none  [shards(): jnp.mean(scaled * xf, axis=1, keepdims=True)]
    all_gather x1, waiting for transfers between devices: 3.71 us -> 6.23 us  [shards(): piece = lax.all_gather(local_t, ('z', 'y'), axis=0, tiled=True)]
    convert_element_type x1, other arithmetic: 2.6 us -> 4.7 us  [shards(): grads = grads.astype(jnp.bfloat16)]
    transpose x1, local copies, waits for them, and re-layouts: 1.97 us -> 0.38 us  [shards(): split_normed = normed.reshape(tok_rows, row_blocks, groups, part_rows).tr...]
  transfers between devices with their start and end apart: 3 -> 3, of which waited for: 3 -> 3; matrix products, arithmetic and copies ran while one was open for 24% -> 22% of each run, Pallas kernels for 15% -> 15%
where the time goes in v11:
time: 148 us; the launch traced here: 147 us
  waiting for transfers between devices  55 us (37%)
  Pallas kernels  22.5 us (15%)
  starting transfers between devices  19.3 us (13%)
  local copies, waits for them, and re-layouts  15.6 us (11%)
  between operations  14.2 us (10%)
  other arithmetic  13.8 us (9%)
  matrix products  6.74 us (5%)
    all_to_all x1, waiting for transfers between devices, shards(): lax.all_to_all(sent, ('x', 'c'), split_axis=1, concat_axis=0, tiled=True)  45.9 us
    pallas_call x1, Pallas kernels, normed_grad_of(): pl.pallas_call(_normed_grad_kernel, grid_spec=spec, out_shape=(jax.ShapeD...  15.4 us
    all_to_all x1, starting transfers between devices, shards(): lax.all_to_all(sent, ('x', 'c'), split_axis=1, concat_axis=0, tiled=True)  10.5 us
    all_to_all x1, starting transfers between devices, shards(): lax.all_to_all(partial, ('z', 'y'), split_axis=0, concat_axis=0, tiled=True)  8.78 us
    pallas_call x1, Pallas kernels, pick_blocks(): pl.pallas_call(functools.partial(_pick_kernel, part_rows=part_rows, divis...  7.04 us
    dot_general x1, matrix products, shards(): lax.dot_general(grad_all, slab, (((0,), (0,)), ((), ())), preferred_eleme...  6.74 us
    all_to_all x1, local copies, waits for them, and re-layouts, shards(): lax.all_to_all(sent, ('x', 'c'), split_axis=1, concat_axis=0, tiled=True)  6.51 us
    all_gather x1, waiting for transfers between devices, shards(): piece = lax.all_gather(local_t, ('z', 'y'), axis=0, tiled=True)  6.23 us
  transfers between devices with their start and end apart: 3, of which 3 were waited for; matrix products, arithmetic and copies ran while one was open for 22% of the time, Pallas kernels for 15%

profile of v11, /device:TPU:6, one launch (start us, length us, event | category | flops | bytes accessed | tf_op | source)
XLA Modules:
  0.0 147.1 jit_solution(17685652514384615744)
XLA Ops:
  7.2 1.2 reshape.135
  8.6 0.8 reshape.136
  9.4 1.1 copy.28
  10.6 0.7 convert_element_type.28
  11.3 2.1 %fusion = f32[128]{0:T(128)S(1)} fusion(bf16[128,8192]{1,0:T(8,128)(2,1)} %x_ref.1), kind=kLoop, calls=%fused_computation.3 | loop fusion | flops 3145600 | bytes 2097664 | tf_op jit(solution)/shard_map/reduce_sum | solution.py:141
  13.4 1.9 %fusion.2 = bf16[128,8192]{1,0:T(8,128)(2,1)} fusion(bf16[128,8192]{1,0:T(8,128)(2,1)S(1)} %copy-done, f32[8192]{0:T(1024)S(1)} %copy-done.2, f32[128]{0:T(128)S(1)} %get-tuple-element.19), kind=kLoop, calls=%fused_computation.5 | loop fusion | flops 4194304 | bytes 4227584 | tf_op jit(solution)/shard_map/convert_element_type | solution.py:142
  15.3 3.2 %copy.26 = bf16[128,8192]{0,1:T(8,128)(2,1)S(1)} copy(bf16[128,8192]{1,0:T(8,128)(2,1)} %fusion.2) | data formatting | bytes 4194304 | tf_op jit(solution)/shard_map/convert_element_type | solution.py:142
  18.5 0.4 copy.34
  19.2 0.3 broadcast_in_dim.12
  19.5 2.3 %pad_maximum_fusion = bf16[128,8,2048]{0,2,1:T(8,128)(2,1)} fusion(bf16[128,8,1024]{0,2,1:T(8,128)(2,1)S(1)} %broadcast_in_dim.12, bf16[128,8,1024]{0,2,1:T(8,128)(2,1)S(1)} %bitcast.23), kind=kLoop, calls=%fused_computation.9 | loop fusion | flops 8388608 | bytes 8388608 | tf_op jit(solution)/shard_map/concatenate | solution.py:157
  21.8 10.5 %all-to-all-start = ((bf16[128,8,2048]{0,2,1:T(8,128)(2,1)}), bf16[128,8,2048]{0,2,1:T(8,128)(2,1)}, u32[]{:S(2)}, u32[]{:S(2)}) async-start(bf16[128,8,2048]{0,2,1:T(8,128)(2,1)} %pad_maximum_fusion), calls=%async_computation | async-start | bytes 8388608 | tf_op jit(solution)/shard_map/all_to_all | solution.py:160
  32.3 0.8 copy.31.gp_ref
  33.2 0.7 reshape.129.cols_ref
  34.1 45.9 %all-to-all-done = bf16[128,8,2048]{0,2,1:T(8,128)(2,1)} async-done(((bf16[128,8,2048]{0,2,1:T(8,128)(2,1)}), bf16[128,8,2048]{0,2,1:T(8,128)(2,1)}, u32[]{:S(2)}, u32[]{:S(2)}) %all-to-all-start) | async-done | bytes 4194336 | tf_op jit(solution)/shard_map/all_to_all | solution.py:160
  80.0 6.5 %copy.29 = bf16[8,128,1,2048]{3,1,0,2:T(8,128)(2,1)} copy(bf16[8,128,1,2048]{1,3,0,2:T(8,128)(2,1)} %bitcast.7) | data formatting | bytes 8388608 | tf_op jit(solution)/shard_map/all_to_all | solution.py:160
  86.5 6.7 %fusion.6.pt_ref = f32[1024,1024]{1,0:T(8,128)} fusion(bf16[1024,2048]{1,0:T(8,128)(2,1)} %bitcast.24), kind=kOutput, calls=%fused_computation.10 | convolution fusion | flops 2147483648 | bytes 8388608 | tf_op jit(solution)/shard_map/dot_general | solution.py:166
  93.2 7.0 %shard_map.86 = bf16[64,3,16,128]{3,2,1,0:T(8,128)(2,1)} custom-call(s32[768]{0:T(1024)} %reshape.129.cols_ref, s32[128]{0:T(128)} %cnt_ref.3, f32[1024,1024]{1,0:T(8,128)} %fusion.6.pt_ref), custom_call_target="tpu_custom_call" | custom-call | tf_op jit(solution)/shard_map/pallas_call | solution.py:125
  100.2 6.2 %all-gather.2.cloned.1.call-done.bt_ref = bf16[128,3,64,128]{3,2,1,0:T(8,128)(2,1)} async-done(((bf16[2,3,64,128]{3,2,1,0:T(8,128)(2,1)}), bf16[128,3,64,128]{3,2,1,0:T(8,128)(2,1)}) %all-gather.2.cloned.1.call-update) | async-done | bytes 6291472 | tf_op jit(solution)/shard_map/all_gather | solution.py:150
  106.5 8.8 %all-to-all-start.1 = ((bf16[64,3,16,128]{3,2,1,0:T(8,128)(2,1)}), bf16[64,3,16,128]{3,2,1,0:T(8,128)(2,1)S(1)}, u32[]{:S(2)}, u32[]{:S(2)}) async-start(bf16[64,3,16,128]{3,2,1,0:T(8,128)(2,1)} %shard_map.86), calls=%async_computation.1 | async-start | bytes 1572864 | tf_op jit(solution)/shard_map/all_to_all | solution.py:171
  115.3 15.4 %shard_map.87 = (f32[128,8192]{1,0:T(8,128)}, f32[128,128]{1,0:T(8,128)}) custom-call(s32[768]{0:T(1024)} %reshape.129.cols_ref, s32[128]{0:T(128)} %cnt_ref.3, bf16[128,1024]{1,0:T(8,128)(2,1)} %copy.31.gp_ref, bf16[128,3,64,128]{3,2,1,0:T(8,128)(2,1)} %all-gather.2.cloned.1.call-done.bt_ref, bf16[128,8192]{1,0:T(8,128)(2,1)} %x_ref.1, f32[1,8192]{1,0:T(1,128)} %bitcast.29), custom_call_target="tpu_custom_call" | custom-call | tf_op jit(solution)/shard_map/pallas_call | solution.py:84
  130.7 0.9 multiply_reduce_fusion
  131.7 4.7 %fusion.5 = bf16[128,8192]{1,0:T(8,128)(2,1)} fusion(bf16[128,8192]{1,0:T(8,128)(2,1)S(1)} %copy-done.1, f32[128,8192]{1,0:T(8,128)} %get-tuple-element.10, f32[128]{0:T(128)S(1)} %multiply_reduce_fusion, f32[128]{0:T(128)S(1)} %get-tuple-element.18, f32[8192]{0:T(1024)S(1)} %copy-done.3, f32[128]{0:T(128)S(1)} %get-tuple-element.19), kind=kLoop, calls=%fused_computation.8 | loop fusion | flops 7340032 | bytes 8422912 | tf_op jit(solution)/shard_map/convert_element_type | solution.py:175
  136.4 2.8 %all-to-all-done.1 = bf16[64,3,16,128]{3,2,1,0:T(8,128)(2,1)S(1)} async-done(((bf16[64,3,16,128]{3,2,1,0:T(8,128)(2,1)}), bf16[64,3,16,128]{3,2,1,0:T(8,128)(2,1)S(1)}, u32[]{:S(2)}, u32[]{:S(2)}) %all-to-all-start.1) | async-done | bytes 786464 | tf_op jit(solution)/shard_map/all_to_all | solution.py:171
  139.5 0.7 broadcast_select_fusion
  (28 shorter events, 1.1 us)
Async XLA Ops:
  7.2 6.2 %copy-start = (bf16[128,8192]{1,0:T(8,128)(2,1)S(1)}, bf16[128,8192]{1,0:T(8,128)(2,1)}, u32[]{:S(2)}) copy-start(bf16[128,8192]{1,0:T(8,128)(2,1)} %x_ref.1) | copy-start | bytes 6291460
  7.2 6.2 %copy-start.2 = (f32[8192]{0:T(1024)S(1)}, f32[8192]{0:T(1024)}, u32[]{:S(2)}) copy-start(f32[8192]{0:T(1024)} %param.8) | copy-start | bytes 98308
  7.2 99.3 %all-gather.2.cloned.1.call-start = ((), (), s32[]{:S(2)}) async-start(), calls=%async_computation.2 | async-start | bytes 6389760 | tf_op jit(solution)/shard_map/all_gather | solution.py:150
  21.8 11.3 %copy-start.4 = (s32[128,6]{0,1:T(8,128)S(1)}, s32[128,6]{0,1:T(8,128)}, u32[]{:S(2)}) copy-start(s32[128,6]{0,1:T(8,128)} %param.11) | copy-start | bytes 9220
  21.8 12.2 %copy-start.5 = (s32[128]{0:T(128)S(1)}, s32[128]{0:T(128)}, u32[]{:S(2)}) copy-start(s32[128]{0:T(128)} %cnt_ref.3) | copy-start | bytes 1540
  21.8 58.1 %all-to-all-start = ((bf16[128,8,2048]{0,2,1:T(8,128)(2,1)}), bf16[128,8,2048]{0,2,1:T(8,128)(2,1)}, u32[]{:S(2)}, u32[]{:S(2)}) async-start(bf16[128,8,2048]{0,2,1:T(8,128)(2,1)} %pad_maximum_fusion), calls=%async_computation | async-start | bytes 8388608 | tf_op jit(solution)/shard_map/all_to_all | solution.py:160
  106.5 32.7 %all-to-all-start.1 = ((bf16[64,3,16,128]{3,2,1,0:T(8,128)(2,1)}), bf16[64,3,16,128]{3,2,1,0:T(8,128)(2,1)S(1)}, u32[]{:S(2)}, u32[]{:S(2)}) async-start(bf16[64,3,16,128]{3,2,1,0:T(8,128)(2,1)} %shard_map.86), calls=%async_computation.1 | async-start | bytes 1572864 | tf_op jit(solution)/shard_map/all_to_all | solution.py:171
  115.3 16.4 %copy-start.1 = (bf16[128,8192]{1,0:T(8,128)(2,1)S(1)}, bf16[128,8192]{1,0:T(8,128)(2,1)}, u32[]{:S(2)}) copy-start(bf16[128,8192]{1,0:T(8,128)(2,1)} %x_ref.1) | copy-start | bytes 6291460
  115.3 16.4 %copy-start.3 = (f32[8192]{0:T(1024)S(1)}, f32[8192]{0:T(1024)}, u32[]{:S(2)}) copy-start(f32[8192]{0:T(1024)} %param.8) | copy-start | bytes 98308
Sparse Core Ops, SparseCore 0:
  11.0 95.4 all-gather.1

commit v12 on v10

--- a/solution.py
+++ b/solution.py
@@ -16,7 +16,7 @@
 BLK = 64
 MOSTR = 6
 SEQ_LEN = 1024
-ROWS_PER_STEP = 32
+ROWS_PER_STEP = 64
 
 
 def rope_back(grad, positions):
@@ -101,7 +101,7 @@
 
 def pick_blocks(product_t, cols, counts, part_rows, divisor, devices):
     per_dev = product_t.shape[1] // devices
-    width = max(256, per_dev)
+    width = max(512, per_dev)
     dests = width // per_dev
     chunks = product_t.shape[1] // width
     spec = pltpu.PrefetchScalarGridSpec(

time: 148 us -> 149 us (level)
  waiting for transfers between devices: 53.1 us -> 51 us
  Pallas kernels: 21.5 us -> 23.4 us
  transfers between devices with their start and end apart: 3 -> 3, of which waited for: 3 -> 3; matrix products, arithmetic and copies ran while one was open for 24% -> 24% of each run, Pallas kernels for 15% -> 16%
where the time goes in v12:
time: 149 us; the launch traced here: 147 us
  waiting for transfers between devices  51 us (34%)
  Pallas kernels  23.4 us (16%)
  starting transfers between devices  19.4 us (13%)
  local copies, waits for them, and re-layouts  18.6 us (12%)
  between operations  14.2 us (10%)
  other arithmetic  13.7 us (9%)
  matrix products  6.7 us (4%)
    all_to_all x1, waiting for transfers between devices, shards(): lax.all_to_all(sent, ('x', 'c'), split_axis=1, concat_axis=0, tiled=True)  45.9 us
    pallas_call x1, Pallas kernels, normed_grad_of(): pl.pallas_call(_normed_grad_kernel, grid_spec=spec, out_shape=jax.ShapeDt...  15.1 us
    all_to_all x1, starting transfers between devices, shards(): lax.all_to_all(sent, ('x', 'c'), split_axis=1, concat_axis=0, tiled=True)  10.5 us
    all_to_all x1, starting transfers between devices, shards(): lax.all_to_all(partial, ('z', 'y'), split_axis=0, concat_axis=0, tiled=True)  8.88 us
    pallas_call x1, Pallas kernels, pick_blocks(): pl.pallas_call(functools.partial(_pick_kernel, part_rows=part_rows, divis...  8.25 us
    dot_general x1, matrix products, shards(): lax.dot_general(grad_all, slab, (((0,), (0,)), ((), ())), preferred_eleme...  6.7 us
    all_to_all x1, local copies, waits for them, and re-layouts, shards(): lax.all_to_all(sent, ('x', 'c'), split_axis=1, concat_axis=0, tiled=True)  6.54 us
    convert_element_type x1, local copies, waits for them, and re-layouts, shards(): normed = (xf * inv_rms * norm_gain).astype(jnp.bfloat16)  4.11 us
  transfers between devices with their start and end apart: 3, of which 3 were waited for; matrix products, arithmetic and copies ran while one was open for 24% of the time, Pallas kernels for 16%

profile of v12, /device:TPU:6, one launch (start us, length us, event | category | flops | bytes accessed | tf_op | source)
XLA Modules:
  0.0 147.0 jit_solution(14305017459888246255)
XLA Ops:
  7.2 1.2 reshape.138
  8.6 0.8 reshape.139
  9.4 1.1 copy.28
  10.6 0.7 convert_element_type.28
  11.3 2.1 %fusion = f32[128]{0:T(128)S(1)} fusion(bf16[128,8192]{1,0:T(8,128)(2,1)} %param.7), kind=kLoop, calls=%fused_computation.4 | loop fusion | flops 3145600 | bytes 2097664 | tf_op jit(solution)/shard_map/reduce_sum | solution.py:129
  13.4 1.9 %fusion.2 = bf16[128,8192]{1,0:T(8,128)(2,1)} fusion(bf16[128,8192]{1,0:T(8,128)(2,1)S(1)} %copy-done.1, f32[8192]{0:T(1024)S(1)} %copy-done.2, f32[128]{0:T(128)S(1)} %get-tuple-element.15), kind=kLoop, calls=%fused_computation.6 | loop fusion | flops 4194304 | bytes 4227584 | tf_op jit(solution)/shard_map/convert_element_type | solution.py:130
  15.3 4.1 %copy.26 = bf16[128,8192]{0,1:T(8,128)(2,1)} copy(bf16[128,8192]{1,0:T(8,128)(2,1)} %fusion.2) | data formatting | bytes 4194304 | tf_op jit(solution)/shard_map/convert_element_type | solution.py:130
  19.4 2.0 %copy.34 = bf16[128,8,128,8]{0,3,2,1:T(8,128)(2,1)S(1)} copy(bf16[128,8,128,8]{0,3,1,2:T(8,128)(2,1)} %bitcast.21) | data formatting | bytes 4194304 | tf_op jit(solution)/shard_map/transpose | solution.py:142
  22.0 2.3 %pad_maximum_fusion = bf16[128,8,2048]{0,2,1:T(8,128)(2,1)} fusion(bf16[128,8,1024]{0,2,1:T(8,128)(2,1)S(1)} %broadcast_in_dim.10, bf16[128,8,1024]{0,2,1:T(8,128)(2,1)S(1)} %bitcast.22), kind=kLoop, calls=%fused_computation.11 | loop fusion | flops 8388608 | bytes 8388608 | tf_op jit(solution)/shard_map/concatenate | solution.py:145
  24.3 10.5 %all-to-all-start = ((bf16[128,8,2048]{0,2,1:T(8,128)(2,1)}), bf16[128,8,2048]{0,2,1:T(8,128)(2,1)}, u32[]{:S(2)}, u32[]{:S(2)}) async-start(bf16[128,8,2048]{0,2,1:T(8,128)(2,1)} %pad_maximum_fusion), calls=%async_computation | async-start | bytes 8388608 | tf_op jit(solution)/shard_map/all_to_all | solution.py:148
  34.8 0.8 copy.31.gp_ref
  35.7 0.7 reshape.132.cols_ref
  36.6 45.9 %all-to-all-done = bf16[128,8,2048]{0,2,1:T(8,128)(2,1)} async-done(((bf16[128,8,2048]{0,2,1:T(8,128)(2,1)}), bf16[128,8,2048]{0,2,1:T(8,128)(2,1)}, u32[]{:S(2)}, u32[]{:S(2)}) %all-to-all-start) | async-done | bytes 4194336 | tf_op jit(solution)/shard_map/all_to_all | solution.py:148
  82.5 6.5 %copy.29 = bf16[8,128,1,2048]{3,1,0,2:T(8,128)(2,1)} copy(bf16[8,128,1,2048]{1,3,0,2:T(8,128)(2,1)} %bitcast.7) | data formatting | bytes 8388608 | tf_op jit(solution)/shard_map/all_to_all | solution.py:148
  89.0 6.7 %fusion.7.pt_ref = f32[1024,1024]{1,0:T(8,128)} fusion(bf16[1024,2048]{1,0:T(8,128)(2,1)} %bitcast.23), kind=kOutput, calls=%fused_computation.12 | convolution fusion | flops 2147483648 | bytes 8388608 | tf_op jit(solution)/shard_map/dot_general | solution.py:154
  95.7 8.3 %shard_map.86 = bf16[64,3,16,128]{3,2,1,0:T(8,128)(2,1)} custom-call(s32[768]{0:T(1024)} %reshape.132.cols_ref, s32[128]{0:T(128)} %cnt_ref.3, f32[1024,1024]{1,0:T(8,128)} %fusion.7.pt_ref), custom_call_target="tpu_custom_call" | custom-call | tf_op jit(solution)/shard_map/pallas_call | solution.py:113
  104.0 2.5 %all-gather.2.cloned.1.call-done.bt_ref = bf16[128,3,64,128]{3,2,1,0:T(8,128)(2,1)} async-done(((bf16[2,3,64,128]{3,2,1,0:T(8,128)(2,1)}), bf16[128,3,64,128]{3,2,1,0:T(8,128)(2,1)}) %all-gather.2.cloned.1.call-update) | async-done | bytes 6291472 | tf_op jit(solution)/shard_map/all_gather | solution.py:138
  106.5 8.9 %all-to-all-start.1 = ((bf16[64,3,16,128]{3,2,1,0:T(8,128)(2,1)}), bf16[64,3,16,128]{3,2,1,0:T(8,128)(2,1)S(1)}, u32[]{:S(2)}, u32[]{:S(2)}) async-start(bf16[64,3,16,128]{3,2,1,0:T(8,128)(2,1)} %shard_map.86), calls=%async_computation.1 | async-start | bytes 1572864 | tf_op jit(solution)/shard_map/all_to_all | solution.py:159
  115.4 15.1 %shard_map.87 = f32[128,8192]{1,0:T(8,128)} custom-call(s32[768]{0:T(1024)} %reshape.132.cols_ref, s32[128]{0:T(128)} %cnt_ref.3, bf16[128,1024]{1,0:T(8,128)(2,1)} %copy.31.gp_ref, bf16[128,3,64,128]{3,2,1,0:T(8,128)(2,1)} %all-gather.2.cloned.1.call-done.bt_ref), custom_call_target="tpu_custom_call" | custom-call | tf_op jit(solution)/shard_map/pallas_call | solution.py:75
  130.5 3.0 %fusion.6 = f32[128]{0:T(128)S(1)} fusion(bf16[128,8192]{1,0:T(8,128)(2,1)S(1)} %copy-done.1, f32[128,8192]{1,0:T(8,128)} %shard_map.87, f32[8192]{0:T(1024)S(1)} %copy-done.2), kind=kLoop, calls=%fused_computation.10 | loop fusion | flops 4194176 | bytes 6324736 | tf_op jit(solution)/shard_map/reduce_sum | solution.py:162
  133.5 0.5 copy-done
  133.9 2.6 %fusion.5 = bf16[128,8192]{1,0:T(8,128)(2,1)} fusion(bf16[128,8192]{1,0:T(8,128)(2,1)S(1)} %copy-done.1, f32[128,8192]{1,0:T(8,128)S(1)} %copy-done, f32[128]{0:T(128)S(1)} %broadcast_multiply_fusion, f32[128]{0:T(128)S(1)} %get-tuple-element.14, f32[8192]{0:T(1024)S(1)} %copy-done.2, f32[128]{0:T(128)S(1)} %get-tuple-element.15), kind=kLoop, calls=%fused_computation.9 | loop fusion | flops 7340032 | bytes 8422912 | tf_op jit(solution)/shard_map/convert_element_type | solution.py:163
  136.5 2.6 %all-to-all-done.1 = bf16[64,3,16,128]{3,2,1,0:T(8,128)(2,1)S(1)} async-done(((bf16[64,3,16,128]{3,2,1,0:T(8,128)(2,1)}), bf16[64,3,16,128]{3,2,1,0:T(8,128)(2,1)S(1)}, u32[]{:S(2)}, u32[]{:S(2)}) %all-to-all-start.1) | async-done | bytes 786464 | tf_op jit(solution)/shard_map/all_to_all | solution.py:159
  139.5 0.7 broadcast_select_fusion
  (27 shorter events, 1.4 us)
Async XLA Ops:
  7.2 6.2 %copy-start.1 = (bf16[128,8192]{1,0:T(8,128)(2,1)S(1)}, bf16[128,8192]{1,0:T(8,128)(2,1)}, u32[]{:S(2)}) copy-start(bf16[128,8192]{1,0:T(8,128)(2,1)} %param.7) | copy-start | bytes 6291460
  7.2 6.2 %copy-start.2 = (f32[8192]{0:T(1024)S(1)}, f32[8192]{0:T(1024)}, u32[]{:S(2)}) copy-start(f32[8192]{0:T(1024)} %param.8) | copy-start | bytes 98308
  7.2 99.3 %all-gather.2.cloned.1.call-start = ((), (), s32[]{:S(2)}) async-start(), calls=%async_computation.2 | async-start | bytes 6389760 | tf_op jit(solution)/shard_map/all_gather | solution.py:138
  24.3 11.3 %copy-start.3 = (s32[128,6]{0,1:T(8,128)S(1)}, s32[128,6]{0,1:T(8,128)}, u32[]{:S(2)}) copy-start(s32[128,6]{0,1:T(8,128)} %param.11) | copy-start | bytes 9220
  24.3 12.2 %copy-start.4 = (s32[128]{0:T(128)S(1)}, s32[128]{0:T(128)}, u32[]{:S(2)}) copy-start(s32[128]{0:T(128)} %cnt_ref.3) | copy-start | bytes 1540
  24.3 58.2 %all-to-all-start = ((bf16[128,8,2048]{0,2,1:T(8,128)(2,1)}), bf16[128,8,2048]{0,2,1:T(8,128)(2,1)}, u32[]{:S(2)}, u32[]{:S(2)}) async-start(bf16[128,8,2048]{0,2,1:T(8,128)(2,1)} %pad_maximum_fusion), calls=%async_computation | async-start | bytes 8388608 | tf_op jit(solution)/shard_map/all_to_all | solution.py:148
  106.5 32.7 %all-to-all-start.1 = ((bf16[64,3,16,128]{3,2,1,0:T(8,128)(2,1)}), bf16[64,3,16,128]{3,2,1,0:T(8,128)(2,1)S(1)}, u32[]{:S(2)}, u32[]{:S(2)}) async-start(bf16[64,3,16,128]{3,2,1,0:T(8,128)(2,1)} %shard_map.86), calls=%async_computation.1 | async-start | bytes 1572864 | tf_op jit(solution)/shard_map/all_to_all | solution.py:159
  130.5 3.4 %copy-start = (f32[128,8192]{1,0:T(8,128)S(1)}, f32[128,8192]{1,0:T(8,128)}, u32[]{:S(2)}) copy-start(f32[128,8192]{1,0:T(8,128)} %shard_map.87) | copy-start | bytes 12582916
Sparse Core Ops, SparseCore 0:
  11.0 95.3 all-gather.1
